TPU v7x, 256 devices: a whole 4x4x8 slice. The times are simulated.
256 devices in a mesh: section: 2 (over core), req: 32 (over z, y), head: 4 (over x).
Axes of the slice: x: 4, y: 4, z: 8, core: 2. Of those that a mesh axis runs over, the one named last changes fastest.
Arguments:
- token_ids: int32 [128, 4], P('req'), may hold values from 0 to 31999
- request_order: int32 [128], replicated, may hold values from 0 to 127, each once
- window_lengths: int32 [128], replicated, may hold values from 1 to 512, as said below
- embed_table: bfloat16 [32000, 2048], P(('req', 'head')), may hold values from -6 to 6
- cache_arrived: bfloat16 [2, 128, 512, 2, 2048], P('section', None, 'req', None, 'head'), may hold values from -16 to 16
- state_arrived: float32 [2, 128, 128, 16, 128], P('section', None, 'req', 'head'), may hold values from -2 to 2
- conv_history: bfloat16 [2, 128, 3, 3, 2048], P('section', 'req', None, None, 'head'), may hold values from -6 to 6
- sink_cache: bfloat16 [2, 128, 4, 2, 2048], P('section', 'req', None, None, 'head'), may hold values from -16 to 16
- w_qkv: bfloat16 [2, 2048, 3, 2048], P('section', None, None, 'head'), may hold values from -0.125 to 0.125
- w_out: bfloat16 [2, 2048, 2048], P('section', 'head'), may hold values from -0.125 to 0.125
- w_beta: bfloat16 [2, 2048, 16], P('section', None, 'head'), may hold values from -0.125 to 0.125
- conv_taps: float32 [2, 4, 3, 2048], P('section', None, None, 'head'), may hold values from -3 to 3
- pre_gain: float32 [2, 2048], P('section'), may hold values from 0.25 to 1.75
- out_gain: float32 [2, 2048], P('section', 'head'), may hold values from 0.25 to 1.75
- score_scale_table: float32 [2, 16], P('section', 'head'), may hold values from 4 to 512
Outputs:
- layer_out: bfloat16 [2, 128, 4, 2048], P('section', 'req')
- final_state: float32 [2, 128, 128, 16, 128], P('section', 'req', None, 'head')
Inputs may be any that keep to these rules, and one draw needn't show every extreme that they name: `request_order`: a permutation of the arriving requests. `window_lengths`: some request holds a full window.
All inputs are finite; a program needn't handle non-finite values.
Results may differ from a plain program's by a relative error of at most 0.025.
Values may be sent and summed in bfloat16 or wider, within the bound.
No kernel may reach another device: no remote copies, remote signals or barrier semaphores. Data moves between devices by JAX's collectives and lax.ppermute only.
A program may use at most 128 MiB of HBM per device.

v0:
```python
import jax
import jax.numpy as jnp
from jax import lax
from jax.experimental import pallas as pl
from jax.experimental.pallas import tpu as pltpu
from jax.sharding import PartitionSpec as P

WIN = 512


epsilon = 1e-06
negative_big = -1e30


def rms_scale(values, gain_row):
    return (
        values * lax.rsqrt(jnp.mean(values * values, axis=-1, keepdims=True) + epsilon) * gain_row
    )


def unit_rows(values):
    return values * lax.rsqrt(jnp.sum(values * values, axis=-1, keepdims=True) + epsilon)


def spread(value, axis):
    peers = lax.axis_size(axis)
    copies = jnp.broadcast_to(value[None], (peers,) + value.shape)
    return lax.all_to_all(copies, axis, 0, 0, tiled=True)


def head_sum(value):
    peers = lax.axis_size("head")
    step = 1
    while step < peers:
        pairs = [(i, i ^ step) for i in range(peers)]
        value = value + lax.ppermute(value, "head", pairs)
        step *= 2
    return value


def delta_rule_kernel(beta_ref, state_ref, key_ref, query_ref, value_ref, state_out, read_out):
    slots, key_rows, _ = state_ref.shape
    heads = key_ref.shape[1]
    tokens = value_ref.shape[1]
    for s in range(slots):
        for h in range(heads):
            cols = pl.ds(h * key_rows, key_rows)
            matrix = state_ref[s, :, cols]
            key_cols = key_ref[s, h]
            query_cols = query_ref[s, h]
            for t in range(tokens):
                k_t = key_cols[:, t : t + 1]
                predicted = jnp.sum(matrix * k_t, axis=0, keepdims=True)
                v_t = value_ref[s, pl.ds(t, 1), cols]
                gate = beta_ref[(s * tokens + t) * heads + h]
                matrix = matrix + gate * (k_t * (v_t - predicted))
                read_out[s, pl.ds(t, 1), cols] = jnp.sum(
                    matrix * query_cols[:, t : t + 1], axis=0, keepdims=True
                )
            state_out[s, :, cols] = matrix


def delta_rule(start_state, key_vec, query_vec, value_vec, beta_gate):
    slots, key_rows, heads, value_cols = start_state.shape
    tokens = key_vec.shape[1]
    vmem = pl.BlockSpec(memory_space=pltpu.VMEM)
    new_state, readout = pl.pallas_call(
        delta_rule_kernel,
        out_shape=(
            jax.ShapeDtypeStruct((slots, key_rows, heads * value_cols), jnp.float32),
            jax.ShapeDtypeStruct((slots, tokens, heads * value_cols), jnp.float32),
        ),
        in_specs=[pl.BlockSpec(memory_space=pltpu.SMEM), vmem, vmem, vmem, vmem],
        out_specs=(vmem, vmem),
        cost_estimate=pl.CostEstimate(
            flops=8 * slots * heads * tokens * key_rows * value_cols,
            bytes_accessed=8 * slots * key_rows * heads * value_cols,
            transcendentals=0,
        ),
    )(
        beta_gate.reshape(-1),
        start_state.reshape(slots, key_rows, heads * value_cols),
        jnp.transpose(key_vec, (0, 2, 3, 1)),
        jnp.transpose(query_vec, (0, 2, 3, 1)),
        value_vec.reshape(slots, tokens, heads * value_cols),
    )
    return (
        new_state.reshape(slots, key_rows, heads, value_cols),
        readout.reshape(slots, tokens, heads, value_cols),
    )


def shards(
    token_ids,
    request_order,
    window_lengths,
    embed_table,
    cache_arrived,
    state_arrived,
    conv_history,
    sink_cache,
    w_qkv,
    w_out,
    w_beta,
    conv_taps,
    pre_gain,
    out_gain,
    score_scale_table,
):
    slot_count, token_count = token_ids.shape
    groups = lax.axis_size("req")
    heads_dev = score_scale_table.shape[1]
    width = pre_gain.shape[1]
    local_width = out_gain.shape[1]
    head_dim = local_width // heads_dev
    group_index = lax.axis_index("req")
    section_index = lax.axis_index("section")
    vocab_dev = embed_table.shape[0]
    rows = slot_count * token_count

    all_ids = spread(token_ids, "req")
    first_row = lax.axis_index(("req", "head")) * vocab_dev
    onehot = (
        all_ids.reshape(-1)[:, None] == first_row + jnp.arange(vocab_dev, dtype=jnp.int32)[None, :]
    ).astype(jnp.bfloat16)
    looked_up = jnp.dot(onehot, embed_table, preferred_element_type=jnp.float32).astype(jnp.bfloat16)
    arrived_rows = lax.all_to_all(
        looked_up.reshape(groups, rows, width), "req", 0, 0, tiled=True
    )
    partial_rows = jnp.sum(arrived_rows.astype(jnp.float32), axis=0).astype(jnp.bfloat16)
    embedded = jnp.sum(spread(partial_rows, "head").astype(jnp.float32), axis=0).astype(jnp.bfloat16)

    ordered_states = jnp.take(state_arrived[0], request_order, axis=0)
    start_state = lax.all_to_all(ordered_states, "req", 0, 1, tiled=True)

    ordered_cache = jnp.take(cache_arrived[0], request_order, axis=0)
    cache_rows = ordered_cache.shape[1]
    all_slots = ordered_cache.shape[0]
    stored_key_rows = ordered_cache[:, :, 0].reshape(all_slots, cache_rows, heads_dev, head_dim)
    cache_values = ordered_cache[:, :, 1].reshape(all_slots, cache_rows, heads_dev, head_dim)
    all_lengths = jnp.take(window_lengths, request_order)
    positions = group_index * cache_rows + jnp.arange(cache_rows, dtype=jnp.int32)
    new_index = jnp.arange(token_count, dtype=jnp.int32)
    cache_limit = jnp.maximum(WIN - all_lengths[:, None], new_index[None, :] + 1)
    cache_mask = positions[None, None, None, :] >= cache_limit[:, :, None, None]

    sink_count = sink_cache.shape[2]
    anchor_key_rows = sink_cache[0][:, :, 0].reshape(slot_count, sink_count, heads_dev, head_dim)
    sink_values = sink_cache[0][:, :, 1].reshape(slot_count, sink_count, heads_dev, head_dim)
    qkv_matrix = w_qkv[0].reshape(width, 3 * local_width)
    conv_weights = conv_taps[0]
    scale = score_scale_table[0]
    gain_head = out_gain[0].reshape(heads_dev, head_dim)
    history = conv_history[0]
    fresh_mask = (new_index[None, :] <= new_index[:, None])[None, :, None, :]

    def layer(stream):
        normed = rms_scale(stream.astype(jnp.float32), pre_gain[0]).astype(jnp.bfloat16)
        projected = (
            jnp.dot(normed, qkv_matrix, preferred_element_type=jnp.float32)
            .astype(jnp.bfloat16)
            .reshape(slot_count, token_count, 3, local_width)
        )
        sequence = jnp.concatenate([history, projected], axis=1).astype(jnp.float32)
        taps = conv_weights.shape[0]
        mixed_rows = sum(
            sequence[:, i : i + token_count] * conv_weights[i][None, None] for i in range(taps)
        )
        activated = jax.nn.silu(mixed_rows)
        query_vec = unit_rows(activated[:, :, 0].reshape(slot_count, token_count, heads_dev, head_dim))
        key_vec = unit_rows(activated[:, :, 1].reshape(slot_count, token_count, heads_dev, head_dim))
        value_vec = activated[:, :, 2].reshape(slot_count, token_count, heads_dev, head_dim)
        beta_gate = jax.nn.sigmoid(
            jnp.dot(normed, w_beta[0], preferred_element_type=jnp.float32)
        ).reshape(slot_count, token_count, heads_dev)

        query_halfwidth = query_vec.astype(jnp.bfloat16)
        all_queries = spread(query_halfwidth, "req").reshape(
            all_slots, token_count, heads_dev, head_dim
        )
        stored_scores = (
            jnp.einsum(
                "rthd,rwhd->rthw",
                all_queries,
                stored_key_rows,
                preferred_element_type=jnp.float32,
            )
            * scale[None, None, :, None]
        )
        local_max = jnp.max(jnp.where(cache_mask, stored_scores, negative_big), axis=-1)
        local_weights = jnp.where(cache_mask, jnp.exp(stored_scores - local_max[..., None]), 0.0)
        local_sum = jnp.sum(local_weights, axis=-1)
        local_part = jnp.einsum(
            "rthw,rwhd->rthd",
            local_weights.astype(jnp.bfloat16),
            cache_values,
            preferred_element_type=jnp.float32,
        )
        stats = jnp.concatenate(
            [
                local_sum,
                local_max,
                jnp.zeros((all_slots, token_count, head_dim - 2 * heads_dev), jnp.float32),
            ],
            axis=-1,
        )
        packed = jnp.concatenate([local_part, stats[:, :, None, :]], axis=2).reshape(
            groups, slot_count, token_count, heads_dev + 1, head_dim
        )
        gathered = lax.all_to_all(packed, "req", 0, 0, tiled=True)
        part_numer = gathered[:, :, :, :heads_dev]
        part_sum = gathered[:, :, :, heads_dev, :heads_dev]
        part_max = gathered[:, :, :, heads_dev, heads_dev : 2 * heads_dev]

        delta_state, readout = delta_rule(start_state, key_vec, query_vec, value_vec, beta_gate)

        new_keys = key_vec.astype(jnp.bfloat16)
        new_values = value_vec.astype(jnp.bfloat16)
        anchor_scores = (
            jnp.einsum(
                "sthd,sjhd->sthj", query_halfwidth, anchor_key_rows, preferred_element_type=jnp.float32
            )
            * scale[None, None, :, None]
        )
        incoming_scores = (
            jnp.einsum(
                "sthd,suhd->sthu", query_halfwidth, new_keys, preferred_element_type=jnp.float32
            )
            * scale[None, None, :, None]
        )
        highest = jnp.maximum(
            jnp.max(anchor_scores, axis=-1),
            jnp.max(jnp.where(fresh_mask, incoming_scores, negative_big), axis=-1),
        )
        highest = jnp.maximum(highest, jnp.max(part_max, axis=0))
        part_scale = jnp.exp(part_max - highest[None])
        sink_weights = jnp.exp(anchor_scores - highest[..., None])
        fresh_weights = jnp.where(fresh_mask, jnp.exp(incoming_scores - highest[..., None]), 0.0)
        weight_sum = (
            jnp.sum(part_scale * part_sum, axis=0)
            + jnp.sum(sink_weights, axis=-1)
            + jnp.sum(fresh_weights, axis=-1)
        )
        numerator = jnp.sum(part_scale[..., None] * part_numer, axis=0)
        numerator = numerator + jnp.einsum(
            "sthj,sjhd->sthd",
            sink_weights.astype(jnp.bfloat16),
            sink_values,
            preferred_element_type=jnp.float32,
        )
        numerator = numerator + jnp.einsum(
            "sthu,suhd->sthd",
            fresh_weights.astype(jnp.bfloat16),
            new_values,
            preferred_element_type=jnp.float32,
        )
        attended = numerator / weight_sum[..., None]
        mixed_heads = (
            (rms_scale(readout, gain_head[None, None]) + attended)
            .astype(jnp.bfloat16)
            .reshape(rows, local_width)
        )
        partial_out = jnp.dot(mixed_heads, w_out[0], preferred_element_type=jnp.float32)
        mixer_out = head_sum(partial_out)
        stream_out = (stream.astype(jnp.float32) + mixer_out).astype(jnp.bfloat16)
        return stream_out, delta_state

    first_out, first_state = layer(embedded)
    received = lax.ppermute(first_out, "section", [(0, 1)])
    second_out, second_state = layer(received)
    is_first = section_index == 0
    produced = jnp.where(is_first, first_out, second_out).reshape(slot_count, token_count, width)
    final_state = jnp.where(is_first, first_state, second_state)
    return (produced[None], final_state[None])


def solution(mesh):
    return jax.shard_map(
        shards,
        mesh=mesh,
        in_specs=(
            P("req", None),
            P(),
            P(),
            P(("req", "head"), None),
            P("section", None, "req", None, "head"),
            P("section", None, "req", "head", None),
            P("section", "req", None, None, "head"),
            P("section", "req", None, None, "head"),
            P("section", None, None, "head"),
            P("section", "head", None),
            P("section", None, "head"),
            P("section", None, None, "head"),
            P("section", None),
            P("section", "head"),
            P("section", "head"),
        ),
        out_specs=(P("section", "req", None, None), P("section", "req", None, "head", None)),
        check_vma=False,
    )
```

profile of v0, /device:TPU:2, one launch (start us, length us, event | category | flops | bytes accessed | tf_op | source)
XLA Modules:
  0.0 367.1 jit_solution(12796941628594289788)
XLA Ops:
  0.6 1.5 broadcast_in_dim.141
  2.1 11.5 %all-to-all-start = ((s32[32,4,4]{2,1,0:T(4,128)}), s32[32,4,4]{2,1,0:T(4,128)S(1)}, u32[]{:S(2)}, u32[]{:S(2)}) async-start(s32[32,4,4]{2,1,0:T(4,128)} %broadcast_in_dim.141), calls=%async_computation | async-start | bytes 131072 | tf_op jit(solution)/shard_map/all_to_all | solution.py:28
  13.6 9.9 %all-to-all-done = s32[32,4,4]{2,1,0:T(4,128)S(1)} async-done(((s32[32,4,4]{2,1,0:T(4,128)}), s32[32,4,4]{2,1,0:T(4,128)S(1)}, u32[]{:S(2)}, u32[]{:S(2)}) %all-to-all-start) | async-done | bytes 2080 | tf_op jit(solution)/shard_map/all_to_all | solution.py:28
  23.7 3.3 convolution_convert_fusion
  27.0 4.9 %all-to-all-start.1 = ((bf16[32,16,2048]{2,1,0:T(8,128)(2,1)}), bf16[32,16,2048]{2,1,0:T(8,128)(2,1)}, u32[]{:S(2)}, u32[]{:S(2)}) async-start(bf16[32,16,2048]{2,1,0:T(8,128)(2,1)} %bitcast.201), calls=%async_computation.1 | async-start | bytes 4194304 | tf_op jit(solution)/shard_map/all_to_all | solution.py:127
  32.0 5.3 %copy.510 = bf16[1,128,16,2,512]{4,2,3,1,0:T(8,128)(2,1)} copy(bf16[1,128,16,2,512]{4,3,2,1,0:T(2,128)(2,1)} %param.19) | data formatting | bytes 8388608 | tf_op args[4]
  38.6 5.0 %gather_fusion.1 = bf16[128,16,2,512]{3,1,2,0:T(8,128)(2,1)} fusion(bf16[128,16,2,512]{3,1,2,0:T(8,128)(2,1)} %bitcast.200, s32[1024]{0:T(1024)S(1)} %pad_clamp_fusion), kind=kCustom, calls=%fused_computation.1 | custom fusion | bytes 8389120 | tf_op jit(solution)/shard_map/jit(_take)/gather | solution.py:136
  43.6 8.8 %copy.379 = bf16[1,2048,3,512]{1,3,2,0:T(8,128)(2,1)} copy(bf16[1,2048,3,512]{3,1,2,0:T(8,128)(2,1)} %param.23) | data formatting | bytes 12582912 | tf_op args[8]
  52.5 29.1 %all-to-all-done.1 = bf16[32,16,2048]{2,1,0:T(8,128)(2,1)} async-done(((bf16[32,16,2048]{2,1,0:T(8,128)(2,1)}), bf16[32,16,2048]{2,1,0:T(8,128)(2,1)}, u32[]{:S(2)}, u32[]{:S(2)}) %all-to-all-start.1) | async-done | bytes 2097184 | tf_op jit(solution)/shard_map/all_to_all | solution.py:127
  81.6 1.9 reduce_sum.186
  84.2 4.8 %all-to-all-start.2 = ((bf16[4,16,2048]{2,1,0:T(8,128)(2,1)}), bf16[4,16,2048]{2,1,0:T(8,128)(2,1)S(1)}, u32[]{:S(2)}, u32[]{:S(2)}) async-start(bf16[4,16,2048]{2,1,0:T(8,128)(2,1)} %broadcast_in_dim.142), calls=%async_computation.2 | async-start | bytes 524288 | tf_op jit(solution)/shard_map/all_to_all | solution.py:28
  89.1 5.2 %all-to-all-done.2 = bf16[4,16,2048]{2,1,0:T(8,128)(2,1)S(1)} async-done(((bf16[4,16,2048]{2,1,0:T(8,128)(2,1)}), bf16[4,16,2048]{2,1,0:T(8,128)(2,1)S(1)}, u32[]{:S(2)}, u32[]{:S(2)}) %all-to-all-start.2) | async-done | bytes 262176 | tf_op jit(solution)/shard_map/all_to_all | solution.py:28
  94.5 4.5 %convolution_convert_fusion.2 = bf16[16,1536]{1,0:T(8,128)(2,1)S(1)} fusion(bf16[2048,1536]{0,1:T(8,128)(2,1)} %bitcast.198, bf16[16,2048]{1,0:T(8,128)(2,1)S(1)} %reduce_sum.187, f32[2048]{0:T(1024)S(1)} %bitcast.230, f32[16]{0:T(128)S(1)} %add_rsqrt_fusion.7), kind=kOutput, calls=%fused_computation.7 | convolution fusion | flops 100818944 | bytes 6414400 | tf_op jit(solution)/shard_map/dot_general | solution.py:160
  102.5 5.4 %all-to-all-start.4 = ((bf16[32,4,4,4,128]{4,2,3,1,0:T(4,128)(2,1)}), bf16[32,4,4,4,128]{4,2,3,1,0:T(4,128)(2,1)}, u32[]{:S(2)}, u32[]{:S(2)}) async-start(bf16[32,4,4,4,128]{4,2,3,1,0:T(4,128)(2,1)} %broadcast_in_dim.150), calls=%async_computation.4 | async-start | bytes 1048576 | tf_op jit(solution)/shard_map/all_to_all | solution.py:28
  107.9 4.7 %broadcast_select_fusion = bf16[128,16,2,512]{3,1,2,0:T(8,128)(2,1)} fusion(bf16[128,16,2,512]{3,1,2,0:T(8,128)(2,1)} %gather_fusion.1, pred[128]{0:T(512)(128)(4,1)S(1)} %get-tuple-element.27), kind=kLoop, calls=%fused_computation.4 | loop fusion | flops 2097152 | bytes 8388736 | tf_op jit(solution)/shard_map/jit(_take)/select_n | solution.py:136
  112.6 2.4 gather_fusion
  115.0 4.7 %fusion.124 = (bf16[128,16,1,512]{3,1,2,0:T(8,128)(2,1)}, bf16[128,16,1,512]{3,1,2,0:T(8,128)(2,1)}) fusion(bf16[128,16,2,512]{3,1,2,0:T(8,128)(2,1)} %broadcast_select_fusion), kind=kLoop, calls=%fused_computation.218 | loop fusion | bytes 8388608 | tf_op jit(solution)/shard_map/slice | solution.py:140
  119.7 4.5 %copy.386 = bf16[128,16,1,512]{0,3,1,2:T(8,128)(2,1)} copy(bf16[128,16,1,512]{3,1,2,0:T(8,128)(2,1)} %get-tuple-element.30) | data formatting | bytes 4194304 | tf_op jit(solution)/shard_map/slice | solution.py:140
  124.2 4.6 %copy.390 = bf16[128,16,4,128]{3,1,2,0:T(8,128)(2,1)} copy(bf16[128,16,4,128]{0,3,2,1:T(8,128)(2,1)} %bitcast.202) | data formatting | bytes 4194304 | tf_op jit(solution)/shard_map/reshape;squeeze | solution.py:140
  128.8 4.5 %copy.387 = bf16[128,16,1,512]{0,3,1,2:T(8,128)(2,1)} copy(bf16[128,16,1,512]{3,1,2,0:T(8,128)(2,1)} %get-tuple-element.31) | data formatting | bytes 4194304 | tf_op jit(solution)/shard_map/slice | solution.py:139
  133.4 4.6 %copy.389 = bf16[128,16,4,128]{3,1,2,0:T(8,128)(2,1)} copy(bf16[128,16,4,128]{0,3,2,1:T(8,128)(2,1)} %bitcast.203) | data formatting | bytes 4194304 | tf_op jit(solution)/shard_map/reshape;squeeze | solution.py:139
  139.4 9.9 %all-to-all-start.3 = ((f32[128,4,4,128]{3,2,1,0:T(4,128)}), f32[128,4,4,128]{3,2,1,0:T(4,128)S(1)}, u32[]{:S(2)}, u32[]{:S(2)}) async-start(f32[128,4,4,128]{3,2,1,0:T(4,128)} %broadcast_select_fusion.1), calls=%async_computation.3 | async-start | bytes 2097152 | tf_op jit(solution)/shard_map/all_to_all | solution.py:134
  149.6 3.9 %select_reduce_fusion.1 = (f32[128,4,4]{1,2,0:T(4,128)S(1)}, f32[128,4,4,16]{3,1,2,0:T(4,128)}) fusion(pred[128,4,16]{2,1,0:T(4,128)(4,1)S(1)} %broadcast_compare_fusion, f32[4]{0:T(128)S(1)} %bitcast.253, bf16[128,16,4,128]{3,1,2,0:T(8,128)(2,1)} %copy.389, bf16[128,4,4,128]{3,1,2,0:T(4,128)(2,1)} %bitcast.16), kind=kOutput, calls=%fused_computation.56 | convolution fusion | flops 8484864 | bytes 2768912 | tf_op jit(solution)/shard_map/rthd,rwhd->rthw/dot_general | solution.py:182
  153.5 1.6 copy.392
  155.1 3.1 fusion.28
  158.2 2.5 copy.391
  161.9 2.7 fusion.34
  166.0 7.3 %all-to-all-done.3 = f32[128,4,4,128]{3,2,1,0:T(4,128)S(1)} async-done(((f32[128,4,4,128]{3,2,1,0:T(4,128)}), f32[128,4,4,128]{3,2,1,0:T(4,128)S(1)}, u32[]{:S(2)}, u32[]{:S(2)}) %all-to-all-start.3) | async-done | bytes 1048608 | tf_op jit(solution)/shard_map/all_to_all | solution.py:134
  174.3 5.5 %all-to-all-start.5 = ((f32[32,4,4,5,128]{4,2,1,3,0:T(4,128)}), f32[32,4,4,5,128]{4,2,1,3,0:T(4,128)S(1)}, u32[]{:S(2)}, u32[]{:S(2)}) async-start(f32[32,4,4,5,128]{4,2,1,3,0:T(4,128)} %pad_maximum_fusion), calls=%async_computation.5 | async-start | bytes 2621440 | tf_op jit(solution)/shard_map/all_to_all | solution.py:210
  180.5 1.6 slice_reduce_fusion
  182.1 2.3 copy.511
  184.4 2.6 reshape.281.state_ref
  187.1 1.5 fusion.25
  195.0 2.1 select_reduce_fusion.3
  197.0 1.5 copy.407
  198.6 2.2 copy.382
  200.7 2.1 copy.381
  202.8 5.2 %shard_map.158 = (f32[4,128,512]{2,1,0:T(8,128)}, f32[4,4,512]{2,1,0:T(4,128)}) custom-call(f32[64]{0:T(128)} %reshape_reshape.6.beta_ref, f32[4,128,512]{2,1,0:T(8,128)} %reshape.281.state_ref, f32[4,4,128,4]{3,2,1,0:T(8,128)} %bitcast.208, f32[4,4,128,4]{3,2,1,0:T(8,128)} %bitcast.206, f32[4,4,512]{2,1,0:T(4,128)} %get-tuple-element.35.value_ref), custom_call_target="tpu_custom_call" | custom-call | flops 8388608 | bytes 2097152 | tf_op jit(solution)/shard_map/pallas_call | solution.py:67
  212.3 2.1 fusion.126
  223.6 1.6 fusion.46
  227.9 2.5 copy.402
  230.4 1.6 fusion.27
  234.5 1.5 collective-permute-start
  236.0 4.1 %collective-permute-done = f32[16,2048]{1,0:T(8,128)S(1)} collective-permute-done((f32[16,2048]{1,0:T(8,128)S(1)}, f32[16,2048]{1,0:T(8,128)S(1)}, u32[]{:S(2)}, u32[]{:S(2)}) %collective-permute-start) | collective-permute-done | bytes 131104 | tf_op jit(solution)/shard_map/ppermute | solution.py:36
  240.1 2.1 collective-permute-start.1
  242.1 4.5 %collective-permute-done.1 = f32[16,2048]{1,0:T(8,128)S(1)} collective-permute-done((f32[16,2048]{1,0:T(8,128)S(1)}, f32[16,2048]{1,0:T(8,128)S(1)}, u32[]{:S(2)}, u32[]{:S(2)}) %collective-permute-start.1) | collective-permute-done | bytes 131104 | tf_op jit(solution)/shard_map/ppermute | solution.py:36
  246.7 1.5 collective-permute-start.2
  249.5 4.6 %convolution_convert_fusion.1 = bf16[16,1536]{1,0:T(8,128)(2,1)S(1)} fusion(bf16[2048,1536]{0,1:T(8,128)(2,1)} %bitcast.199, bf16[16,2048]{1,0:T(8,128)(2,1)S(1)} %collective-permute-done.2, f32[16]{0:T(128)S(1)} %add_rsqrt_fusion.6, f32[2048]{0:T(1024)S(1)} %bitcast.231), kind=kOutput, calls=%fused_computation.6 | convolution fusion | flops 100818944 | bytes 6414400 | tf_op jit(solution)/shard_map/dot_general | solution.py:160
  256.8 27.5 %all_to_all.50 = bf16[32,4,4,4,128]{4,2,3,1,0:T(4,128)(2,1)S(1)} all-to-all(bf16[32,4,4,4,128]{4,2,3,1,0:T(4,128)(2,1)S(1)} %broadcast_in_dim.156), channel_id=1, replica_groups=mesh['section'=2,'req'=32,'head'=4] {'req'}, dimensions={0} | all-to-all | bytes 1048576 | tf_op jit(solution)/shard_map/all_to_all | solution.py:28
  284.3 3.1 select_reduce_fusion
  287.4 1.9 fusion.32
  292.7 2.6 pad_maximum_fusion.1
  295.3 4.8 %all-to-all-start.7 = ((f32[32,4,4,5,128]{4,2,1,3,0:T(4,128)}), f32[32,4,4,5,128]{4,2,1,3,0:T(4,128)S(1)}, u32[]{:S(2)}, u32[]{:S(2)}) async-start(f32[32,4,4,5,128]{4,2,1,3,0:T(4,128)} %pad_maximum_fusion.1), calls=%async_computation.7 | async-start | bytes 2621440 | tf_op jit(solution)/shard_map/all_to_all | solution.py:210
  302.6 1.5 select_reduce_fusion.2
  306.4 2.1 copy.417
  308.5 5.3 %shard_map.159 = (f32[4,128,512]{2,1,0:T(8,128)}, f32[4,4,512]{2,1,0:T(4,128)}) custom-call(f32[64]{0:T(128)} %reshape_reshape.7.beta_ref, f32[4,128,512]{2,1,0:T(8,128)} %reshape.281.state_ref, f32[4,4,128,4]{3,2,1,0:T(8,128)} %bitcast.207, f32[4,4,128,4]{3,2,1,0:T(8,128)} %bitcast.205, f32[4,4,512]{2,1,0:T(4,128)} %get-tuple-element.32.value_ref), custom_call_target="tpu_custom_call" | custom-call | flops 8388608 | bytes 2097152 | tf_op jit(solution)/shard_map/pallas_call | solution.py:67
  315.3 1.5 fusion.127
  316.8 16.2 %all-to-all-done.7 = f32[32,4,4,5,128]{4,2,1,3,0:T(4,128)S(1)} async-done(((f32[32,4,4,5,128]{4,2,1,3,0:T(4,128)}), f32[32,4,4,5,128]{4,2,1,3,0:T(4,128)S(1)}, u32[]{:S(2)}, u32[]{:S(2)}) %all-to-all-start.7) | async-done | bytes 1310752 | tf_op jit(solution)/shard_map/all_to_all | solution.py:210
  342.1 1.6 fusion.44
  346.4 2.5 copy.435
  348.9 1.6 fusion.26
  354.1 4.7 %collective-permute-done.3 = f32[16,2048]{1,0:T(8,128)S(1)} collective-permute-done((f32[16,2048]{1,0:T(8,128)S(1)}, f32[16,2048]{1,0:T(8,128)S(1)}, u32[]{:S(2)}, u32[]{:S(2)}) %collective-permute-start.3) | collective-permute-done | bytes 131104 | tf_op jit(solution)/shard_map/ppermute | solution.py:36
  358.8 2.4 collective-permute-start.4
  364.0 1.5 collective-permute-done.4
  (187 shorter events, 69.8 us)
Async XLA Ops:
  0.6 233.5 %copy-start = (bf16[1,512,2048]{2,1,0:T(8,128)(2,1)S(1)}, bf16[1,512,2048]{2,1,0:T(8,128)(2,1)}, u32[]{:S(2)}) copy-start(bf16[1,512,2048]{2,1,0:T(8,128)(2,1)} %param.24) | copy-start | bytes 6291460
  2.1 21.5 %all-to-all-start = ((s32[32,4,4]{2,1,0:T(4,128)}), s32[32,4,4]{2,1,0:T(4,128)S(1)}, u32[]{:S(2)}, u32[]{:S(2)}) async-start(s32[32,4,4]{2,1,0:T(4,128)} %broadcast_in_dim.141), calls=%async_computation | async-start | bytes 131072 | tf_op jit(solution)/shard_map/all_to_all | solution.py:28
  27.0 4.9 %copy-start.22 = (bf16[1,4,3,3,512]{4,1,3,2,0:T(4,128)(2,1)S(1)}, bf16[1,4,3,3,512]{4,1,3,2,0:T(4,128)(2,1)}, u32[]{:S(2)}) copy-start(bf16[1,4,3,3,512]{4,1,3,2,0:T(4,128)(2,1)} %param.21) | copy-start | bytes 110596
  27.0 54.6 %all-to-all-start.1 = ((bf16[32,16,2048]{2,1,0:T(8,128)(2,1)}), bf16[32,16,2048]{2,1,0:T(8,128)(2,1)}, u32[]{:S(2)}, u32[]{:S(2)}) async-start(bf16[32,16,2048]{2,1,0:T(8,128)(2,1)} %bitcast.201), calls=%async_computation.1 | async-start | bytes 4194304 | tf_op jit(solution)/shard_map/all_to_all | solution.py:127
  32.0 67.1 %copy-start.4 = (bf16[1,4,3,3,512]{4,2,1,3,0:T(4,128)(2,1)}, bf16[1,4,3,3,512]{4,2,1,3,0:T(4,128)(2,1)S(1)}, u32[]{:S(2)}) copy-start(bf16[1,4,3,3,512]{4,2,1,3,0:T(4,128)(2,1)S(1)} %copy.512) | copy-start | bytes 110596
  32.0 5.3 %copy-start.32 = (s32[128]{0:T(128)S(1)}, s32[128]{0:T(128)}, u32[]{:S(2)}) copy-start(s32[128]{0:T(128)} %param.16) | copy-start | bytes 1540
  32.0 5.3 %copy-start.1 = (s32[128]{0:T(128)S(1)}, s32[128]{0:T(128)}, u32[]{:S(2)}) copy-start(s32[128]{0:T(128)} %param.17) | copy-start | bytes 1540
  43.6 8.8 %copy-start.26 = (f32[1,4,3,512]{3,1,2,0:T(4,128)S(1)}, f32[1,4,3,512]{3,1,2,0:T(4,128)}, u32[]{:S(2)}) copy-start(f32[1,4,3,512]{3,1,2,0:T(4,128)} %param.26) | copy-start | bytes 73732
  52.5 42.0 %copy-start.23 = (f32[1,2048]{1,0:T(1,128)S(1)}, f32[1,2048]{1,0:T(1,128)}, u32[]{:S(2)}) copy-start(f32[1,2048]{1,0:T(1,128)} %param.27) | copy-start | bytes 24580
  52.5 46.7 %copy-start.12 = (f32[3,512]{1,0:T(4,128)}, f32[3,512]{1,0:T(4,128)S(1)}, u32[]{:S(2)}) copy-start(f32[3,512]{1,0:T(4,128)S(1)} %get-tuple-element.56) | copy-start | bytes 18436
  52.5 46.7 %copy-start.14 = (f32[3,512]{1,0:T(4,128)}, f32[3,512]{1,0:T(4,128)S(1)}, u32[]{:S(2)}) copy-start(f32[3,512]{1,0:T(4,128)S(1)} %get-tuple-element.57) | copy-start | bytes 18436
  52.5 46.7 %copy-start.16 = (f32[3,512]{1,0:T(4,128)}, f32[3,512]{1,0:T(4,128)S(1)}, u32[]{:S(2)}) copy-start(f32[3,512]{1,0:T(4,128)S(1)} %get-tuple-element.54) | copy-start | bytes 18436
  52.5 46.7 %copy-start.18 = (f32[3,512]{1,0:T(4,128)}, f32[3,512]{1,0:T(4,128)S(1)}, u32[]{:S(2)}) copy-start(f32[3,512]{1,0:T(4,128)S(1)} %get-tuple-element.55) | copy-start | bytes 18436
  84.2 10.0 %all-to-all-start.2 = ((bf16[4,16,2048]{2,1,0:T(8,128)(2,1)}), bf16[4,16,2048]{2,1,0:T(8,128)(2,1)S(1)}, u32[]{:S(2)}, u32[]{:S(2)}) async-start(bf16[4,16,2048]{2,1,0:T(8,128)(2,1)} %broadcast_in_dim.142), calls=%async_computation.2 | async-start | bytes 524288 | tf_op jit(solution)/shard_map/all_to_all | solution.py:28
  94.5 4.5 %copy-start.29 = (f32[16]{0:T(128)}, f32[16]{0:T(128)S(1)}, u32[]{:S(2)}) copy-start(f32[16]{0:T(128)S(1)} %add_rsqrt_fusion.7) | copy-start | bytes 196
  99.3 0.6 copy-start.6
  101.5 11.1 %copy-start.20 = (bf16[4,4,4,128]{3,2,1,0:T(4,128)(2,1)}, bf16[4,4,4,128]{3,2,1,0:T(4,128)(2,1)S(1)}, u32[]{:S(2)}) copy-start(bf16[4,4,4,128]{3,2,1,0:T(4,128)(2,1)S(1)} %get-tuple-element.28) | copy-start | bytes 49156
  102.5 36.9 %all-to-all-start.4 = ((bf16[32,4,4,4,128]{4,2,3,1,0:T(4,128)(2,1)}), bf16[32,4,4,4,128]{4,2,3,1,0:T(4,128)(2,1)}, u32[]{:S(2)}, u32[]{:S(2)}) async-start(bf16[32,4,4,4,128]{4,2,3,1,0:T(4,128)(2,1)} %broadcast_in_dim.150), calls=%async_computation.4 | async-start | bytes 1048576 | tf_op jit(solution)/shard_map/all_to_all | solution.py:28
  138.1 22.6 %copy-start.27 = (f32[128]{0:T(128)}, f32[128]{0:T(128)S(1)}, u32[]{:S(2)}) copy-start(f32[128]{0:T(128)S(1)} %pad.11.clone) | copy-start | bytes 1540
  138.1 11.5 %copy-start.34 = (f32[1,4]{1,0:T(1,128)S(1)}, f32[1,4]{1,0:T(1,128)}, u32[]{:S(2)}) copy-start(f32[1,4]{1,0:T(1,128)} %param.29) | copy-start | bytes 52
  139.4 34.0 %all-to-all-start.3 = ((f32[128,4,4,128]{3,2,1,0:T(4,128)}), f32[128,4,4,128]{3,2,1,0:T(4,128)S(1)}, u32[]{:S(2)}, u32[]{:S(2)}) async-start(f32[128,4,4,128]{3,2,1,0:T(4,128)} %broadcast_select_fusion.1), calls=%async_computation.3 | async-start | bytes 2097152 | tf_op jit(solution)/shard_map/all_to_all | solution.py:134
  173.4 1.0 copy-start.2
  174.3 40.1 %all-to-all-start.5 = ((f32[32,4,4,5,128]{4,2,1,3,0:T(4,128)}), f32[32,4,4,5,128]{4,2,1,3,0:T(4,128)S(1)}, u32[]{:S(2)}, u32[]{:S(2)}) async-start(f32[32,4,4,5,128]{4,2,1,3,0:T(4,128)} %pad_maximum_fusion), calls=%async_computation.5 | async-start | bytes 2621440 | tf_op jit(solution)/shard_map/all_to_all | solution.py:210
  179.8 0.7 copy-start.36
  232.0 17.5 %copy-start.24 = (f32[1,2048]{1,0:T(1,128)S(1)}, f32[1,2048]{1,0:T(1,128)}, u32[]{:S(2)}) copy-start(f32[1,2048]{1,0:T(1,128)} %param.27) | copy-start | bytes 24580
  234.5 5.5 %collective-permute-start = (f32[16,2048]{1,0:T(8,128)S(1)}, f32[16,2048]{1,0:T(8,128)S(1)}, u32[]{:S(2)}, u32[]{:S(2)}) collective-permute-start(f32[16,2048]{1,0:T(8,128)S(1)} %fusion.2), channel_id=1, source_target_pairs={{0,1},{1,0},{2,3},{3,2},{4,5},{5,4},{6,7},{7,6},{8,9},{9,8},{10,11... | collective-permute-start | bytes 393224 | tf_op jit(solution)/shard_map/ppermute | solution.py:36
  240.1 6.6 %collective-permute-start.1 = (f32[16,2048]{1,0:T(8,128)S(1)}, f32[16,2048]{1,0:T(8,128)S(1)}, u32[]{:S(2)}, u32[]{:S(2)}) collective-permute-start(f32[16,2048]{1,0:T(8,128)S(1)} %add.229), channel_id=1, source_target_pairs={{0,2},{1,3},{2,0},{3,1},{4,6},{5,7},{6,4},{7,5},{8,10},{9,11},{10,... | collective-permute-start | bytes 393224 | tf_op jit(solution)/shard_map/ppermute | solution.py:36
  246.6 2.3 copy-start.8
  246.7 2.2 collective-permute-start.2
  249.0 0.5 copy-start.30
  249.5 4.7 %copy-start.5 = (bf16[1,4,3,3,512]{4,2,1,3,0:T(4,128)(2,1)S(1)}, bf16[1,4,3,3,512]{4,2,1,3,0:T(4,128)(2,1)}, u32[]{:S(2)}) copy-start(bf16[1,4,3,3,512]{4,2,1,3,0:T(4,128)(2,1)} %copy-done.4) | copy-start | bytes 110596
  249.5 4.8 %copy-start.13 = (f32[3,512]{1,0:T(4,128)S(1)}, f32[3,512]{1,0:T(4,128)}, u32[]{:S(2)}) copy-start(f32[3,512]{1,0:T(4,128)} %copy-done.12) | copy-start | bytes 18436
  249.5 4.8 %copy-start.15 = (f32[3,512]{1,0:T(4,128)S(1)}, f32[3,512]{1,0:T(4,128)}, u32[]{:S(2)}) copy-start(f32[3,512]{1,0:T(4,128)} %copy-done.14) | copy-start | bytes 18436
  249.5 4.8 %copy-start.17 = (f32[3,512]{1,0:T(4,128)S(1)}, f32[3,512]{1,0:T(4,128)}, u32[]{:S(2)}) copy-start(f32[3,512]{1,0:T(4,128)} %copy-done.16) | copy-start | bytes 18436
  249.5 4.8 %copy-start.19 = (f32[3,512]{1,0:T(4,128)S(1)}, f32[3,512]{1,0:T(4,128)}, u32[]{:S(2)}) copy-start(f32[3,512]{1,0:T(4,128)} %copy-done.18) | copy-start | bytes 18436
  254.1 30.2 %copy-start.35 = (f32[1,4]{1,0:T(1,128)S(1)}, f32[1,4]{1,0:T(1,128)}, u32[]{:S(2)}) copy-start(f32[1,4]{1,0:T(1,128)} %param.29) | copy-start | bytes 52
  254.4 0.6 copy-start.7
  256.5 27.8 %copy-start.21 = (bf16[4,4,4,128]{3,2,1,0:T(4,128)(2,1)}, bf16[4,4,4,128]{3,2,1,0:T(4,128)(2,1)S(1)}, u32[]{:S(2)}) copy-start(bf16[4,4,4,128]{3,2,1,0:T(4,128)(2,1)S(1)} %get-tuple-element.20) | copy-start | bytes 49156
  284.3 3.1 copy-start.3
  289.3 3.1 copy-start.28
  292.6 7.5 %copy-start.25 = (f32[1,2048]{1,0:T(1,128)S(1)}, f32[1,2048]{1,0:T(1,128)}, u32[]{:S(2)}) copy-start(f32[1,2048]{1,0:T(1,128)} %param.27) | copy-start | bytes 24580
  292.6 7.5 %copy-start.31 = (f32[16]{0:T(128)S(1)}, f32[16]{0:T(128)}, u32[]{:S(2)}) copy-start(f32[16]{0:T(128)} %copy-done.30) | copy-start | bytes 196
  292.7 7.5 %copy-start.33 = (bf16[1,2048,4]{1,2,0:T(4,128)(2,1)S(1)}, bf16[1,2048,4]{1,2,0:T(4,128)(2,1)}, u32[]{:S(2)}) copy-start(bf16[1,2048,4]{1,2,0:T(4,128)(2,1)} %param.25) | copy-start | bytes 49156
  295.3 9.7 %copy-start.10 = (f32[4,4,4,128]{3,2,1,0:T(4,128)S(1)}, f32[4,4,4,128]{3,2,1,0:T(4,128)}, u32[]{:S(2)}) copy-start(f32[4,4,4,128]{3,2,1,0:T(4,128)} %get-tuple-element.21) | copy-start | bytes 98308
  295.3 37.8 %all-to-all-start.7 = ((f32[32,4,4,5,128]{4,2,1,3,0:T(4,128)}), f32[32,4,4,5,128]{4,2,1,3,0:T(4,128)S(1)}, u32[]{:S(2)}, u32[]{:S(2)}) async-start(f32[32,4,4,5,128]{4,2,1,3,0:T(4,128)} %pad_maximum_fusion.1), calls=%async_computation.7 | async-start | bytes 2621440 | tf_op jit(solution)/shard_map/all_to_all | solution.py:210
  308.5 29.5 %copy-start.11 = (f32[4,4,4,4]{1,3,2,0:T(4,128)S(1)}, f32[4,4,4,4]{1,3,2,0:T(4,128)}, u32[]{:S(2)}) copy-start(f32[4,4,4,4]{1,3,2,0:T(4,128)} %copy.440) | copy-start | bytes 3076
  352.9 5.9 %collective-permute-start.3 = (f32[16,2048]{1,0:T(8,128)S(1)}, f32[16,2048]{1,0:T(8,128)S(1)}, u32[]{:S(2)}, u32[]{:S(2)}) collective-permute-start(f32[16,2048]{1,0:T(8,128)S(1)} %fusion), channel_id=1, source_target_pairs={{0,1},{1,0},{2,3},{3,2},{4,5},{5,4},{6,7},{7,6},{8,9},{9,8},{10,11... | collective-permute-start | bytes 393224 | tf_op jit(solution)/shard_map/ppermute | solution.py:36
  358.8 6.7 %collective-permute-start.4 = (f32[16,2048]{1,0:T(8,128)S(1)}, f32[16,2048]{1,0:T(8,128)}, u32[]{:S(2)}, u32[]{:S(2)}) collective-permute-start(f32[16,2048]{1,0:T(8,128)S(1)} %add.246), channel_id=1, source_target_pairs={{0,2},{1,3},{2,0},{3,1},{4,6},{5,7},{6,4},{7,5},{8,10},{9,11},{10,... | collective-permute-start | bytes 393224 | tf_op jit(solution)/shard_map/ppermute | solution.py:36
  361.2 4.3 %copy-start.9 = (bf16[16,2048]{1,0:T(8,128)(2,1)S(1)}, bf16[16,2048]{1,0:T(8,128)(2,1)}, u32[]{:S(2)}) copy-start(bf16[16,2048]{1,0:T(8,128)(2,1)} %copy-done.8) | copy-start | bytes 196612
where the time goes:
time: 371 us; the launch traced here: 367 us
  local copies, waits for them, and re-layouts  108 us (29%)
  waiting for transfers between devices  83.2 us (22%)
  starting transfers between devices  55.4 us (15%)
  other arithmetic  43.7 us (12%)
  matrix products  37.7 us (10%)
  blocking collectives  27.5 us (7%)
  Pallas kernels  10.5 us (3%)
    all_to_all x1, waiting for transfers between devices, shards(): lax.all_to_all(looked_up.reshape(groups, rows, width), 'req', 0, 0, tiled...  29.1 us
    all_to_all x1, blocking collectives, spread(): return lax.all_to_all(copies, axis, 0, 0, tiled=True)  27.5 us
    all_to_all x3, starting transfers between devices, spread(): return lax.all_to_all(copies, axis, 0, 0, tiled=True)  21.7 us
    unnamed x80, local copies, waits for them, and re-layouts  17.7 us
    all_to_all x2, waiting for transfers between devices, layer(): gathered = lax.all_to_all(packed, 'req', 0, 0, tiled=True)  16.2 us
    all_to_all x3, waiting for transfers between devices, spread(): return lax.all_to_all(copies, axis, 0, 0, tiled=True)  15.2 us
    ppermute x4, waiting for transfers between devices, head_sum(): value = value + lax.ppermute(value, 'head', pairs)  14.8 us
    pallas_call x2, Pallas kernels, delta_rule(): pl.pallas_call(delta_rule_kernel, out_shape=(jax.ShapeDtypeStruct((slots,...  10.5 us
  transfers between devices with their start and end apart: 12, of which 10 were waited for; matrix products, arithmetic and copies ran while one was open for 31% of the time, Pallas kernels for 3%

commit v1 on v0

--- a/solution.py
+++ b/solution.py
@@ -42,22 +42,26 @@
     slots, key_rows, _ = state_ref.shape
     heads = key_ref.shape[1]
     tokens = value_ref.shape[1]
-    for s in range(slots):
-        for h in range(heads):
-            cols = pl.ds(h * key_rows, key_rows)
-            matrix = state_ref[s, :, cols]
-            key_cols = key_ref[s, h]
-            query_cols = query_ref[s, h]
-            for t in range(tokens):
-                k_t = key_cols[:, t : t + 1]
-                predicted = jnp.sum(matrix * k_t, axis=0, keepdims=True)
-                v_t = value_ref[s, pl.ds(t, 1), cols]
-                gate = beta_ref[(s * tokens + t) * heads + h]
-                matrix = matrix + gate * (k_t * (v_t - predicted))
-                read_out[s, pl.ds(t, 1), cols] = jnp.sum(
-                    matrix * query_cols[:, t : t + 1], axis=0, keepdims=True
-                )
-            state_out[s, :, cols] = matrix
+    def one_block(index, carry):
+        s = index // heads
+        h = index % heads
+        cols = pl.ds(pl.multiple_of(h * key_rows, key_rows), key_rows)
+        matrix = state_ref[s, :, cols]
+        key_cols = key_ref[s, h]
+        query_cols = query_ref[s, h]
+        for t in range(tokens):
+            k_t = key_cols[:, t : t + 1]
+            predicted = jnp.sum(matrix * k_t, axis=0, keepdims=True)
+            v_t = value_ref[s, pl.ds(t, 1), cols]
+            gate = beta_ref[(s * tokens + t) * heads + h]
+            matrix = matrix + gate * (k_t * (v_t - predicted))
+            read_out[s, pl.ds(t, 1), cols] = jnp.sum(
+                matrix * query_cols[:, t : t + 1], axis=0, keepdims=True
+            )
+        state_out[s, :, cols] = matrix
+        return carry
+
+    lax.fori_loop(0, slots * heads, one_block, 0)
 
 
 def delta_rule(start_state, key_vec, query_vec, value_vec, beta_gate):
@@ -133,11 +137,13 @@
     ordered_states = jnp.take(state_arrived[0], request_order, axis=0)
     start_state = lax.all_to_all(ordered_states, "req", 0, 1, tiled=True)
 
-    ordered_cache = jnp.take(cache_arrived[0], request_order, axis=0)
-    cache_rows = ordered_cache.shape[1]
-    all_slots = ordered_cache.shape[0]
-    stored_key_rows = ordered_cache[:, :, 0].reshape(all_slots, cache_rows, heads_dev, head_dim)
-    cache_values = ordered_cache[:, :, 1].reshape(all_slots, cache_rows, heads_dev, head_dim)
+    all_slots, cache_rows = cache_arrived.shape[1], cache_arrived.shape[2]
+    by_head = jnp.transpose(
+        cache_arrived[0].reshape(all_slots, cache_rows, 2, heads_dev, head_dim), (2, 0, 3, 1, 4)
+    )
+    ordered_cache = jnp.take(by_head, request_order, axis=1)
+    stored_key_rows = ordered_cache[0]
+    cache_values = ordered_cache[1]
     all_lengths = jnp.take(window_lengths, request_order)
     positions = group_index * cache_rows + jnp.arange(cache_rows, dtype=jnp.int32)
     new_index = jnp.arange(token_count, dtype=jnp.int32)
@@ -180,7 +186,7 @@
         )
         stored_scores = (
             jnp.einsum(
-                "rthd,rwhd->rthw",
+                "rthd,rhwd->rthw",
                 all_queries,
                 stored_key_rows,
                 preferred_element_type=jnp.float32,
@@ -191,7 +197,7 @@
         local_weights = jnp.where(cache_mask, jnp.exp(stored_scores - local_max[..., None]), 0.0)
         local_sum = jnp.sum(local_weights, axis=-1)
         local_part = jnp.einsum(
-            "rthw,rwhd->rthd",
+            "rthw,rhwd->rthd",
             local_weights.astype(jnp.bfloat16),
             cache_values,
             preferred_element_type=jnp.float32,

time: 371 us -> 350 us (0.943)
  waiting for transfers between devices: 83.2 us -> 74 us
  local copies, waits for them, and re-layouts: 108 us -> 99.9 us
  starting transfers between devices: 55.4 us -> 50.1 us
    all_to_all x1, waiting for transfers between devices: 29.1 us -> 10.9 us  [shards(): lax.all_to_all(looked_up.reshape(groups, rows, width), 'req', 0, 0, tiled...]
    slice x3 -> x0, local copies, waits for them, and re-layouts: 13.8 us -> none  [the longest x2 9.26 us: shards(): ordered_cache[:, :, 1].reshape(all_slots, cache_rows, heads_dev, head_dim)]
    all_to_all x3, waiting for transfers between devices: 15.2 us -> 28.5 us  [spread(): return lax.all_to_all(copies, axis, 0, 0, tiled=True)]
    unnamed x80 -> x86, local copies, waits for them, and re-layouts: 17.7 us -> 23.6 us
    all_to_all x1, starting transfers between devices: 9.88 us -> 4.24 us  [shards(): start_state = lax.all_to_all(ordered_states, 'req', 0, 1, tiled=True)]
    another operation x3 -> x2, local copies, waits for them, and re-layouts: 9.19 us -> 7.96 us  [the longest x1 7.96 us: shards(): cache_arrived[0].reshape(all_slots, cache_rows, 2, heads_dev, head_dim)]
  transfers between devices with their start and end apart: 12 -> 12, of which waited for: 10 -> 11; matrix products, arithmetic and copies ran while one was open for 31% -> 30% of each run, Pallas kernels for 3% -> 4%
where the time goes in v1:
time: 350 us; the launch traced here: 345 us
  local copies, waits for them, and re-layouts  99.9 us (29%)
  waiting for transfers between devices  74 us (21%)
  starting transfers between devices  50.1 us (14%)
  other arithmetic  42.2 us (12%)
  matrix products  37.4 us (11%)
  blocking collectives  27.5 us (8%)
  Pallas kernels  12.9 us (4%)
    all_to_all x3, waiting for transfers between devices, spread(): return lax.all_to_all(copies, axis, 0, 0, tiled=True)  28.5 us
    all_to_all x1, blocking collectives, spread(): return lax.all_to_all(copies, axis, 0, 0, tiled=True)  27.5 us
    unnamed x86, local copies, waits for them, and re-layouts  23.6 us
    all_to_all x3, starting transfers between devices, spread(): return lax.all_to_all(copies, axis, 0, 0, tiled=True)  21.7 us
    all_to_all x2, waiting for transfers between devices, layer(): gathered = lax.all_to_all(packed, 'req', 0, 0, tiled=True)  14.9 us
    ppermute x4, waiting for transfers between devices, head_sum(): value = value + lax.ppermute(value, 'head', pairs)  13.8 us
    pallas_call x2, Pallas kernels, delta_rule(): pl.pallas_call(delta_rule_kernel, out_shape=(jax.ShapeDtypeStruct((slots,...  12.9 us
    all_to_all x1, waiting for transfers between devices, shards(): lax.all_to_all(looked_up.reshape(groups, rows, width), 'req', 0, 0, tiled...  10.9 us
  transfers between devices with their start and end apart: 12, of which 11 were waited for; matrix products, arithmetic and copies ran while one was open for 30% of the time, Pallas kernels for 4%

profile of v1, /device:TPU:2, one launch (start us, length us, event | category | flops | bytes accessed | tf_op | source)
XLA Modules:
  0.0 345.4 jit_solution(12731005273827763697)
XLA Ops:
  0.6 1.5 broadcast_in_dim.141
  2.1 11.5 %all-to-all-start = ((s32[32,4,4]{2,1,0:T(4,128)}), s32[32,4,4]{2,1,0:T(4,128)S(1)}, u32[]{:S(2)}, u32[]{:S(2)}) async-start(s32[32,4,4]{2,1,0:T(4,128)} %broadcast_in_dim.141), calls=%async_computation | async-start | bytes 131072 | tf_op jit(solution)/shard_map/all_to_all | solution.py:28
  13.6 9.9 %all-to-all-done = s32[32,4,4]{2,1,0:T(4,128)S(1)} async-done(((s32[32,4,4]{2,1,0:T(4,128)}), s32[32,4,4]{2,1,0:T(4,128)S(1)}, u32[]{:S(2)}, u32[]{:S(2)}) %all-to-all-start) | async-done | bytes 2080 | tf_op jit(solution)/shard_map/all_to_all | solution.py:28
  23.7 3.3 convolution_convert_fusion
  27.0 4.9 %all-to-all-start.1 = ((bf16[32,16,2048]{2,1,0:T(8,128)(2,1)}), bf16[32,16,2048]{2,1,0:T(8,128)(2,1)}, u32[]{:S(2)}, u32[]{:S(2)}) async-start(bf16[32,16,2048]{2,1,0:T(8,128)(2,1)} %bitcast.217), calls=%async_computation.1 | async-start | bytes 4194304 | tf_op jit(solution)/shard_map/all_to_all | solution.py:131
  32.0 1.7 gather_fusion.2
  33.7 2.4 gather_fusion
  36.2 11.2 %copy.366 = bf16[1,128,16,2,512]{1,4,3,2,0:T(8,128)(2,1)} copy(bf16[1,128,16,2,512]{4,3,2,1,0:T(2,128)(2,1)} %param.19) | data formatting | bytes 8388608 | tf_op args[4]
  47.3 8.0 %copy.367 = bf16[128,16,2,4,128]{4,1,3,0,2:T(8,128)(2,1)} copy(bf16[128,16,2,4,128]{0,4,3,2,1:T(8,128)(2,1)} %bitcast.216) | data formatting | bytes 8388608 | tf_op jit(solution)/shard_map/reshape;squeeze | solution.py:142
  55.3 5.3 %gather_fusion.1 = bf16[128,2,4,16,128]{4,3,2,1,0:T(8,128)(2,1)} fusion(bf16[2,128,4,16,128]{4,3,2,1,0:T(8,128)(2,1)} %bitcast.215, s32[1024]{0:T(1024)S(1)} %pad_clamp_fusion), kind=kCustom, calls=%fused_computation.1 | custom fusion | bytes 8389120 | tf_op jit(solution)/shard_map/jit(_take)/gather | solution.py:144
  60.6 8.8 %copy.360 = bf16[1,2048,3,512]{1,3,2,0:T(8,128)(2,1)} copy(bf16[1,2048,3,512]{3,1,2,0:T(8,128)(2,1)} %param.23) | data formatting | bytes 12582912 | tf_op args[8]
  70.7 10.9 %all-to-all-done.1 = bf16[32,16,2048]{2,1,0:T(8,128)(2,1)} async-done(((bf16[32,16,2048]{2,1,0:T(8,128)(2,1)}), bf16[32,16,2048]{2,1,0:T(8,128)(2,1)}, u32[]{:S(2)}, u32[]{:S(2)}) %all-to-all-start.1) | async-done | bytes 2097184 | tf_op jit(solution)/shard_map/all_to_all | solution.py:131
  81.6 1.9 reduce_sum.186
  84.2 4.8 %all-to-all-start.2 = ((bf16[4,16,2048]{2,1,0:T(8,128)(2,1)}), bf16[4,16,2048]{2,1,0:T(8,128)(2,1)S(1)}, u32[]{:S(2)}, u32[]{:S(2)}) async-start(bf16[4,16,2048]{2,1,0:T(8,128)(2,1)} %broadcast_in_dim.142), calls=%async_computation.2 | async-start | bytes 524288 | tf_op jit(solution)/shard_map/all_to_all | solution.py:28
  89.1 5.2 %all-to-all-done.2 = bf16[4,16,2048]{2,1,0:T(8,128)(2,1)S(1)} async-done(((bf16[4,16,2048]{2,1,0:T(8,128)(2,1)}), bf16[4,16,2048]{2,1,0:T(8,128)(2,1)S(1)}, u32[]{:S(2)}, u32[]{:S(2)}) %all-to-all-start.2) | async-done | bytes 262176 | tf_op jit(solution)/shard_map/all_to_all | solution.py:28
  95.1 4.5 %convolution_convert_fusion.2 = bf16[16,1536]{1,0:T(8,128)(2,1)S(1)} fusion(bf16[2048,1536]{0,1:T(8,128)(2,1)} %bitcast.213, bf16[16,2048]{1,0:T(8,128)(2,1)S(1)} %reduce_sum.187, f32[2048]{0:T(1024)} %bitcast.243, f32[16]{0:T(128)S(1)} %add_rsqrt_fusion.7), kind=kOutput, calls=%fused_computation.7 | convolution fusion | flops 100818944 | bytes 6414400 | tf_op jit(solution)/shard_map/dot_general | solution.py:166
  102.5 5.4 %all-to-all-start.4 = ((bf16[32,4,4,4,128]{4,2,3,1,0:T(4,128)(2,1)}), bf16[32,4,4,4,128]{4,2,3,1,0:T(4,128)(2,1)}, u32[]{:S(2)}, u32[]{:S(2)}) async-start(bf16[32,4,4,4,128]{4,2,3,1,0:T(4,128)(2,1)} %broadcast_in_dim.150), calls=%async_computation.4 | async-start | bytes 1048576 | tf_op jit(solution)/shard_map/all_to_all | solution.py:28
  109.5 13.3 %all-to-all-done.4 = bf16[32,4,4,4,128]{4,2,3,1,0:T(4,128)(2,1)} async-done(((bf16[32,4,4,4,128]{4,2,3,1,0:T(4,128)(2,1)}), bf16[32,4,4,4,128]{4,2,3,1,0:T(4,128)(2,1)}, u32[]{:S(2)}, u32[]{:S(2)}) %all-to-all-start.4) | async-done | bytes 524320 | tf_op jit(solution)/shard_map/all_to_all | solution.py:28
  122.8 4.2 %all-to-all-start.3 = ((f32[128,4,4,128]{3,2,1,0:T(4,128)}), f32[128,4,4,128]{3,2,1,0:T(4,128)S(1)}, u32[]{:S(2)}, u32[]{:S(2)}) async-start(f32[128,4,4,128]{3,2,1,0:T(4,128)} %broadcast_select_fusion), calls=%async_computation.3 | async-start | bytes 2097152 | tf_op jit(solution)/shard_map/all_to_all | solution.py:138
  127.1 2.6 fusion
  129.7 3.7 %select_reduce_fusion.1 = (f32[128,4,4]{1,2,0:T(4,128)S(1)}, f32[128,4,4,16]{3,1,2,0:T(4,128)}) fusion(pred[128,4,16]{2,1,0:T(4,128)(4,1)S(1)} %broadcast_compare_fusion, f32[4]{0:T(128)S(1)} %bitcast.267, bf16[128,4,4,128]{3,1,2,0:T(4,128)(2,1)} %bitcast.18, bf16[2,128,4,16,128]{4,3,2,1,0:T(8,128)(2,1)S(1)} %fusion), kind=kOutput, calls=%fused_computation.62 | convolution fusion | flops 8484864 | bytes 2826752 | tf_op jit(solution)/shard_map/rthd,rhwd->rthw/dot_general | solution.py:188
  133.4 1.6 copy.371
  135.0 3.1 fusion.35
  138.1 2.5 copy.370
  141.9 2.7 fusion.6
  146.0 5.0 %all-to-all-done.3 = f32[128,4,4,128]{3,2,1,0:T(4,128)S(1)} async-done(((f32[128,4,4,128]{3,2,1,0:T(4,128)}), f32[128,4,4,128]{3,2,1,0:T(4,128)S(1)}, u32[]{:S(2)}, u32[]{:S(2)}) %all-to-all-start.3) | async-done | bytes 1048608 | tf_op jit(solution)/shard_map/all_to_all | solution.py:138
  152.0 5.5 %all-to-all-start.5 = ((f32[32,4,4,5,128]{4,2,1,3,0:T(4,128)}), f32[32,4,4,5,128]{4,2,1,3,0:T(4,128)S(1)}, u32[]{:S(2)}, u32[]{:S(2)}) async-start(f32[32,4,4,5,128]{4,2,1,3,0:T(4,128)} %pad_maximum_fusion), calls=%async_computation.5 | async-start | bytes 2621440 | tf_op jit(solution)/shard_map/all_to_all | solution.py:216
  158.1 1.6 slice_reduce_fusion
  159.7 2.3 copy.489
  162.1 2.6 reshape.281.state_ref
  164.7 1.5 fusion.32
  171.1 1.4 fusion.127
  172.5 2.1 select_reduce_fusion.3
  174.6 1.6 copy.386
  176.1 2.2 copy.363
  178.3 2.1 copy.362
  180.4 6.4 %shard_map.158 = (f32[4,128,512]{2,1,0:T(8,128)}, f32[4,4,512]{2,1,0:T(4,128)}) custom-call(f32[64]{0:T(128)} %reshape_reshape.6.beta_ref, f32[4,128,512]{2,1,0:T(8,128)} %reshape.281.state_ref, f32[4,4,128,4]{3,2,1,0:T(8,128)} %bitcast.222, f32[4,4,128,4]{3,2,1,0:T(8,128)} %bitcast.220, f32[4,4,512]{2,1,0:T(4,128)} %get-tuple-element.33.value_ref), custom_call_target="tpu_custom_call" | custom-call | flops 8388608 | bytes 2097152 | tf_op jit(solution)/shard_map/pallas_call | solution.py:71
  191.1 2.1 fusion.130
  198.1 1.5 fusion.75
  200.9 1.4 copy.391
  202.3 1.6 fusion.51
  206.7 2.5 copy.381
  209.2 1.6 fusion.34
  213.3 1.5 collective-permute-start
  214.7 4.0 %collective-permute-done = f32[16,2048]{1,0:T(8,128)S(1)} collective-permute-done((f32[16,2048]{1,0:T(8,128)S(1)}, f32[16,2048]{1,0:T(8,128)S(1)}, u32[]{:S(2)}, u32[]{:S(2)}) %collective-permute-start) | collective-permute-done | bytes 131104 | tf_op jit(solution)/shard_map/ppermute | solution.py:36
  218.7 2.1 collective-permute-start.1
  220.8 4.5 %collective-permute-done.1 = f32[16,2048]{1,0:T(8,128)S(1)} collective-permute-done((f32[16,2048]{1,0:T(8,128)S(1)}, f32[16,2048]{1,0:T(8,128)S(1)}, u32[]{:S(2)}, u32[]{:S(2)}) %collective-permute-start.1) | collective-permute-done | bytes 131104 | tf_op jit(solution)/shard_map/ppermute | solution.py:36
  228.3 4.6 %convolution_convert_fusion.1 = bf16[16,1536]{1,0:T(8,128)(2,1)S(1)} fusion(bf16[2048,1536]{0,1:T(8,128)(2,1)} %bitcast.214, bf16[16,2048]{1,0:T(8,128)(2,1)S(1)} %collective-permute-done.2, f32[16]{0:T(128)S(1)} %add_rsqrt_fusion.6, f32[2048]{0:T(1024)S(1)} %bitcast.245), kind=kOutput, calls=%fused_computation.6 | convolution fusion | flops 100818944 | bytes 6414400 | tf_op jit(solution)/shard_map/dot_general | solution.py:166
  235.5 27.5 %all_to_all.50 = bf16[32,4,4,4,128]{4,2,3,1,0:T(4,128)(2,1)S(1)} all-to-all(bf16[32,4,4,4,128]{4,2,3,1,0:T(4,128)(2,1)S(1)} %broadcast_in_dim.156), channel_id=1, replica_groups=mesh['section'=2,'req'=32,'head'=4] {'req'}, dimensions={0} | all-to-all | bytes 1048576 | tf_op jit(solution)/shard_map/all_to_all | solution.py:28
  263.0 3.1 select_reduce_fusion
  266.2 1.9 fusion.5
  271.4 2.6 pad_maximum_fusion.1
  274.0 4.8 %all-to-all-start.7 = ((f32[32,4,4,5,128]{4,2,1,3,0:T(4,128)}), f32[32,4,4,5,128]{4,2,1,3,0:T(4,128)S(1)}, u32[]{:S(2)}, u32[]{:S(2)}) async-start(f32[32,4,4,5,128]{4,2,1,3,0:T(4,128)} %pad_maximum_fusion.1), calls=%async_computation.7 | async-start | bytes 2621440 | tf_op jit(solution)/shard_map/all_to_all | solution.py:216
  281.4 1.5 select_reduce_fusion.2
  285.2 2.1 copy.396
  287.3 6.5 %shard_map.159 = (f32[4,128,512]{2,1,0:T(8,128)}, f32[4,4,512]{2,1,0:T(4,128)}) custom-call(f32[64]{0:T(128)} %reshape_reshape.7.beta_ref, f32[4,128,512]{2,1,0:T(8,128)} %reshape.281.state_ref, f32[4,4,128,4]{3,2,1,0:T(8,128)} %bitcast.221, f32[4,4,128,4]{3,2,1,0:T(8,128)} %bitcast.219, f32[4,4,512]{2,1,0:T(4,128)} %get-tuple-element.30.value_ref), custom_call_target="tpu_custom_call" | custom-call | flops 8388608 | bytes 2097152 | tf_op jit(solution)/shard_map/pallas_call | solution.py:71
  295.3 1.5 fusion.131
  296.8 14.9 %all-to-all-done.7 = f32[32,4,4,5,128]{4,2,1,3,0:T(4,128)S(1)} async-done(((f32[32,4,4,5,128]{4,2,1,3,0:T(4,128)}), f32[32,4,4,5,128]{4,2,1,3,0:T(4,128)S(1)}, u32[]{:S(2)}, u32[]{:S(2)}) %all-to-all-start.7) | async-done | bytes 1310752 | tf_op jit(solution)/shard_map/all_to_all | solution.py:216
  320.8 1.6 fusion.49
  325.1 2.5 copy.412
  327.6 1.6 fusion.33
  332.9 4.3 %collective-permute-done.3 = f32[16,2048]{1,0:T(8,128)S(1)} collective-permute-done((f32[16,2048]{1,0:T(8,128)S(1)}, f32[16,2048]{1,0:T(8,128)S(1)}, u32[]{:S(2)}, u32[]{:S(2)}) %collective-permute-start.3) | collective-permute-done | bytes 131104 | tf_op jit(solution)/shard_map/ppermute | solution.py:36
  337.2 2.8 collective-permute-start.4
  340.0 1.5 broadcast_select_fusion.1
  (189 shorter events, 66.7 us)
Async XLA Ops:
  0.6 212.2 %copy-start = (bf16[1,512,2048]{2,1,0:T(8,128)(2,1)S(1)}, bf16[1,512,2048]{2,1,0:T(8,128)(2,1)}, u32[]{:S(2)}) copy-start(bf16[1,512,2048]{2,1,0:T(8,128)(2,1)} %param.24) | copy-start | bytes 6291460
  2.1 21.5 %all-to-all-start = ((s32[32,4,4]{2,1,0:T(4,128)}), s32[32,4,4]{2,1,0:T(4,128)S(1)}, u32[]{:S(2)}, u32[]{:S(2)}) async-start(s32[32,4,4]{2,1,0:T(4,128)} %broadcast_in_dim.141), calls=%async_computation | async-start | bytes 131072 | tf_op jit(solution)/shard_map/all_to_all | solution.py:28
  27.0 4.9 %copy-start.23 = (bf16[1,4,3,3,512]{4,1,3,2,0:T(4,128)(2,1)S(1)}, bf16[1,4,3,3,512]{4,1,3,2,0:T(4,128)(2,1)}, u32[]{:S(2)}) copy-start(bf16[1,4,3,3,512]{4,1,3,2,0:T(4,128)(2,1)} %param.21) | copy-start | bytes 110596
  27.0 4.9 %copy-start.34 = (s32[128]{0:T(128)S(1)}, s32[128]{0:T(128)}, u32[]{:S(2)}) copy-start(s32[128]{0:T(128)} %param.16) | copy-start | bytes 1540
  27.0 5.0 %copy-start.1 = (s32[128]{0:T(128)S(1)}, s32[128]{0:T(128)}, u32[]{:S(2)}) copy-start(s32[128]{0:T(128)} %param.17) | copy-start | bytes 1540
  27.0 54.6 %all-to-all-start.1 = ((bf16[32,16,2048]{2,1,0:T(8,128)(2,1)}), bf16[32,16,2048]{2,1,0:T(8,128)(2,1)}, u32[]{:S(2)}, u32[]{:S(2)}) async-start(bf16[32,16,2048]{2,1,0:T(8,128)(2,1)} %bitcast.217), calls=%async_computation.1 | async-start | bytes 4194304 | tf_op jit(solution)/shard_map/all_to_all | solution.py:131
  32.0 67.7 %copy-start.5 = (bf16[1,4,3,3,512]{4,2,1,3,0:T(4,128)(2,1)}, bf16[1,4,3,3,512]{4,2,1,3,0:T(4,128)(2,1)S(1)}, u32[]{:S(2)}) copy-start(bf16[1,4,3,3,512]{4,2,1,3,0:T(4,128)(2,1)S(1)} %copy.490) | copy-start | bytes 110596
  60.6 10.1 %copy-start.26 = (f32[1,4,3,512]{3,1,2,0:T(4,128)S(1)}, f32[1,4,3,512]{3,1,2,0:T(4,128)}, u32[]{:S(2)}) copy-start(f32[1,4,3,512]{3,1,2,0:T(4,128)} %param.26) | copy-start | bytes 73732
  70.7 29.1 %copy-start.13 = (f32[3,512]{1,0:T(4,128)}, f32[3,512]{1,0:T(4,128)S(1)}, u32[]{:S(2)}) copy-start(f32[3,512]{1,0:T(4,128)S(1)} %get-tuple-element.54) | copy-start | bytes 18436
  70.7 29.1 %copy-start.15 = (f32[3,512]{1,0:T(4,128)}, f32[3,512]{1,0:T(4,128)S(1)}, u32[]{:S(2)}) copy-start(f32[3,512]{1,0:T(4,128)S(1)} %get-tuple-element.55) | copy-start | bytes 18436
  84.2 10.0 %all-to-all-start.2 = ((bf16[4,16,2048]{2,1,0:T(8,128)(2,1)}), bf16[4,16,2048]{2,1,0:T(8,128)(2,1)S(1)}, u32[]{:S(2)}, u32[]{:S(2)}) async-start(bf16[4,16,2048]{2,1,0:T(8,128)(2,1)} %broadcast_in_dim.142), calls=%async_computation.2 | async-start | bytes 524288 | tf_op jit(solution)/shard_map/all_to_all | solution.py:28
  89.1 10.7 %copy-start.17 = (f32[3,512]{1,0:T(4,128)}, f32[3,512]{1,0:T(4,128)S(1)}, u32[]{:S(2)}) copy-start(f32[3,512]{1,0:T(4,128)S(1)} %get-tuple-element.52) | copy-start | bytes 18436
  89.1 10.7 %copy-start.19 = (f32[3,512]{1,0:T(4,128)}, f32[3,512]{1,0:T(4,128)S(1)}, u32[]{:S(2)}) copy-start(f32[3,512]{1,0:T(4,128)S(1)} %get-tuple-element.53) | copy-start | bytes 18436
  94.5 0.6 copy-start.30
  99.6 8.3 %copy-start.27 = (s32[128]{0:T(128)S(1)}, s32[128]{0:T(128)}, u32[]{:S(2)}) copy-start(s32[128]{0:T(128)} %gather_fusion.2) | copy-start | bytes 1540
  99.6 8.3 %copy-start.35 = (s32[128]{0:T(128)S(1)}, s32[128]{0:T(128)}, u32[]{:S(2)}) copy-start(s32[128]{0:T(128)} %param.16) | copy-start | bytes 1540
  99.6 8.3 %copy-start.31 = (s32[4]{0:T(128)S(1)}, s32[4]{0:T(128)}, u32[]{:S(2)}) copy-start(s32[4]{0:T(128)} %iota_add_fusion.1) | copy-start | bytes 52
  99.9 9.6 %copy-start.7 = (f32[4,4,3,512]{3,1,0,2:T(4,128)}, f32[4,4,3,512]{3,1,0,2:T(4,128)S(1)}, u32[]{:S(2)}) copy-start(f32[4,4,3,512]{3,1,0,2:T(4,128)S(1)} %divide_multiply_fusion.1) | copy-start | bytes 294916
  101.4 6.5 %copy-start.21 = (bf16[4,4,4,128]{3,2,1,0:T(4,128)(2,1)}, bf16[4,4,4,128]{3,2,1,0:T(4,128)(2,1)S(1)}, u32[]{:S(2)}) copy-start(bf16[4,4,4,128]{3,2,1,0:T(4,128)(2,1)S(1)} %get-tuple-element.28) | copy-start | bytes 49156
  102.5 20.4 %all-to-all-start.4 = ((bf16[32,4,4,4,128]{4,2,3,1,0:T(4,128)(2,1)}), bf16[32,4,4,4,128]{4,2,3,1,0:T(4,128)(2,1)}, u32[]{:S(2)}, u32[]{:S(2)}) async-start(bf16[32,4,4,4,128]{4,2,3,1,0:T(4,128)(2,1)} %broadcast_in_dim.150), calls=%async_computation.4 | async-start | bytes 1048576 | tf_op jit(solution)/shard_map/all_to_all | solution.py:28
  122.8 28.1 %all-to-all-start.3 = ((f32[128,4,4,128]{3,2,1,0:T(4,128)}), f32[128,4,4,128]{3,2,1,0:T(4,128)S(1)}, u32[]{:S(2)}, u32[]{:S(2)}) async-start(f32[128,4,4,128]{3,2,1,0:T(4,128)} %broadcast_select_fusion), calls=%async_computation.3 | async-start | bytes 2097152 | tf_op jit(solution)/shard_map/all_to_all | solution.py:138
  127.1 2.6 copy-start.37
  129.7 3.7 %copy-start.2 = (bf16[2,128,4,16,128]{4,3,2,1,0:T(8,128)(2,1)}, bf16[2,128,4,16,128]{4,3,2,1,0:T(8,128)(2,1)S(1)}, u32[]{:S(2)}) copy-start(bf16[2,128,4,16,128]{4,3,2,1,0:T(8,128)(2,1)S(1)} %fusion) | copy-start | bytes 12582916
  133.4 7.2 %copy-start.28 = (f32[128]{0:T(128)S(1)}, f32[128]{0:T(128)}, u32[]{:S(2)}) copy-start(f32[128]{0:T(128)} %pad.11.clone) | copy-start | bytes 1540
  151.0 1.0 copy-start.4
  152.0 41.2 %all-to-all-start.5 = ((f32[32,4,4,5,128]{4,2,1,3,0:T(4,128)}), f32[32,4,4,5,128]{4,2,1,3,0:T(4,128)S(1)}, u32[]{:S(2)}, u32[]{:S(2)}) async-start(f32[32,4,4,5,128]{4,2,1,3,0:T(4,128)} %pad_maximum_fusion), calls=%async_computation.5 | async-start | bytes 2621440 | tf_op jit(solution)/shard_map/all_to_all | solution.py:216
  157.5 0.7 copy-start.39
  210.8 17.4 %copy-start.24 = (f32[1,2048]{1,0:T(1,128)S(1)}, f32[1,2048]{1,0:T(1,128)}, u32[]{:S(2)}) copy-start(f32[1,2048]{1,0:T(1,128)} %param.27) | copy-start | bytes 24580
  213.3 5.4 %collective-permute-start = (f32[16,2048]{1,0:T(8,128)S(1)}, f32[16,2048]{1,0:T(8,128)S(1)}, u32[]{:S(2)}, u32[]{:S(2)}) collective-permute-start(f32[16,2048]{1,0:T(8,128)S(1)} %fusion.3), channel_id=1, source_target_pairs={{0,1},{1,0},{2,3},{3,2},{4,5},{5,4},{6,7},{7,6},{8,9},{9,8},{10,11... | collective-permute-start | bytes 393224 | tf_op jit(solution)/shard_map/ppermute | solution.py:36
  218.7 6.6 %collective-permute-start.1 = (f32[16,2048]{1,0:T(8,128)S(1)}, f32[16,2048]{1,0:T(8,128)S(1)}, u32[]{:S(2)}, u32[]{:S(2)}) collective-permute-start(f32[16,2048]{1,0:T(8,128)S(1)} %add.229), channel_id=1, source_target_pairs={{0,2},{1,3},{2,0},{3,1},{4,6},{5,7},{6,4},{7,5},{8,10},{9,11},{10,... | collective-permute-start | bytes 393224 | tf_op jit(solution)/shard_map/ppermute | solution.py:36
  225.3 2.3 copy-start.9
  225.3 2.2 collective-permute-start.2
  227.6 0.6 copy-start.32
  228.2 4.7 %copy-start.6 = (bf16[1,4,3,3,512]{4,2,1,3,0:T(4,128)(2,1)S(1)}, bf16[1,4,3,3,512]{4,2,1,3,0:T(4,128)(2,1)}, u32[]{:S(2)}) copy-start(bf16[1,4,3,3,512]{4,2,1,3,0:T(4,128)(2,1)} %copy-done.5) | copy-start | bytes 110596
  228.2 4.8 %copy-start.14 = (f32[3,512]{1,0:T(4,128)S(1)}, f32[3,512]{1,0:T(4,128)}, u32[]{:S(2)}) copy-start(f32[3,512]{1,0:T(4,128)} %copy-done.13) | copy-start | bytes 18436
  228.2 4.8 %copy-start.16 = (f32[3,512]{1,0:T(4,128)S(1)}, f32[3,512]{1,0:T(4,128)}, u32[]{:S(2)}) copy-start(f32[3,512]{1,0:T(4,128)} %copy-done.15) | copy-start | bytes 18436
  228.2 4.8 %copy-start.18 = (f32[3,512]{1,0:T(4,128)S(1)}, f32[3,512]{1,0:T(4,128)}, u32[]{:S(2)}) copy-start(f32[3,512]{1,0:T(4,128)} %copy-done.17) | copy-start | bytes 18436
  228.3 4.8 %copy-start.20 = (f32[3,512]{1,0:T(4,128)S(1)}, f32[3,512]{1,0:T(4,128)}, u32[]{:S(2)}) copy-start(f32[3,512]{1,0:T(4,128)} %copy-done.19) | copy-start | bytes 18436
  232.8 30.2 %copy-start.38 = (f32[1,4]{1,0:T(1,128)S(1)}, f32[1,4]{1,0:T(1,128)}, u32[]{:S(2)}) copy-start(f32[1,4]{1,0:T(1,128)} %param.29) | copy-start | bytes 52
  233.2 0.6 copy-start.8
  235.3 27.8 %copy-start.22 = (bf16[4,4,4,128]{3,2,1,0:T(4,128)(2,1)}, bf16[4,4,4,128]{3,2,1,0:T(4,128)(2,1)S(1)}, u32[]{:S(2)}) copy-start(bf16[4,4,4,128]{3,2,1,0:T(4,128)(2,1)S(1)} %get-tuple-element.20) | copy-start | bytes 49156
  263.0 3.1 copy-start.3
  268.0 3.1 copy-start.29
  271.4 7.5 %copy-start.25 = (f32[1,2048]{1,0:T(1,128)S(1)}, f32[1,2048]{1,0:T(1,128)}, u32[]{:S(2)}) copy-start(f32[1,2048]{1,0:T(1,128)} %param.27) | copy-start | bytes 24580
  271.4 7.5 %copy-start.33 = (f32[16]{0:T(128)S(1)}, f32[16]{0:T(128)}, u32[]{:S(2)}) copy-start(f32[16]{0:T(128)} %copy-done.32) | copy-start | bytes 196
  271.4 7.5 %copy-start.36 = (bf16[1,2048,4]{1,2,0:T(4,128)(2,1)S(1)}, bf16[1,2048,4]{1,2,0:T(4,128)(2,1)}, u32[]{:S(2)}) copy-start(bf16[1,2048,4]{1,2,0:T(4,128)(2,1)} %param.25) | copy-start | bytes 49156
  274.0 9.8 %copy-start.11 = (f32[4,4,4,128]{3,2,1,0:T(4,128)S(1)}, f32[4,4,4,128]{3,2,1,0:T(4,128)}, u32[]{:S(2)}) copy-start(f32[4,4,4,128]{3,2,1,0:T(4,128)} %get-tuple-element.21) | copy-start | bytes 98308
  274.0 37.7 %all-to-all-start.7 = ((f32[32,4,4,5,128]{4,2,1,3,0:T(4,128)}), f32[32,4,4,5,128]{4,2,1,3,0:T(4,128)S(1)}, u32[]{:S(2)}, u32[]{:S(2)}) async-start(f32[32,4,4,5,128]{4,2,1,3,0:T(4,128)} %pad_maximum_fusion.1), calls=%async_computation.7 | async-start | bytes 2621440 | tf_op jit(solution)/shard_map/all_to_all | solution.py:216
  287.3 29.4 %copy-start.12 = (f32[4,4,4,4]{1,3,2,0:T(4,128)S(1)}, f32[4,4,4,4]{1,3,2,0:T(4,128)}, u32[]{:S(2)}) copy-start(f32[4,4,4,4]{1,3,2,0:T(4,128)} %copy.417) | copy-start | bytes 3076
  331.6 5.6 %collective-permute-start.3 = (f32[16,2048]{1,0:T(8,128)S(1)}, f32[16,2048]{1,0:T(8,128)S(1)}, u32[]{:S(2)}, u32[]{:S(2)}) collective-permute-start(f32[16,2048]{1,0:T(8,128)S(1)} %fusion.1), channel_id=1, source_target_pairs={{0,1},{1,0},{2,3},{3,2},{4,5},{5,4},{6,7},{7,6},{8,9},{9,8},{10,11... | collective-permute-start | bytes 393224 | tf_op jit(solution)/shard_map/ppermute | solution.py:36
  337.2 6.7 %collective-permute-start.4 = (f32[16,2048]{1,0:T(8,128)S(1)}, f32[16,2048]{1,0:T(8,128)}, u32[]{:S(2)}, u32[]{:S(2)}) collective-permute-start(f32[16,2048]{1,0:T(8,128)S(1)} %add.246), channel_id=1, source_target_pairs={{0,2},{1,3},{2,0},{3,1},{4,6},{5,7},{6,4},{7,5},{8,10},{9,11},{10,... | collective-permute-start | bytes 393224 | tf_op jit(solution)/shard_map/ppermute | solution.py:36
  340.0 3.8 %copy-start.10 = (bf16[16,2048]{1,0:T(8,128)(2,1)S(1)}, bf16[16,2048]{1,0:T(8,128)(2,1)}, u32[]{:S(2)}) copy-start(bf16[16,2048]{1,0:T(8,128)(2,1)} %copy-done.9) | copy-start | bytes 196612

commit v2 on v1

--- a/solution.py
+++ b/solution.py
@@ -158,7 +158,13 @@
     scale = score_scale_table[0]
     gain_head = out_gain[0].reshape(heads_dev, head_dim)
     history = conv_history[0]
-    fresh_mask = (new_index[None, :] <= new_index[:, None])[None, :, None, :]
+    home_mask = jnp.concatenate(
+        [
+            jnp.ones((token_count, sink_count), jnp.bool_),
+            new_index[None, :] <= new_index[:, None],
+        ],
+        axis=1,
+    )[None, :, None, :]
 
     def layer(stream):
         normed = rms_scale(stream.astype(jnp.float32), pre_gain[0]).astype(jnp.bfloat16)
@@ -220,45 +226,29 @@
 
         delta_state, readout = delta_rule(start_state, key_vec, query_vec, value_vec, beta_gate)
 
-        new_keys = key_vec.astype(jnp.bfloat16)
-        new_values = value_vec.astype(jnp.bfloat16)
-        anchor_scores = (
+        home_keys = jnp.concatenate([anchor_key_rows, key_vec.astype(jnp.bfloat16)], axis=1)
+        home_values = jnp.concatenate([sink_values, value_vec.astype(jnp.bfloat16)], axis=1)
+        home_scores = (
             jnp.einsum(
-                "sthd,sjhd->sthj", query_halfwidth, anchor_key_rows, preferred_element_type=jnp.float32
+                "sthd,sjhd->sthj", query_halfwidth, home_keys, preferred_element_type=jnp.float32
             )
             * scale[None, None, :, None]
         )
-        incoming_scores = (
-            jnp.einsum(
-                "sthd,suhd->sthu", query_halfwidth, new_keys, preferred_element_type=jnp.float32
-            )
-            * scale[None, None, :, None]
-        )
-        highest = jnp.maximum(
-            jnp.max(anchor_scores, axis=-1),
-            jnp.max(jnp.where(fresh_mask, incoming_scores, negative_big), axis=-1),
-        )
-        highest = jnp.maximum(highest, jnp.max(part_max, axis=0))
+        home_max = jnp.max(jnp.where(home_mask, home_scores, negative_big), axis=-1)
+        home_weights = jnp.where(home_mask, jnp.exp(home_scores - home_max[..., None]), 0.0)
+        home_sum = jnp.sum(home_weights, axis=-1)
+        home_part = jnp.einsum(
+            "sthj,sjhd->sthd",
+            home_weights.astype(jnp.bfloat16),
+            home_values,
+            preferred_element_type=jnp.float32,
+        )
+        highest = jnp.maximum(home_max, jnp.max(part_max, axis=0))
         part_scale = jnp.exp(part_max - highest[None])
-        sink_weights = jnp.exp(anchor_scores - highest[..., None])
-        fresh_weights = jnp.where(fresh_mask, jnp.exp(incoming_scores - highest[..., None]), 0.0)
-        weight_sum = (
-            jnp.sum(part_scale * part_sum, axis=0)
-            + jnp.sum(sink_weights, axis=-1)
-            + jnp.sum(fresh_weights, axis=-1)
-        )
-        numerator = jnp.sum(part_scale[..., None] * part_numer, axis=0)
-        numerator = numerator + jnp.einsum(
-            "sthj,sjhd->sthd",
-            sink_weights.astype(jnp.bfloat16),
-            sink_values,
-            preferred_element_type=jnp.float32,
-        )
-        numerator = numerator + jnp.einsum(
-            "sthu,suhd->sthd",
-            fresh_weights.astype(jnp.bfloat16),
-            new_values,
-            preferred_element_type=jnp.float32,
+        home_scale = jnp.exp(home_max - highest)
+        weight_sum = home_scale * home_sum + jnp.sum(part_scale * part_sum, axis=0)
+        numerator = home_scale[..., None] * home_part + jnp.sum(
+            part_scale[..., None] * part_numer, axis=0
         )
         attended = numerator / weight_sum[..., None]
         mixed_heads = (

time: 350 us -> 330 us (0.943)
  local copies, waits for them, and re-layouts: 99.9 us -> 92 us
  matrix products: 37.4 us -> 30.3 us
  other arithmetic: 42.2 us -> 37.7 us
    dot_general x8 -> x4, matrix products: 11.2 us -> 4.01 us  [the longest x2 2.05 us: layer(): jnp.einsum('sthj,sjhd->sthd', home_weights.astype(jnp.bfloat16), home_val...]
    reduce_sum x4 -> x2, local copies, waits for them, and re-layouts: 5.55 us -> 1.51 us  [layer(): weight_sum = home_scale * home_sum + jnp.sum(part_scale * part_sum, axis=0)]
    convert_element_type x0 -> x4, local copies, waits for them, and re-layouts: none -> 3.94 us  [the longest x2 2.73 us: layer(): value_vec.astype(jnp.bfloat16)]
    unnamed x86 -> x75, local copies, waits for them, and re-layouts: 23.6 us -> 22.8 us
  transfers between devices with their start and end apart: 12 -> 12, of which waited for: 11 -> 11; matrix products, arithmetic and copies ran while one was open for 30% -> 31% of each run, Pallas kernels for 4% -> 4%
where the time goes in v2:
time: 330 us; the launch traced here: 326 us
  local copies, waits for them, and re-layouts  92 us (28%)
  waiting for transfers between devices  74.1 us (22%)
  starting transfers between devices  50.1 us (15%)
  other arithmetic  37.7 us (11%)
  matrix products  30.3 us (9%)
  blocking collectives  27.5 us (8%)
  Pallas kernels  12.9 us (4%)
    all_to_all x3, waiting for transfers between devices, spread(): return lax.all_to_all(copies, axis, 0, 0, tiled=True)  28.5 us
    all_to_all x1, blocking collectives, spread(): return lax.all_to_all(copies, axis, 0, 0, tiled=True)  27.5 us
    unnamed x75, local copies, waits for them, and re-layouts  22.8 us
    all_to_all x3, starting transfers between devices, spread(): return lax.all_to_all(copies, axis, 0, 0, tiled=True)  21.7 us
    all_to_all x2, waiting for transfers between devices, layer(): gathered = lax.all_to_all(packed, 'req', 0, 0, tiled=True)  15 us
    ppermute x4, waiting for transfers between devices, head_sum(): value = value + lax.ppermute(value, 'head', pairs)  13.8 us
    pallas_call x2, Pallas kernels, delta_rule(): pl.pallas_call(delta_rule_kernel, out_shape=(jax.ShapeDtypeStruct((slots,...  12.9 us
    all_to_all x1, waiting for transfers between devices, shards(): lax.all_to_all(looked_up.reshape(groups, rows, width), 'req', 0, 0, tiled...  10.8 us
  transfers between devices with their start and end apart: 12, of which 11 were waited for; matrix products, arithmetic and copies ran while one was open for 31% of the time, Pallas kernels for 4%

profile of v2, /device:TPU:2, one launch (start us, length us, event | category | flops | bytes accessed | tf_op | source)
XLA Modules:
  0.0 325.9 jit_solution(6209939395867816202)
XLA Ops:
  0.6 1.5 broadcast_in_dim.135
  2.1 11.5 %all-to-all-start = ((s32[32,4,4]{2,1,0:T(4,128)}), s32[32,4,4]{2,1,0:T(4,128)S(1)}, u32[]{:S(2)}, u32[]{:S(2)}) async-start(s32[32,4,4]{2,1,0:T(4,128)} %broadcast_in_dim.135), calls=%async_computation | async-start | bytes 131072 | tf_op jit(solution)/shard_map/all_to_all | solution.py:28
  13.6 9.9 %all-to-all-done = s32[32,4,4]{2,1,0:T(4,128)S(1)} async-done(((s32[32,4,4]{2,1,0:T(4,128)}), s32[32,4,4]{2,1,0:T(4,128)S(1)}, u32[]{:S(2)}, u32[]{:S(2)}) %all-to-all-start) | async-done | bytes 2080 | tf_op jit(solution)/shard_map/all_to_all | solution.py:28
  23.7 3.3 %convolution_convert_fusion = bf16[512,2048]{1,0:T(8,128)(2,1)} fusion(bf16[250,2048]{1,0:T(8,128)(2,1)} %param.18, s32[250]{0:T(256)S(1)} %iota_add_fusion, s32[512]{0:T(512)S(1)} %eq.19), kind=kOutput, calls=%fused_computation.5 | convolution fusion | flops 525464576 | bytes 3124200 | tf_op jit(solution)/shard_map/dot_general | solution.py:130
  27.0 4.9 %all-to-all-start.1 = ((bf16[32,16,2048]{2,1,0:T(8,128)(2,1)}), bf16[32,16,2048]{2,1,0:T(8,128)(2,1)}, u32[]{:S(2)}, u32[]{:S(2)}) async-start(bf16[32,16,2048]{2,1,0:T(8,128)(2,1)} %bitcast.191), calls=%async_computation.1 | async-start | bytes 4194304 | tf_op jit(solution)/shard_map/all_to_all | solution.py:131
  32.0 1.8 gather_fusion.2
  33.8 2.4 gather_fusion
  36.2 11.2 %copy.338 = bf16[1,128,16,2,512]{1,4,3,2,0:T(8,128)(2,1)} copy(bf16[1,128,16,2,512]{4,3,2,1,0:T(2,128)(2,1)} %param.19) | data formatting | bytes 8388608 | tf_op args[4]
  47.4 8.0 %copy.339 = bf16[128,16,2,4,128]{4,1,3,0,2:T(8,128)(2,1)} copy(bf16[128,16,2,4,128]{0,4,3,2,1:T(8,128)(2,1)} %bitcast.190) | data formatting | bytes 8388608 | tf_op jit(solution)/shard_map/reshape;squeeze | solution.py:142
  55.4 5.3 %gather_fusion.1 = bf16[128,2,4,16,128]{4,3,2,1,0:T(8,128)(2,1)} fusion(bf16[2,128,4,16,128]{4,3,2,1,0:T(8,128)(2,1)} %bitcast.189, s32[1024]{0:T(1024)S(1)} %pad_clamp_fusion), kind=kCustom, calls=%fused_computation.1 | custom fusion | bytes 8389120 | tf_op jit(solution)/shard_map/jit(_take)/gather | solution.py:144
  60.7 8.8 %copy.329 = bf16[1,2048,3,512]{1,3,2,0:T(8,128)(2,1)} copy(bf16[1,2048,3,512]{3,1,2,0:T(8,128)(2,1)} %param.23) | data formatting | bytes 12582912 | tf_op args[8]
  70.8 10.8 %all-to-all-done.1 = bf16[32,16,2048]{2,1,0:T(8,128)(2,1)} async-done(((bf16[32,16,2048]{2,1,0:T(8,128)(2,1)}), bf16[32,16,2048]{2,1,0:T(8,128)(2,1)}, u32[]{:S(2)}, u32[]{:S(2)}) %all-to-all-start.1) | async-done | bytes 2097184 | tf_op jit(solution)/shard_map/all_to_all | solution.py:131
  81.6 1.9 reduce_sum.168
  84.2 4.8 %all-to-all-start.2 = ((bf16[4,16,2048]{2,1,0:T(8,128)(2,1)}), bf16[4,16,2048]{2,1,0:T(8,128)(2,1)S(1)}, u32[]{:S(2)}, u32[]{:S(2)}) async-start(bf16[4,16,2048]{2,1,0:T(8,128)(2,1)} %broadcast_in_dim.136), calls=%async_computation.2 | async-start | bytes 524288 | tf_op jit(solution)/shard_map/all_to_all | solution.py:28
  89.1 5.2 %all-to-all-done.2 = bf16[4,16,2048]{2,1,0:T(8,128)(2,1)S(1)} async-done(((bf16[4,16,2048]{2,1,0:T(8,128)(2,1)}), bf16[4,16,2048]{2,1,0:T(8,128)(2,1)S(1)}, u32[]{:S(2)}, u32[]{:S(2)}) %all-to-all-start.2) | async-done | bytes 262176 | tf_op jit(solution)/shard_map/all_to_all | solution.py:28
  95.0 4.5 %convolution_convert_fusion.2 = bf16[16,1536]{1,0:T(8,128)(2,1)S(1)} fusion(bf16[2048,1536]{0,1:T(8,128)(2,1)} %bitcast.187, bf16[16,2048]{1,0:T(8,128)(2,1)S(1)} %reduce_sum.169, f32[2048]{0:T(1024)} %bitcast.213, f32[16]{0:T(128)S(1)} %add_rsqrt_fusion.7), kind=kOutput, calls=%fused_computation.7 | convolution fusion | flops 100818944 | bytes 6414400 | tf_op jit(solution)/shard_map/dot_general | solution.py:172
  102.4 5.4 %all-to-all-start.4 = ((bf16[32,4,4,4,128]{4,2,3,1,0:T(4,128)(2,1)}), bf16[32,4,4,4,128]{4,2,3,1,0:T(4,128)(2,1)}, u32[]{:S(2)}, u32[]{:S(2)}) async-start(bf16[32,4,4,4,128]{4,2,3,1,0:T(4,128)(2,1)} %broadcast_in_dim.146), calls=%async_computation.4 | async-start | bytes 1048576 | tf_op jit(solution)/shard_map/all_to_all | solution.py:28
  109.4 13.4 %all-to-all-done.4 = bf16[32,4,4,4,128]{4,2,3,1,0:T(4,128)(2,1)} async-done(((bf16[32,4,4,4,128]{4,2,3,1,0:T(4,128)(2,1)}), bf16[32,4,4,4,128]{4,2,3,1,0:T(4,128)(2,1)}, u32[]{:S(2)}, u32[]{:S(2)}) %all-to-all-start.4) | async-done | bytes 524320 | tf_op jit(solution)/shard_map/all_to_all | solution.py:28
  122.8 4.2 %all-to-all-start.3 = ((f32[128,4,4,128]{3,2,1,0:T(4,128)}), f32[128,4,4,128]{3,2,1,0:T(4,128)S(1)}, u32[]{:S(2)}, u32[]{:S(2)}) async-start(f32[128,4,4,128]{3,2,1,0:T(4,128)} %broadcast_select_fusion), calls=%async_computation.3 | async-start | bytes 2097152 | tf_op jit(solution)/shard_map/all_to_all | solution.py:138
  127.1 2.6 fusion
  129.7 3.7 %select_reduce_fusion.1 = (f32[128,4,4]{1,2,0:T(4,128)S(1)}, f32[128,4,4,16]{3,1,2,0:T(4,128)}) fusion(pred[128,4,16]{2,1,0:T(4,128)(4,1)S(1)} %broadcast_compare_fusion, f32[4]{0:T(128)S(1)} %bitcast.233, bf16[128,4,4,128]{3,1,2,0:T(4,128)(2,1)} %bitcast.21, bf16[2,128,4,16,128]{4,3,2,1,0:T(8,128)(2,1)S(1)} %fusion), kind=kOutput, calls=%fused_computation.56 | convolution fusion | flops 8484864 | bytes 2826752 | tf_op jit(solution)/shard_map/rthd,rhwd->rthw/dot_general | solution.py:194
  133.4 1.6 copy.343
  135.0 3.1 fusion.33
  138.0 2.5 copy.342
  141.8 2.7 fusion.6
  144.5 1.4 pad_maximum_fusion
  145.9 5.1 %all-to-all-done.3 = f32[128,4,4,128]{3,2,1,0:T(4,128)S(1)} async-done(((f32[128,4,4,128]{3,2,1,0:T(4,128)}), f32[128,4,4,128]{3,2,1,0:T(4,128)S(1)}, u32[]{:S(2)}, u32[]{:S(2)}) %all-to-all-start.3) | async-done | bytes 1048608 | tf_op jit(solution)/shard_map/all_to_all | solution.py:138
  151.9 5.5 %all-to-all-start.5 = ((f32[32,4,4,5,128]{4,2,1,3,0:T(4,128)}), f32[32,4,4,5,128]{4,2,1,3,0:T(4,128)S(1)}, u32[]{:S(2)}, u32[]{:S(2)}) async-start(f32[32,4,4,5,128]{4,2,1,3,0:T(4,128)} %pad_maximum_fusion), calls=%async_computation.5 | async-start | bytes 2621440 | tf_op jit(solution)/shard_map/all_to_all | solution.py:222
  158.0 1.6 slice_reduce_fusion.1
  159.6 2.3 copy.419
  162.0 2.6 reshape.268.state_ref
  164.6 1.5 fusion.30
  168.7 1.4 reshape_squeeze.27
  171.0 1.4 fusion.115
  173.0 2.2 copy.332
  175.2 2.1 copy.331
  177.3 6.4 %shard_map.158 = (f32[4,128,512]{2,1,0:T(8,128)}, f32[4,4,512]{2,1,0:T(4,128)}) custom-call(f32[64]{0:T(128)} %reshape_reshape.6.beta_ref, f32[4,128,512]{2,1,0:T(8,128)} %reshape.268.state_ref, f32[4,4,128,4]{3,2,1,0:T(8,128)} %bitcast.196, f32[4,4,128,4]{3,2,1,0:T(8,128)} %bitcast.194, f32[4,4,512]{2,1,0:T(4,128)} %get-tuple-element.33.value_ref), custom_call_target="tpu_custom_call" | custom-call | flops 8388608 | bytes 2097152 | tf_op jit(solution)/shard_map/pallas_call | solution.py:71
  183.7 1.4 reshape.270
  186.6 1.4 copy.333
  189.0 1.4 fusion.77
  192.6 1.4 copy.346
  195.3 1.4 copy.349
  196.6 2.2 fusion.49
  198.9 1.4 copy.353
  200.3 2.5 copy.350
  203.6 1.6 fusion.32
  206.7 1.5 collective-permute-start
  208.1 4.0 %collective-permute-done = f32[16,2048]{1,0:T(8,128)S(1)} collective-permute-done((f32[16,2048]{1,0:T(8,128)S(1)}, f32[16,2048]{1,0:T(8,128)S(1)}, u32[]{:S(2)}, u32[]{:S(2)}) %collective-permute-start) | collective-permute-done | bytes 131104 | tf_op jit(solution)/shard_map/ppermute | solution.py:36
  212.1 2.1 collective-permute-start.1
  214.2 4.5 %collective-permute-done.1 = f32[16,2048]{1,0:T(8,128)S(1)} collective-permute-done((f32[16,2048]{1,0:T(8,128)S(1)}, f32[16,2048]{1,0:T(8,128)S(1)}, u32[]{:S(2)}, u32[]{:S(2)}) %collective-permute-start.1) | collective-permute-done | bytes 131104 | tf_op jit(solution)/shard_map/ppermute | solution.py:36
  221.6 4.5 %convolution_convert_fusion.1 = bf16[16,1536]{1,0:T(8,128)(2,1)S(1)} fusion(bf16[2048,1536]{0,1:T(8,128)(2,1)} %bitcast.188, bf16[16,2048]{1,0:T(8,128)(2,1)S(1)} %collective-permute-done.2, f32[16]{0:T(128)S(1)} %add_rsqrt_fusion.6, f32[2048]{0:T(1024)S(1)} %bitcast.215), kind=kOutput, calls=%fused_computation.6 | convolution fusion | flops 100818944 | bytes 6414400 | tf_op jit(solution)/shard_map/dot_general | solution.py:172
  228.8 27.5 %all_to_all.50 = bf16[32,4,4,4,128]{4,2,3,1,0:T(4,128)(2,1)S(1)} all-to-all(bf16[32,4,4,4,128]{4,2,3,1,0:T(4,128)(2,1)S(1)} %broadcast_in_dim.150), channel_id=1, replica_groups=mesh['section'=2,'req'=32,'head'=4] {'req'}, dimensions={0} | all-to-all | bytes 1048576 | tf_op jit(solution)/shard_map/all_to_all | solution.py:28
  256.3 3.1 select_reduce_fusion
  259.4 1.9 fusion.5
  264.7 2.6 pad_maximum_fusion.1
  267.3 4.8 %all-to-all-start.7 = ((f32[32,4,4,5,128]{4,2,1,3,0:T(4,128)}), f32[32,4,4,5,128]{4,2,1,3,0:T(4,128)S(1)}, u32[]{:S(2)}, u32[]{:S(2)}) async-start(f32[32,4,4,5,128]{4,2,1,3,0:T(4,128)} %pad_maximum_fusion.1), calls=%async_computation.7 | async-start | bytes 2621440 | tf_op jit(solution)/shard_map/all_to_all | solution.py:222
  276.7 2.1 copy.357
  278.8 6.4 %shard_map.159 = (f32[4,128,512]{2,1,0:T(8,128)}, f32[4,4,512]{2,1,0:T(4,128)}) custom-call(f32[64]{0:T(128)} %reshape_reshape.7.beta_ref, f32[4,128,512]{2,1,0:T(8,128)} %reshape.268.state_ref, f32[4,4,128,4]{3,2,1,0:T(8,128)} %bitcast.195, f32[4,4,128,4]{3,2,1,0:T(8,128)} %bitcast.193, f32[4,4,512]{2,1,0:T(4,128)} %get-tuple-element.30.value_ref), custom_call_target="tpu_custom_call" | custom-call | flops 8388608 | bytes 2097152 | tf_op jit(solution)/shard_map/pallas_call | solution.py:71
  290.0 15.0 %all-to-all-done.7 = f32[32,4,4,5,128]{4,2,1,3,0:T(4,128)S(1)} async-done(((f32[32,4,4,5,128]{4,2,1,3,0:T(4,128)}), f32[32,4,4,5,128]{4,2,1,3,0:T(4,128)S(1)}, u32[]{:S(2)}, u32[]{:S(2)}) %all-to-all-start.7) | async-done | bytes 1310752 | tf_op jit(solution)/shard_map/all_to_all | solution.py:222
  306.5 2.5 copy.373
  309.0 1.6 fusion.31
  313.3 4.3 %collective-permute-done.3 = f32[16,2048]{1,0:T(8,128)S(1)} collective-permute-done((f32[16,2048]{1,0:T(8,128)S(1)}, f32[16,2048]{1,0:T(8,128)S(1)}, u32[]{:S(2)}, u32[]{:S(2)}) %collective-permute-start.3) | collective-permute-done | bytes 131104 | tf_op jit(solution)/shard_map/ppermute | solution.py:36
  317.7 2.8 collective-permute-start.4
  320.5 1.5 broadcast_select_fusion.1
  (173 shorter events, 48.6 us)
Async XLA Ops:
  0.6 205.6 %copy-start = (bf16[1,512,2048]{2,1,0:T(8,128)(2,1)S(1)}, bf16[1,512,2048]{2,1,0:T(8,128)(2,1)}, u32[]{:S(2)}) copy-start(bf16[1,512,2048]{2,1,0:T(8,128)(2,1)} %param.24) | copy-start | bytes 6291460
  2.1 21.5 %all-to-all-start = ((s32[32,4,4]{2,1,0:T(4,128)}), s32[32,4,4]{2,1,0:T(4,128)S(1)}, u32[]{:S(2)}, u32[]{:S(2)}) async-start(s32[32,4,4]{2,1,0:T(4,128)} %broadcast_in_dim.135), calls=%async_computation | async-start | bytes 131072 | tf_op jit(solution)/shard_map/all_to_all | solution.py:28
  27.0 4.9 %copy-start.18 = (bf16[1,4,3,3,512]{4,1,3,2,0:T(4,128)(2,1)S(1)}, bf16[1,4,3,3,512]{4,1,3,2,0:T(4,128)(2,1)}, u32[]{:S(2)}) copy-start(bf16[1,4,3,3,512]{4,1,3,2,0:T(4,128)(2,1)} %param.21) | copy-start | bytes 110596
  27.0 4.9 %copy-start.30 = (s32[128]{0:T(128)S(1)}, s32[128]{0:T(128)}, u32[]{:S(2)}) copy-start(s32[128]{0:T(128)} %param.16) | copy-start | bytes 1540
  27.0 5.0 %copy-start.1 = (s32[128]{0:T(128)S(1)}, s32[128]{0:T(128)}, u32[]{:S(2)}) copy-start(s32[128]{0:T(128)} %param.17) | copy-start | bytes 1540
  27.0 54.6 %all-to-all-start.1 = ((bf16[32,16,2048]{2,1,0:T(8,128)(2,1)}), bf16[32,16,2048]{2,1,0:T(8,128)(2,1)}, u32[]{:S(2)}, u32[]{:S(2)}) async-start(bf16[32,16,2048]{2,1,0:T(8,128)(2,1)} %bitcast.191), calls=%async_computation.1 | async-start | bytes 4194304 | tf_op jit(solution)/shard_map/all_to_all | solution.py:131
  32.0 67.6 %copy-start.7 = (bf16[1,4,3,3,512]{4,2,1,3,0:T(4,128)(2,1)}, bf16[1,4,3,3,512]{4,2,1,3,0:T(4,128)(2,1)S(1)}, u32[]{:S(2)}) copy-start(bf16[1,4,3,3,512]{4,2,1,3,0:T(4,128)(2,1)S(1)} %copy.420) | copy-start | bytes 110596
  60.7 10.1 %copy-start.22 = (f32[1,4,3,512]{3,1,2,0:T(4,128)S(1)}, f32[1,4,3,512]{3,1,2,0:T(4,128)}, u32[]{:S(2)}) copy-start(f32[1,4,3,512]{3,1,2,0:T(4,128)} %param.26) | copy-start | bytes 73732
  84.2 10.0 %all-to-all-start.2 = ((bf16[4,16,2048]{2,1,0:T(8,128)(2,1)}), bf16[4,16,2048]{2,1,0:T(8,128)(2,1)S(1)}, u32[]{:S(2)}, u32[]{:S(2)}) async-start(bf16[4,16,2048]{2,1,0:T(8,128)(2,1)} %broadcast_in_dim.136), calls=%async_computation.2 | async-start | bytes 524288 | tf_op jit(solution)/shard_map/all_to_all | solution.py:28
  89.1 10.6 %copy-start.12 = (f32[3,512]{1,0:T(4,128)}, f32[3,512]{1,0:T(4,128)S(1)}, u32[]{:S(2)}) copy-start(f32[3,512]{1,0:T(4,128)S(1)} %get-tuple-element.48) | copy-start | bytes 18436
  89.1 10.6 %copy-start.14 = (f32[3,512]{1,0:T(4,128)}, f32[3,512]{1,0:T(4,128)S(1)}, u32[]{:S(2)}) copy-start(f32[3,512]{1,0:T(4,128)S(1)} %get-tuple-element.49) | copy-start | bytes 18436
  94.5 0.5 copy-start.26
  99.5 8.3 %copy-start.24 = (s32[128]{0:T(128)S(1)}, s32[128]{0:T(128)}, u32[]{:S(2)}) copy-start(s32[128]{0:T(128)} %gather_fusion.2) | copy-start | bytes 1540
  99.5 8.3 %copy-start.31 = (s32[128]{0:T(128)S(1)}, s32[128]{0:T(128)}, u32[]{:S(2)}) copy-start(s32[128]{0:T(128)} %param.16) | copy-start | bytes 1540
  99.5 8.3 %copy-start.27 = (s32[4]{0:T(128)S(1)}, s32[4]{0:T(128)}, u32[]{:S(2)}) copy-start(s32[4]{0:T(128)} %iota_add_fusion.1) | copy-start | bytes 52
  99.9 9.6 %copy-start.5 = (f32[4,4,3,512]{3,1,0,2:T(4,128)}, f32[4,4,3,512]{3,1,0,2:T(4,128)S(1)}, u32[]{:S(2)}) copy-start(f32[4,4,3,512]{3,1,0,2:T(4,128)S(1)} %divide_multiply_fusion.1) | copy-start | bytes 294916
  101.3 6.5 %copy-start.17 = (bf16[4,4,4,128]{3,2,1,0:T(4,128)(2,1)}, bf16[4,4,4,128]{3,2,1,0:T(4,128)(2,1)S(1)}, u32[]{:S(2)}) copy-start(bf16[4,4,4,128]{3,2,1,0:T(4,128)(2,1)S(1)} %get-tuple-element.28) | copy-start | bytes 49156
  102.4 20.4 %all-to-all-start.4 = ((bf16[32,4,4,4,128]{4,2,3,1,0:T(4,128)(2,1)}), bf16[32,4,4,4,128]{4,2,3,1,0:T(4,128)(2,1)}, u32[]{:S(2)}, u32[]{:S(2)}) async-start(bf16[32,4,4,4,128]{4,2,3,1,0:T(4,128)(2,1)} %broadcast_in_dim.146), calls=%async_computation.4 | async-start | bytes 1048576 | tf_op jit(solution)/shard_map/all_to_all | solution.py:28
  122.8 28.1 %all-to-all-start.3 = ((f32[128,4,4,128]{3,2,1,0:T(4,128)}), f32[128,4,4,128]{3,2,1,0:T(4,128)S(1)}, u32[]{:S(2)}, u32[]{:S(2)}) async-start(f32[128,4,4,128]{3,2,1,0:T(4,128)} %broadcast_select_fusion), calls=%async_computation.3 | async-start | bytes 2097152 | tf_op jit(solution)/shard_map/all_to_all | solution.py:138
  127.1 2.6 copy-start.33
  129.7 3.7 %copy-start.2 = (bf16[2,128,4,16,128]{4,3,2,1,0:T(8,128)(2,1)}, bf16[2,128,4,16,128]{4,3,2,1,0:T(8,128)(2,1)S(1)}, u32[]{:S(2)}) copy-start(bf16[2,128,4,16,128]{4,3,2,1,0:T(8,128)(2,1)S(1)} %fusion) | copy-start | bytes 12582916
  150.9 1.0 copy-start.4
  151.9 39.8 %all-to-all-start.5 = ((f32[32,4,4,5,128]{4,2,1,3,0:T(4,128)}), f32[32,4,4,5,128]{4,2,1,3,0:T(4,128)S(1)}, u32[]{:S(2)}, u32[]{:S(2)}) async-start(f32[32,4,4,5,128]{4,2,1,3,0:T(4,128)} %pad_maximum_fusion), calls=%async_computation.5 | async-start | bytes 2621440 | tf_op jit(solution)/shard_map/all_to_all | solution.py:222
  189.0 1.4 copy-start.16
  189.0 1.4 copy-start.21
  205.2 16.4 %copy-start.19 = (f32[1,2048]{1,0:T(1,128)S(1)}, f32[1,2048]{1,0:T(1,128)}, u32[]{:S(2)}) copy-start(f32[1,2048]{1,0:T(1,128)} %param.27) | copy-start | bytes 24580
  206.7 5.4 %collective-permute-start = (f32[16,2048]{1,0:T(8,128)S(1)}, f32[16,2048]{1,0:T(8,128)S(1)}, u32[]{:S(2)}, u32[]{:S(2)}) collective-permute-start(f32[16,2048]{1,0:T(8,128)S(1)} %fusion.3), channel_id=1, source_target_pairs={{0,1},{1,0},{2,3},{3,2},{4,5},{5,4},{6,7},{7,6},{8,9},{9,8},{10,11... | collective-permute-start | bytes 393224 | tf_op jit(solution)/shard_map/ppermute | solution.py:36
  212.1 6.6 %collective-permute-start.1 = (f32[16,2048]{1,0:T(8,128)S(1)}, f32[16,2048]{1,0:T(8,128)S(1)}, u32[]{:S(2)}, u32[]{:S(2)}) collective-permute-start(f32[16,2048]{1,0:T(8,128)S(1)} %add.207), channel_id=1, source_target_pairs={{0,2},{1,3},{2,0},{3,1},{4,6},{5,7},{6,4},{7,5},{8,10},{9,11},{10,... | collective-permute-start | bytes 393224 | tf_op jit(solution)/shard_map/ppermute | solution.py:36
  218.7 2.3 copy-start.9
  218.7 2.2 collective-permute-start.2
  221.0 0.6 copy-start.28
  221.6 4.6 %copy-start.8 = (bf16[1,4,3,3,512]{4,2,1,3,0:T(4,128)(2,1)S(1)}, bf16[1,4,3,3,512]{4,2,1,3,0:T(4,128)(2,1)}, u32[]{:S(2)}) copy-start(bf16[1,4,3,3,512]{4,2,1,3,0:T(4,128)(2,1)} %copy-done.7) | copy-start | bytes 110596
  221.6 4.7 %copy-start.13 = (f32[3,512]{1,0:T(4,128)S(1)}, f32[3,512]{1,0:T(4,128)}, u32[]{:S(2)}) copy-start(f32[3,512]{1,0:T(4,128)} %copy-done.12) | copy-start | bytes 18436
  221.6 4.7 %copy-start.15 = (f32[3,512]{1,0:T(4,128)S(1)}, f32[3,512]{1,0:T(4,128)}, u32[]{:S(2)}) copy-start(f32[3,512]{1,0:T(4,128)} %copy-done.14) | copy-start | bytes 18436
  226.1 30.2 %copy-start.34 = (f32[1,4]{1,0:T(1,128)S(1)}, f32[1,4]{1,0:T(1,128)}, u32[]{:S(2)}) copy-start(f32[1,4]{1,0:T(1,128)} %param.29) | copy-start | bytes 52
  226.5 0.6 copy-start.6
  256.3 3.1 copy-start.3
  261.3 3.1 copy-start.25
  264.7 7.5 %copy-start.20 = (f32[1,2048]{1,0:T(1,128)S(1)}, f32[1,2048]{1,0:T(1,128)}, u32[]{:S(2)}) copy-start(f32[1,2048]{1,0:T(1,128)} %param.27) | copy-start | bytes 24580
  264.7 7.5 %copy-start.29 = (f32[16]{0:T(128)S(1)}, f32[16]{0:T(128)}, u32[]{:S(2)}) copy-start(f32[16]{0:T(128)} %copy-done.28) | copy-start | bytes 196
  264.7 7.5 %copy-start.32 = (bf16[1,2048,4]{1,2,0:T(4,128)(2,1)S(1)}, bf16[1,2048,4]{1,2,0:T(4,128)(2,1)}, u32[]{:S(2)}) copy-start(bf16[1,2048,4]{1,2,0:T(4,128)(2,1)} %param.25) | copy-start | bytes 49156
  267.3 8.0 %copy-start.11 = (f32[4,4,4,128]{3,2,1,0:T(4,128)S(1)}, f32[4,4,4,128]{3,2,1,0:T(4,128)}, u32[]{:S(2)}) copy-start(f32[4,4,4,128]{3,2,1,0:T(4,128)} %get-tuple-element.19) | copy-start | bytes 98308
  267.3 37.7 %all-to-all-start.7 = ((f32[32,4,4,5,128]{4,2,1,3,0:T(4,128)}), f32[32,4,4,5,128]{4,2,1,3,0:T(4,128)S(1)}, u32[]{:S(2)}, u32[]{:S(2)}) async-start(f32[32,4,4,5,128]{4,2,1,3,0:T(4,128)} %pad_maximum_fusion.1), calls=%async_computation.7 | async-start | bytes 2621440 | tf_op jit(solution)/shard_map/all_to_all | solution.py:222
  287.8 22.8 %copy-start.23 = (f32[4,4,4]{1,2,0:T(4,128)S(1)}, f32[4,4,4]{1,2,0:T(4,128)}, u32[]{:S(2)}) copy-start(f32[4,4,4]{1,2,0:T(4,128)} %copy.359) | copy-start | bytes 772
  312.0 5.6 %collective-permute-start.3 = (f32[16,2048]{1,0:T(8,128)S(1)}, f32[16,2048]{1,0:T(8,128)S(1)}, u32[]{:S(2)}, u32[]{:S(2)}) collective-permute-start(f32[16,2048]{1,0:T(8,128)S(1)} %fusion.1), channel_id=1, source_target_pairs={{0,1},{1,0},{2,3},{3,2},{4,5},{5,4},{6,7},{7,6},{8,9},{9,8},{10,11... | collective-permute-start | bytes 393224 | tf_op jit(solution)/shard_map/ppermute | solution.py:36
  317.7 6.7 %collective-permute-start.4 = (f32[16,2048]{1,0:T(8,128)S(1)}, f32[16,2048]{1,0:T(8,128)}, u32[]{:S(2)}, u32[]{:S(2)}) collective-permute-start(f32[16,2048]{1,0:T(8,128)S(1)} %add.222), channel_id=1, source_target_pairs={{0,2},{1,3},{2,0},{3,1},{4,6},{5,7},{6,4},{7,5},{8,10},{9,11},{10,... | collective-permute-start | bytes 393224 | tf_op jit(solution)/shard_map/ppermute | solution.py:36
  320.5 3.8 %copy-start.10 = (bf16[16,2048]{1,0:T(8,128)(2,1)S(1)}, bf16[16,2048]{1,0:T(8,128)(2,1)}, u32[]{:S(2)}) copy-start(bf16[16,2048]{1,0:T(8,128)(2,1)} %copy-done.9) | copy-start | bytes 196612

commit v3 on v2

--- a/solution.py
+++ b/solution.py
@@ -122,17 +122,24 @@
     vocab_dev = embed_table.shape[0]
     rows = slot_count * token_count
 
-    all_ids = spread(token_ids, "req")
+    half = token_count // 2
+    all_ids = lax.dynamic_slice_in_dim(spread(token_ids, "req"), section_index * half, half, 2)
     first_row = lax.axis_index(("req", "head")) * vocab_dev
     onehot = (
         all_ids.reshape(-1)[:, None] == first_row + jnp.arange(vocab_dev, dtype=jnp.int32)[None, :]
     ).astype(jnp.bfloat16)
     looked_up = jnp.dot(onehot, embed_table, preferred_element_type=jnp.float32).astype(jnp.bfloat16)
     arrived_rows = lax.all_to_all(
-        looked_up.reshape(groups, rows, width), "req", 0, 0, tiled=True
+        looked_up.reshape(groups, slot_count * half, width), "req", 0, 0, tiled=True
     )
     partial_rows = jnp.sum(arrived_rows.astype(jnp.float32), axis=0).astype(jnp.bfloat16)
-    embedded = jnp.sum(spread(partial_rows, "head").astype(jnp.float32), axis=0).astype(jnp.bfloat16)
+    own_half = (
+        jnp.sum(spread(partial_rows, "head").astype(jnp.float32), axis=0)
+        .astype(jnp.bfloat16)
+        .reshape(slot_count, half, width)
+    )
+    other_half = lax.ppermute(own_half, "section", [(0, 1), (1, 0)])
+    embedded = jnp.concatenate([own_half, other_half], axis=1).reshape(rows, width)
 
     ordered_states = jnp.take(state_arrived[0], request_order, axis=0)
     start_state = lax.all_to_all(ordered_states, "req", 0, 1, tiled=True)

time: 330 us -> 350 us (1.061)
  waiting for transfers between devices: 74.1 us -> 99 us
    all_to_all x1, waiting for transfers between devices: 10.8 us -> 27.1 us  [shards(): lax.all_to_all(looked_up.reshape(groups, slot_count * half, width), 'req'...]
    unnamed x75 -> x73, local copies, waits for them, and re-layouts: 22.8 us -> 22.3 us
  transfers between devices with their start and end apart: 12 -> 13, of which waited for: 11 -> 11; matrix products, arithmetic and copies ran while one was open for 31% -> 29% of each run, Pallas kernels for 4% -> 4%
where the time goes in v3:
time: 350 us; the launch traced here: 345 us
  waiting for transfers between devices  99 us (28%)
  local copies, waits for them, and re-layouts  91.2 us (26%)
  starting transfers between devices  47.5 us (14%)
  other arithmetic  35.6 us (10%)
  matrix products  29.7 us (8%)
  blocking collectives  28 us (8%)
  Pallas kernels  12.9 us (4%)
    all_to_all x3, waiting for transfers between devices, spread(): return lax.all_to_all(copies, axis, 0, 0, tiled=True)  31.2 us
    all_to_all x1, blocking collectives, spread(): return lax.all_to_all(copies, axis, 0, 0, tiled=True)  28 us
    all_to_all x1, waiting for transfers between devices, shards(): lax.all_to_all(looked_up.reshape(groups, slot_count * half, width), 'req'...  27.1 us
    unnamed x73, local copies, waits for them, and re-layouts  22.3 us
    all_to_all x3, starting transfers between devices, spread(): return lax.all_to_all(copies, axis, 0, 0, tiled=True)  21.7 us
    ppermute x4, waiting for transfers between devices, head_sum(): value = value + lax.ppermute(value, 'head', pairs)  16.6 us
    all_to_all x2, waiting for transfers between devices, layer(): gathered = lax.all_to_all(packed, 'req', 0, 0, tiled=True)  14.9 us
    pallas_call x2, Pallas kernels, delta_rule(): pl.pallas_call(delta_rule_kernel, out_shape=(jax.ShapeDtypeStruct((slots,...  12.9 us
  transfers between devices with their start and end apart: 13, of which 11 were waited for; matrix products, arithmetic and copies ran while one was open for 29% of the time, Pallas kernels for 4%

profile of v3, /device:TPU:2, one launch (start us, length us, event | category | flops | bytes accessed | tf_op | source)
XLA Modules:
  0.0 345.3 jit_solution(6355695992636133986)
XLA Ops:
  0.6 1.5 broadcast_in_dim.135
  2.1 11.5 %all-to-all-start = ((s32[32,4,4]{2,1,0:T(4,128)}), s32[32,4,4]{2,1,0:T(4,128)S(1)}, u32[]{:S(2)}, u32[]{:S(2)}) async-start(s32[32,4,4]{2,1,0:T(4,128)} %broadcast_in_dim.135), calls=%async_computation | async-start | bytes 131072 | tf_op jit(solution)/shard_map/all_to_all | solution.py:28
  13.6 9.9 %all-to-all-done = s32[32,4,4]{2,1,0:T(4,128)S(1)} async-done(((s32[32,4,4]{2,1,0:T(4,128)}), s32[32,4,4]{2,1,0:T(4,128)S(1)}, u32[]{:S(2)}, u32[]{:S(2)}) %all-to-all-start) | async-done | bytes 2080 | tf_op jit(solution)/shard_map/all_to_all | solution.py:28
  23.9 2.7 fusion.1
  26.6 4.1 %all-to-all-start.1 = ((bf16[32,8,2048]{2,1,0:T(8,128)(2,1)}), bf16[32,8,2048]{2,1,0:T(8,128)(2,1)S(1)}, u32[]{:S(2)}, u32[]{:S(2)}) async-start(bf16[32,8,2048]{2,1,0:T(8,128)(2,1)} %fusion.1), calls=%async_computation.1 | async-start | bytes 2097152 | tf_op jit(solution)/shard_map/all_to_all | solution.py:132
  30.7 27.1 %all-to-all-done.1 = bf16[32,8,2048]{2,1,0:T(8,128)(2,1)S(1)} async-done(((bf16[32,8,2048]{2,1,0:T(8,128)(2,1)}), bf16[32,8,2048]{2,1,0:T(8,128)(2,1)S(1)}, u32[]{:S(2)}, u32[]{:S(2)}) %all-to-all-start.1) | async-done | bytes 1048608 | tf_op jit(solution)/shard_map/all_to_all | solution.py:132
  58.7 4.8 %all-to-all-start.2 = ((bf16[4,8,2048]{2,1,0:T(8,128)(2,1)}), bf16[4,8,2048]{2,1,0:T(8,128)(2,1)S(1)}, u32[]{:S(2)}, u32[]{:S(2)}) async-start(bf16[4,8,2048]{2,1,0:T(8,128)(2,1)} %broadcast_in_dim.136), calls=%async_computation.2 | async-start | bytes 262144 | tf_op jit(solution)/shard_map/all_to_all | solution.py:28
  63.5 4.5 %all-to-all-done.2 = bf16[4,8,2048]{2,1,0:T(8,128)(2,1)S(1)} async-done(((bf16[4,8,2048]{2,1,0:T(8,128)(2,1)}), bf16[4,8,2048]{2,1,0:T(8,128)(2,1)S(1)}, u32[]{:S(2)}, u32[]{:S(2)}) %all-to-all-start.2) | async-done | bytes 131104 | tf_op jit(solution)/shard_map/all_to_all | solution.py:28
  69.5 2.4 gather_fusion
  71.9 11.2 %copy.338 = bf16[1,128,16,2,512]{1,4,3,2,0:T(8,128)(2,1)} copy(bf16[1,128,16,2,512]{4,3,2,1,0:T(2,128)(2,1)} %param.19) | data formatting | bytes 8388608 | tf_op args[4]
  83.0 8.0 %copy.339 = bf16[128,16,2,4,128]{4,1,3,0,2:T(8,128)(2,1)} copy(bf16[128,16,2,4,128]{0,4,3,2,1:T(8,128)(2,1)} %bitcast.193) | data formatting | bytes 8388608 | tf_op jit(solution)/shard_map/reshape;squeeze | solution.py:149
  91.0 5.3 %gather_fusion.1 = bf16[128,2,4,16,128]{4,3,2,1,0:T(8,128)(2,1)} fusion(bf16[2,128,4,16,128]{4,3,2,1,0:T(8,128)(2,1)} %bitcast.192, s32[1024]{0:T(1024)S(1)} %pad_clamp_fusion), kind=kCustom, calls=%fused_computation.1 | custom fusion | bytes 8389120 | tf_op jit(solution)/shard_map/jit(_take)/gather | solution.py:151
  96.3 8.8 %copy.329 = bf16[1,2048,3,512]{1,3,2,0:T(8,128)(2,1)} copy(bf16[1,2048,3,512]{3,1,2,0:T(8,128)(2,1)} %param.23) | data formatting | bytes 12582912 | tf_op args[8]
  106.1 4.5 %convolution_convert_fusion.2 = bf16[16,1536]{1,0:T(8,128)(2,1)S(1)} fusion(bf16[16,2048]{1,0:T(8,128)(2,1)S(1)} %convert_element_type.125, bf16[2048,1536]{0,1:T(8,128)(2,1)} %bitcast.190), kind=kOutput, calls=%fused_computation.8 | convolution fusion | flops 100687872 | bytes 6406144 | tf_op jit(solution)/shard_map/dot_general | solution.py:179
  113.5 5.4 %all-to-all-start.4 = ((bf16[32,4,4,4,128]{4,2,3,1,0:T(4,128)(2,1)}), bf16[32,4,4,4,128]{4,2,3,1,0:T(4,128)(2,1)}, u32[]{:S(2)}, u32[]{:S(2)}) async-start(bf16[32,4,4,4,128]{4,2,3,1,0:T(4,128)(2,1)} %broadcast_in_dim.146), calls=%async_computation.4 | async-start | bytes 1048576 | tf_op jit(solution)/shard_map/all_to_all | solution.py:28
  120.6 16.7 %all-to-all-done.4 = bf16[32,4,4,4,128]{4,2,3,1,0:T(4,128)(2,1)} async-done(((bf16[32,4,4,4,128]{4,2,3,1,0:T(4,128)(2,1)}), bf16[32,4,4,4,128]{4,2,3,1,0:T(4,128)(2,1)}, u32[]{:S(2)}, u32[]{:S(2)}) %all-to-all-start.4) | async-done | bytes 524320 | tf_op jit(solution)/shard_map/all_to_all | solution.py:28
  137.3 4.9 %all-to-all-start.3 = ((f32[128,4,4,128]{3,2,1,0:T(4,128)}), f32[128,4,4,128]{3,2,1,0:T(4,128)S(1)}, u32[]{:S(2)}, u32[]{:S(2)}) async-start(f32[128,4,4,128]{3,2,1,0:T(4,128)} %broadcast_select_fusion), calls=%async_computation.3 | async-start | bytes 2097152 | tf_op jit(solution)/shard_map/all_to_all | solution.py:145
  142.1 2.6 fusion
  144.8 3.7 %select_reduce_fusion.1 = (f32[128,4,4]{1,2,0:T(4,128)S(1)}, f32[128,4,4,16]{3,1,2,0:T(4,128)}) fusion(pred[128,4,16]{2,1,0:T(4,128)(4,1)S(1)} %broadcast_compare_fusion, f32[4]{0:T(128)S(1)} %bitcast.234, bf16[128,4,4,128]{3,1,2,0:T(4,128)(2,1)} %bitcast.21, bf16[2,128,4,16,128]{4,3,2,1,0:T(8,128)(2,1)S(1)} %fusion), kind=kOutput, calls=%fused_computation.57 | convolution fusion | flops 8484864 | bytes 2826752 | tf_op jit(solution)/shard_map/rthd,rhwd->rthw/dot_general | solution.py:201
  148.5 1.6 copy.343
  150.0 3.1 fusion.34
  153.1 2.5 copy.342
  156.9 2.7 fusion.7
  159.6 1.4 pad_maximum_fusion
  161.0 8.4 %all-to-all-done.3 = f32[128,4,4,128]{3,2,1,0:T(4,128)S(1)} async-done(((f32[128,4,4,128]{3,2,1,0:T(4,128)}), f32[128,4,4,128]{3,2,1,0:T(4,128)S(1)}, u32[]{:S(2)}, u32[]{:S(2)}) %all-to-all-start.3) | async-done | bytes 1048608 | tf_op jit(solution)/shard_map/all_to_all | solution.py:145
  170.3 5.6 %all-to-all-start.5 = ((f32[32,4,4,5,128]{4,2,1,3,0:T(4,128)}), f32[32,4,4,5,128]{4,2,1,3,0:T(4,128)S(1)}, u32[]{:S(2)}, u32[]{:S(2)}) async-start(f32[32,4,4,5,128]{4,2,1,3,0:T(4,128)} %pad_maximum_fusion), calls=%async_computation.5 | async-start | bytes 2621440 | tf_op jit(solution)/shard_map/all_to_all | solution.py:229
  176.6 1.6 slice_reduce_fusion.1
  178.2 2.3 copy.419
  180.5 2.6 reshape.372.state_ref
  183.1 1.6 fusion.31
  187.3 1.4 reshape_squeeze.27
  189.6 1.5 fusion.110
  191.7 2.2 copy.332
  193.8 2.1 copy.331
  195.9 6.4 %shard_map.158 = (f32[4,128,512]{2,1,0:T(8,128)}, f32[4,4,512]{2,1,0:T(4,128)}) custom-call(f32[64]{0:T(128)} %reshape_reshape.6.beta_ref, f32[4,128,512]{2,1,0:T(8,128)} %reshape.372.state_ref, f32[4,4,128,4]{3,2,1,0:T(8,128)} %bitcast.198, f32[4,4,128,4]{3,2,1,0:T(8,128)} %bitcast.196, f32[4,4,512]{2,1,0:T(4,128)} %get-tuple-element.33.value_ref), custom_call_target="tpu_custom_call" | custom-call | flops 8388608 | bytes 2097152 | tf_op jit(solution)/shard_map/pallas_call | solution.py:71
  202.4 1.4 reshape.374
  205.2 1.4 copy.333
  207.6 1.5 fusion.74
  211.2 1.4 copy.346
  213.9 1.4 copy.349
  215.3 2.2 fusion.49
  217.6 1.4 copy.353
  218.9 2.5 copy.350
  222.2 1.6 fusion.33
  225.3 1.5 collective-permute-start.1
  226.8 3.5 %collective-permute-done.1 = f32[16,2048]{1,0:T(8,128)S(1)} collective-permute-done((f32[16,2048]{1,0:T(8,128)S(1)}, f32[16,2048]{1,0:T(8,128)S(1)}, u32[]{:S(2)}, u32[]{:S(2)}) %collective-permute-start.1) | collective-permute-done | bytes 131104 | tf_op jit(solution)/shard_map/ppermute | solution.py:36
  230.3 1.5 collective-permute-start.2
  232.0 4.9 %collective-permute-done.2 = f32[16,2048]{1,0:T(8,128)S(1)} collective-permute-done((f32[16,2048]{1,0:T(8,128)S(1)}, f32[16,2048]{1,0:T(8,128)S(1)}, u32[]{:S(2)}, u32[]{:S(2)}) %collective-permute-start.2) | collective-permute-done | bytes 131104 | tf_op jit(solution)/shard_map/ppermute | solution.py:36
  239.8 4.5 %convolution_convert_fusion.1 = bf16[16,1536]{1,0:T(8,128)(2,1)S(1)} fusion(bf16[2048,1536]{0,1:T(8,128)(2,1)} %bitcast.191, bf16[16,2048]{1,0:T(8,128)(2,1)S(1)} %collective-permute-done.3, f32[2048]{0:T(1024)S(1)} %bitcast.216, f32[16]{0:T(128)S(1)} %add_rsqrt_fusion.7), kind=kOutput, calls=%fused_computation.7 | convolution fusion | flops 100818944 | bytes 6414400 | tf_op jit(solution)/shard_map/dot_general | solution.py:179
  247.0 28.0 %all_to_all.50 = bf16[32,4,4,4,128]{4,2,3,1,0:T(4,128)(2,1)S(1)} all-to-all(bf16[32,4,4,4,128]{4,2,3,1,0:T(4,128)(2,1)S(1)} %broadcast_in_dim.150), channel_id=1, replica_groups=mesh['section'=2,'req'=32,'head'=4] {'req'}, dimensions={0} | all-to-all | bytes 1048576 | tf_op jit(solution)/shard_map/all_to_all | solution.py:28
  275.0 3.1 select_reduce_fusion
  278.1 1.9 fusion.6
  283.4 2.6 pad_maximum_fusion.1
  286.0 4.8 %all-to-all-start.7 = ((f32[32,4,4,5,128]{4,2,1,3,0:T(4,128)}), f32[32,4,4,5,128]{4,2,1,3,0:T(4,128)S(1)}, u32[]{:S(2)}, u32[]{:S(2)}) async-start(f32[32,4,4,5,128]{4,2,1,3,0:T(4,128)} %pad_maximum_fusion.1), calls=%async_computation.7 | async-start | bytes 2621440 | tf_op jit(solution)/shard_map/all_to_all | solution.py:229
  294.0 1.4 copy.358
  295.4 2.1 copy.357
  297.5 6.4 %shard_map.159 = (f32[4,128,512]{2,1,0:T(8,128)}, f32[4,4,512]{2,1,0:T(4,128)}) custom-call(f32[64]{0:T(128)} %reshape_reshape.7.beta_ref, f32[4,128,512]{2,1,0:T(8,128)} %reshape.372.state_ref, f32[4,4,128,4]{3,2,1,0:T(8,128)} %bitcast.197, f32[4,4,128,4]{3,2,1,0:T(8,128)} %bitcast.195, f32[4,4,512]{2,1,0:T(4,128)} %get-tuple-element.30.value_ref), custom_call_target="tpu_custom_call" | custom-call | flops 8388608 | bytes 2097152 | tf_op jit(solution)/shard_map/pallas_call | solution.py:71
  308.7 14.9 %all-to-all-done.7 = f32[32,4,4,5,128]{4,2,1,3,0:T(4,128)S(1)} async-done(((f32[32,4,4,5,128]{4,2,1,3,0:T(4,128)}), f32[32,4,4,5,128]{4,2,1,3,0:T(4,128)S(1)}, u32[]{:S(2)}, u32[]{:S(2)}) %all-to-all-start.7) | async-done | bytes 1310752 | tf_op jit(solution)/shard_map/all_to_all | solution.py:229
  325.1 2.5 copy.373
  327.7 1.6 fusion.32
  330.7 1.8 collective-permute-start.4
  332.5 4.5 %collective-permute-done.4 = f32[16,2048]{1,0:T(8,128)S(1)} collective-permute-done((f32[16,2048]{1,0:T(8,128)S(1)}, f32[16,2048]{1,0:T(8,128)S(1)}, u32[]{:S(2)}, u32[]{:S(2)}) %collective-permute-start.4) | collective-permute-done | bytes 131104 | tf_op jit(solution)/shard_map/ppermute | solution.py:36
  337.3 1.5 broadcast_select_fusion.1
  340.0 3.7 %collective-permute-done.5 = f32[16,2048]{1,0:T(8,128)} collective-permute-done((f32[16,2048]{1,0:T(8,128)S(1)}, f32[16,2048]{1,0:T(8,128)}, u32[]{:S(2)}, u32[]{:S(2)}) %collective-permute-start.5) | collective-permute-done | bytes 131104 | tf_op jit(solution)/shard_map/ppermute | solution.py:36
  (179 shorter events, 45.9 us)
Async XLA Ops:
  0.6 224.3 %copy-start = (bf16[1,512,2048]{2,1,0:T(8,128)(2,1)S(1)}, bf16[1,512,2048]{2,1,0:T(8,128)(2,1)}, u32[]{:S(2)}) copy-start(bf16[1,512,2048]{2,1,0:T(8,128)(2,1)} %param.24) | copy-start | bytes 6291460
  2.1 21.5 %all-to-all-start = ((s32[32,4,4]{2,1,0:T(4,128)}), s32[32,4,4]{2,1,0:T(4,128)S(1)}, u32[]{:S(2)}, u32[]{:S(2)}) async-start(s32[32,4,4]{2,1,0:T(4,128)} %broadcast_in_dim.135), calls=%async_computation | async-start | bytes 131072 | tf_op jit(solution)/shard_map/all_to_all | solution.py:28
  23.8 6.8 %copy-start.29 = (s32[128]{0:T(128)S(1)}, s32[128]{0:T(128)}, u32[]{:S(2)}) copy-start(s32[128]{0:T(128)} %param.16) | copy-start | bytes 1540
  23.8 6.8 %copy-start.24 = (f32[1,4,3,512]{3,1,2,0:T(4,128)S(1)}, f32[1,4,3,512]{3,1,2,0:T(4,128)}, u32[]{:S(2)}) copy-start(f32[1,4,3,512]{3,1,2,0:T(4,128)} %param.26) | copy-start | bytes 73732
  26.5 41.6 %copy-start.19 = (bf16[1,4,3,3,512]{4,1,3,2,0:T(4,128)(2,1)S(1)}, bf16[1,4,3,3,512]{4,1,3,2,0:T(4,128)(2,1)}, u32[]{:S(2)}) copy-start(bf16[1,4,3,3,512]{4,1,3,2,0:T(4,128)(2,1)} %param.21) | copy-start | bytes 110596
  26.5 41.7 %copy-start.1 = (s32[128]{0:T(128)S(1)}, s32[128]{0:T(128)}, u32[]{:S(2)}) copy-start(s32[128]{0:T(128)} %param.17) | copy-start | bytes 1540
  26.6 31.3 %all-to-all-start.1 = ((bf16[32,8,2048]{2,1,0:T(8,128)(2,1)}), bf16[32,8,2048]{2,1,0:T(8,128)(2,1)S(1)}, u32[]{:S(2)}, u32[]{:S(2)}) async-start(bf16[32,8,2048]{2,1,0:T(8,128)(2,1)} %fusion.1), calls=%async_computation.1 | async-start | bytes 2097152 | tf_op jit(solution)/shard_map/all_to_all | solution.py:132
  30.7 80.1 %copy-start.13 = (f32[3,512]{1,0:T(4,128)}, f32[3,512]{1,0:T(4,128)S(1)}, u32[]{:S(2)}) copy-start(f32[3,512]{1,0:T(4,128)S(1)} %get-tuple-element.48) | copy-start | bytes 18436
  30.7 80.1 %copy-start.15 = (f32[3,512]{1,0:T(4,128)}, f32[3,512]{1,0:T(4,128)S(1)}, u32[]{:S(2)}) copy-start(f32[3,512]{1,0:T(4,128)S(1)} %get-tuple-element.49) | copy-start | bytes 18436
  58.7 9.3 %all-to-all-start.2 = ((bf16[4,8,2048]{2,1,0:T(8,128)(2,1)}), bf16[4,8,2048]{2,1,0:T(8,128)(2,1)S(1)}, u32[]{:S(2)}, u32[]{:S(2)}) async-start(bf16[4,8,2048]{2,1,0:T(8,128)(2,1)} %broadcast_in_dim.136), calls=%async_computation.2 | async-start | bytes 262144 | tf_op jit(solution)/shard_map/all_to_all | solution.py:28
  68.1 37.7 %collective-permute-start = (bf16[4,2,2048]{2,1,0:T(2,128)(2,1)S(1)}, bf16[4,2,2048]{2,1,0:T(2,128)(2,1)S(1)}, u32[]{:S(2)}, u32[]{:S(2)}) collective-permute-start(bf16[4,2,2048]{2,1,0:T(2,128)(2,1)S(1)} %reshape.371), channel_id=1, source_target_pairs={{0,128},{128,0},{1,129},{129,1},{2,130},{130,2},{3,131},{131,3},{4... | collective-permute-start | bytes 98312 | tf_op jit(solution)/shard_map/ppermute | solution.py:141
  68.2 42.5 %copy-start.7 = (bf16[1,4,3,3,512]{4,2,1,3,0:T(4,128)(2,1)}, bf16[1,4,3,3,512]{4,2,1,3,0:T(4,128)(2,1)S(1)}, u32[]{:S(2)}) copy-start(bf16[1,4,3,3,512]{4,2,1,3,0:T(4,128)(2,1)S(1)} %copy.420) | copy-start | bytes 110596
  96.3 9.6 %copy-start.20 = (f32[1,2048]{1,0:T(1,128)S(1)}, f32[1,2048]{1,0:T(1,128)}, u32[]{:S(2)}) copy-start(f32[1,2048]{1,0:T(1,128)} %param.27) | copy-start | bytes 24580
  106.1 4.5 %copy-start.9 = (bf16[16,2048]{1,0:T(8,128)(2,1)}, bf16[16,2048]{1,0:T(8,128)(2,1)S(1)}, u32[]{:S(2)}) copy-start(bf16[16,2048]{1,0:T(8,128)(2,1)S(1)} %convert_element_type.125) | copy-start | bytes 196612
  110.6 8.3 %copy-start.30 = (s32[128]{0:T(128)S(1)}, s32[128]{0:T(128)}, u32[]{:S(2)}) copy-start(s32[128]{0:T(128)} %param.16) | copy-start | bytes 1540
  111.0 9.6 %copy-start.5 = (f32[4,4,3,512]{3,1,0,2:T(4,128)}, f32[4,4,3,512]{3,1,0,2:T(4,128)S(1)}, u32[]{:S(2)}) copy-start(f32[4,4,3,512]{3,1,0,2:T(4,128)S(1)} %divide_multiply_fusion.1) | copy-start | bytes 294916
  112.5 6.5 %copy-start.18 = (bf16[4,4,4,128]{3,2,1,0:T(4,128)(2,1)}, bf16[4,4,4,128]{3,2,1,0:T(4,128)(2,1)S(1)}, u32[]{:S(2)}) copy-start(bf16[4,4,4,128]{3,2,1,0:T(4,128)(2,1)S(1)} %get-tuple-element.28) | copy-start | bytes 49156
  113.5 23.7 %all-to-all-start.4 = ((bf16[32,4,4,4,128]{4,2,3,1,0:T(4,128)(2,1)}), bf16[32,4,4,4,128]{4,2,3,1,0:T(4,128)(2,1)}, u32[]{:S(2)}, u32[]{:S(2)}) async-start(bf16[32,4,4,4,128]{4,2,3,1,0:T(4,128)(2,1)} %broadcast_in_dim.146), calls=%async_computation.4 | async-start | bytes 1048576 | tf_op jit(solution)/shard_map/all_to_all | solution.py:28
  137.3 32.1 %all-to-all-start.3 = ((f32[128,4,4,128]{3,2,1,0:T(4,128)}), f32[128,4,4,128]{3,2,1,0:T(4,128)S(1)}, u32[]{:S(2)}, u32[]{:S(2)}) async-start(f32[128,4,4,128]{3,2,1,0:T(4,128)} %broadcast_select_fusion), calls=%async_computation.3 | async-start | bytes 2097152 | tf_op jit(solution)/shard_map/all_to_all | solution.py:145
  142.1 2.6 copy-start.32
  144.8 3.7 %copy-start.2 = (bf16[2,128,4,16,128]{4,3,2,1,0:T(8,128)(2,1)}, bf16[2,128,4,16,128]{4,3,2,1,0:T(8,128)(2,1)S(1)}, u32[]{:S(2)}) copy-start(bf16[2,128,4,16,128]{4,3,2,1,0:T(8,128)(2,1)S(1)} %fusion) | copy-start | bytes 12582916
  169.4 1.0 copy-start.4
  170.3 40.1 %all-to-all-start.5 = ((f32[32,4,4,5,128]{4,2,1,3,0:T(4,128)}), f32[32,4,4,5,128]{4,2,1,3,0:T(4,128)S(1)}, u32[]{:S(2)}, u32[]{:S(2)}) async-start(f32[32,4,4,5,128]{4,2,1,3,0:T(4,128)} %pad_maximum_fusion), calls=%async_computation.5 | async-start | bytes 2621440 | tf_op jit(solution)/shard_map/all_to_all | solution.py:229
  207.6 1.5 copy-start.17
  207.6 1.5 copy-start.23
  223.9 16.0 %copy-start.21 = (f32[1,2048]{1,0:T(1,128)S(1)}, f32[1,2048]{1,0:T(1,128)}, u32[]{:S(2)}) copy-start(f32[1,2048]{1,0:T(1,128)} %param.27) | copy-start | bytes 24580
  225.3 5.0 %collective-permute-start.1 = (f32[16,2048]{1,0:T(8,128)S(1)}, f32[16,2048]{1,0:T(8,128)S(1)}, u32[]{:S(2)}, u32[]{:S(2)}) collective-permute-start(f32[16,2048]{1,0:T(8,128)S(1)} %fusion.4), channel_id=1, source_target_pairs={{0,1},{1,0},{2,3},{3,2},{4,5},{5,4},{6,7},{7,6},{8,9},{9,8},{10,11... | collective-permute-start | bytes 393224 | tf_op jit(solution)/shard_map/ppermute | solution.py:36
  230.3 6.6 %collective-permute-start.2 = (f32[16,2048]{1,0:T(8,128)S(1)}, f32[16,2048]{1,0:T(8,128)S(1)}, u32[]{:S(2)}, u32[]{:S(2)}) collective-permute-start(f32[16,2048]{1,0:T(8,128)S(1)} %add.211), channel_id=1, source_target_pairs={{0,2},{1,3},{2,0},{3,1},{4,6},{5,7},{6,4},{7,5},{8,10},{9,11},{10,... | collective-permute-start | bytes 393224 | tf_op jit(solution)/shard_map/ppermute | solution.py:36
  236.9 7.5 %copy-start.10 = (bf16[16,2048]{1,0:T(8,128)(2,1)}, bf16[16,2048]{1,0:T(8,128)(2,1)S(1)}, u32[]{:S(2)}) copy-start(bf16[16,2048]{1,0:T(8,128)(2,1)S(1)} %add_convert_fusion) | copy-start | bytes 196612
  236.9 2.2 collective-permute-start.3
  239.2 0.6 copy-start.27
  239.8 4.6 %copy-start.8 = (bf16[1,4,3,3,512]{4,2,1,3,0:T(4,128)(2,1)S(1)}, bf16[1,4,3,3,512]{4,2,1,3,0:T(4,128)(2,1)}, u32[]{:S(2)}) copy-start(bf16[1,4,3,3,512]{4,2,1,3,0:T(4,128)(2,1)} %copy-done.7) | copy-start | bytes 110596
  239.8 4.7 %copy-start.14 = (f32[3,512]{1,0:T(4,128)S(1)}, f32[3,512]{1,0:T(4,128)}, u32[]{:S(2)}) copy-start(f32[3,512]{1,0:T(4,128)} %copy-done.13) | copy-start | bytes 18436
  239.8 4.7 %copy-start.16 = (f32[3,512]{1,0:T(4,128)S(1)}, f32[3,512]{1,0:T(4,128)}, u32[]{:S(2)}) copy-start(f32[3,512]{1,0:T(4,128)} %copy-done.15) | copy-start | bytes 18436
  244.4 30.6 %copy-start.33 = (f32[1,4]{1,0:T(1,128)S(1)}, f32[1,4]{1,0:T(1,128)}, u32[]{:S(2)}) copy-start(f32[1,4]{1,0:T(1,128)} %param.29) | copy-start | bytes 52
  244.7 0.6 copy-start.6
  275.0 3.1 copy-start.3
  280.0 3.1 copy-start.26
  283.3 7.5 %copy-start.22 = (f32[1,2048]{1,0:T(1,128)S(1)}, f32[1,2048]{1,0:T(1,128)}, u32[]{:S(2)}) copy-start(f32[1,2048]{1,0:T(1,128)} %param.27) | copy-start | bytes 24580
  283.3 7.5 %copy-start.28 = (f32[16]{0:T(128)S(1)}, f32[16]{0:T(128)}, u32[]{:S(2)}) copy-start(f32[16]{0:T(128)} %copy-done.27) | copy-start | bytes 196
  283.3 7.5 %copy-start.31 = (bf16[1,2048,4]{1,2,0:T(4,128)(2,1)S(1)}, bf16[1,2048,4]{1,2,0:T(4,128)(2,1)}, u32[]{:S(2)}) copy-start(bf16[1,2048,4]{1,2,0:T(4,128)(2,1)} %param.25) | copy-start | bytes 49156
  286.0 8.0 %copy-start.12 = (f32[4,4,4,128]{3,2,1,0:T(4,128)S(1)}, f32[4,4,4,128]{3,2,1,0:T(4,128)}, u32[]{:S(2)}) copy-start(f32[4,4,4,128]{3,2,1,0:T(4,128)} %get-tuple-element.19) | copy-start | bytes 98308
  286.0 37.7 %all-to-all-start.7 = ((f32[32,4,4,5,128]{4,2,1,3,0:T(4,128)}), f32[32,4,4,5,128]{4,2,1,3,0:T(4,128)S(1)}, u32[]{:S(2)}, u32[]{:S(2)}) async-start(f32[32,4,4,5,128]{4,2,1,3,0:T(4,128)} %pad_maximum_fusion.1), calls=%async_computation.7 | async-start | bytes 2621440 | tf_op jit(solution)/shard_map/all_to_all | solution.py:229
  306.5 22.8 %copy-start.25 = (f32[4,4,4]{1,2,0:T(4,128)S(1)}, f32[4,4,4]{1,2,0:T(4,128)}, u32[]{:S(2)}) copy-start(f32[4,4,4]{1,2,0:T(4,128)} %copy.359) | copy-start | bytes 772
  330.7 6.3 %collective-permute-start.4 = (f32[16,2048]{1,0:T(8,128)S(1)}, f32[16,2048]{1,0:T(8,128)S(1)}, u32[]{:S(2)}, u32[]{:S(2)}) collective-permute-start(f32[16,2048]{1,0:T(8,128)S(1)} %fusion.2), channel_id=1, source_target_pairs={{0,1},{1,0},{2,3},{3,2},{4,5},{5,4},{6,7},{7,6},{8,9},{9,8},{10,11... | collective-permute-start | bytes 393224 | tf_op jit(solution)/shard_map/ppermute | solution.py:36
  337.1 6.7 %collective-permute-start.5 = (f32[16,2048]{1,0:T(8,128)S(1)}, f32[16,2048]{1,0:T(8,128)}, u32[]{:S(2)}, u32[]{:S(2)}) collective-permute-start(f32[16,2048]{1,0:T(8,128)S(1)} %add.226), channel_id=1, source_target_pairs={{0,2},{1,3},{2,0},{3,1},{4,6},{5,7},{6,4},{7,5},{8,10},{9,11},{10,... | collective-permute-start | bytes 393224 | tf_op jit(solution)/shard_map/ppermute | solution.py:36
  337.3 6.5 %copy-start.11 = (bf16[16,2048]{1,0:T(8,128)(2,1)S(1)}, bf16[16,2048]{1,0:T(8,128)(2,1)}, u32[]{:S(2)}) copy-start(bf16[16,2048]{1,0:T(8,128)(2,1)} %copy-done.10) | copy-start | bytes 196612

commit v4 on v2

--- a/solution.py
+++ b/solution.py
@@ -208,21 +208,30 @@
             cache_values,
             preferred_element_type=jnp.float32,
         )
+        stats_count = 2 * token_count * heads_dev
         stats = jnp.concatenate(
             [
-                local_sum,
-                local_max,
-                jnp.zeros((all_slots, token_count, head_dim - 2 * heads_dev), jnp.float32),
+                jnp.concatenate([local_sum, local_max], axis=-1).reshape(all_slots, stats_count),
+                jnp.zeros((all_slots, head_dim - stats_count), jnp.float32),
             ],
             axis=-1,
         )
-        packed = jnp.concatenate([local_part, stats[:, :, None, :]], axis=2).reshape(
-            groups, slot_count, token_count, heads_dev + 1, head_dim
-        )
+        packed = jnp.concatenate(
+            [
+                local_part.reshape(all_slots, token_count * heads_dev, head_dim),
+                stats[:, None, :],
+            ],
+            axis=1,
+        ).reshape(groups, slot_count, token_count * heads_dev + 1, head_dim)
         gathered = lax.all_to_all(packed, "req", 0, 0, tiled=True)
-        part_numer = gathered[:, :, :, :heads_dev]
-        part_sum = gathered[:, :, :, heads_dev, :heads_dev]
-        part_max = gathered[:, :, :, heads_dev, heads_dev : 2 * heads_dev]
+        part_numer = gathered[:, :, : token_count * heads_dev].reshape(
+            groups, slot_count, token_count, heads_dev, head_dim
+        )
+        part_stats = gathered[:, :, token_count * heads_dev, :stats_count].reshape(
+            groups, slot_count, token_count, 2 * heads_dev
+        )
+        part_sum = part_stats[..., :heads_dev]
+        part_max = part_stats[..., heads_dev:]
 
         delta_state, readout = delta_rule(start_state, key_vec, query_vec, value_vec, beta_gate)
 

time: 330 us -> 321 us (0.973)
  waiting for transfers between devices: 74.1 us -> 101 us
  local copies, waits for them, and re-layouts: 92 us -> 75.2 us
  other arithmetic: 37.7 us -> 23 us
    all_to_all x1, waiting for transfers between devices: 10.8 us -> 40.7 us  [shards(): lax.all_to_all(looked_up.reshape(groups, rows, width), 'req', 0, 0, tiled...]
    all_to_all x1, waiting for transfers between devices: 5.07 us -> 0.01 us  [shards(): start_state = lax.all_to_all(ordered_states, 'req', 0, 1, tiled=True)]
    exp x2 -> x0, local copies, waits for them, and re-layouts: 5.05 us -> none  [layer(): part_scale = jnp.exp(part_max - highest[None])]
    all_to_all x2, waiting for transfers between devices: 15 us -> 19.5 us  [layer(): gathered = lax.all_to_all(packed, 'req', 0, 0, tiled=True)]
    all_to_all x2, starting transfers between devices: 10.3 us -> 14.3 us  [layer(): gathered = lax.all_to_all(packed, 'req', 0, 0, tiled=True)]
    concatenate x4 -> x2, other arithmetic: 5.44 us -> 1.48 us  [layer(): jnp.concatenate([local_part.reshape(all_slots, token_count * heads_dev, h...]
    all_to_all x3, waiting for transfers between devices: 28.5 us -> 25 us  [spread(): return lax.all_to_all(copies, axis, 0, 0, tiled=True)]
    unnamed x75 -> x105, local copies, waits for them, and re-layouts: 22.8 us -> 21.7 us
  transfers between devices with their start and end apart: 12 -> 12, of which waited for: 11 -> 11; matrix products, arithmetic and copies ran while one was open for 31% -> 25% of each run, Pallas kernels for 4% -> 4%
where the time goes in v4:
time: 321 us; the launch traced here: 318 us
  waiting for transfers between devices  101 us (31%)
  local copies, waits for them, and re-layouts  75.2 us (23%)
  starting transfers between devices  52.7 us (16%)
  matrix products  27.5 us (9%)
  blocking collectives  24.3 us (8%)
  other arithmetic  23 us (7%)
  Pallas kernels  12.9 us (4%)
    all_to_all x1, waiting for transfers between devices, shards(): lax.all_to_all(looked_up.reshape(groups, rows, width), 'req', 0, 0, tiled...  40.7 us
    all_to_all x3, waiting for transfers between devices, spread(): return lax.all_to_all(copies, axis, 0, 0, tiled=True)  25 us
    all_to_all x1, blocking collectives, spread(): return lax.all_to_all(copies, axis, 0, 0, tiled=True)  24.3 us
    all_to_all x3, starting transfers between devices, spread(): return lax.all_to_all(copies, axis, 0, 0, tiled=True)  21.7 us
    unnamed x105, local copies, waits for them, and re-layouts  21.7 us
    all_to_all x2, waiting for transfers between devices, layer(): gathered = lax.all_to_all(packed, 'req', 0, 0, tiled=True)  19.5 us
    ppermute x4, waiting for transfers between devices, head_sum(): value = value + lax.ppermute(value, 'head', pairs)  14.9 us
    all_to_all x2, starting transfers between devices, layer(): gathered = lax.all_to_all(packed, 'req', 0, 0, tiled=True)  14.3 us
  transfers between devices with their start and end apart: 12, of which 11 were waited for; matrix products, arithmetic and copies ran while one was open for 25% of the time, Pallas kernels for 4%

profile of v4, /device:TPU:2, one launch (start us, length us, event | category | flops | bytes accessed | tf_op | source)
XLA Modules:
  0.0 318.2 jit_solution(6714601479322576688)
XLA Ops:
  0.6 1.5 broadcast_in_dim.135
  2.1 11.5 %all-to-all-start = ((s32[32,4,4]{2,1,0:T(4,128)}), s32[32,4,4]{2,1,0:T(4,128)S(1)}, u32[]{:S(2)}, u32[]{:S(2)}) async-start(s32[32,4,4]{2,1,0:T(4,128)} %broadcast_in_dim.135), calls=%async_computation | async-start | bytes 131072 | tf_op jit(solution)/shard_map/all_to_all | solution.py:28
  13.6 9.9 %all-to-all-done = s32[32,4,4]{2,1,0:T(4,128)S(1)} async-done(((s32[32,4,4]{2,1,0:T(4,128)}), s32[32,4,4]{2,1,0:T(4,128)S(1)}, u32[]{:S(2)}, u32[]{:S(2)}) %all-to-all-start) | async-done | bytes 2080 | tf_op jit(solution)/shard_map/all_to_all | solution.py:28
  23.7 3.3 %convolution_convert_fusion = bf16[512,2048]{1,0:T(8,128)(2,1)} fusion(bf16[250,2048]{1,0:T(8,128)(2,1)} %param.18, s32[250]{0:T(256)S(1)} %iota_add_fusion, s32[512]{0:T(512)S(1)} %eq.19), kind=kOutput, calls=%fused_computation.5 | convolution fusion | flops 525464576 | bytes 3124200 | tf_op jit(solution)/shard_map/dot_general | solution.py:130
  27.0 4.9 %all-to-all-start.1 = ((bf16[32,16,2048]{2,1,0:T(8,128)(2,1)}), bf16[32,16,2048]{2,1,0:T(8,128)(2,1)}, u32[]{:S(2)}, u32[]{:S(2)}) async-start(bf16[32,16,2048]{2,1,0:T(8,128)(2,1)} %bitcast.177), calls=%async_computation.1 | async-start | bytes 4194304 | tf_op jit(solution)/shard_map/all_to_all | solution.py:131
  32.0 8.9 %copy.355 = bf16[1,2048,3,512]{1,3,2,0:T(8,128)(2,1)} copy(bf16[1,2048,3,512]{3,1,2,0:T(8,128)(2,1)} %param.23) | data formatting | bytes 12582912 | tf_op args[8]
  40.9 40.7 %all-to-all-done.1 = bf16[32,16,2048]{2,1,0:T(8,128)(2,1)} async-done(((bf16[32,16,2048]{2,1,0:T(8,128)(2,1)}), bf16[32,16,2048]{2,1,0:T(8,128)(2,1)}, u32[]{:S(2)}, u32[]{:S(2)}) %all-to-all-start.1) | async-done | bytes 2097184 | tf_op jit(solution)/shard_map/all_to_all | solution.py:131
  81.6 1.9 reduce_sum.172
  84.3 4.8 %all-to-all-start.2 = ((bf16[4,16,2048]{2,1,0:T(8,128)(2,1)}), bf16[4,16,2048]{2,1,0:T(8,128)(2,1)S(1)}, u32[]{:S(2)}, u32[]{:S(2)}) async-start(bf16[4,16,2048]{2,1,0:T(8,128)(2,1)} %broadcast_in_dim.136), calls=%async_computation.2 | async-start | bytes 524288 | tf_op jit(solution)/shard_map/all_to_all | solution.py:28
  89.1 5.2 %all-to-all-done.2 = bf16[4,16,2048]{2,1,0:T(8,128)(2,1)S(1)} async-done(((bf16[4,16,2048]{2,1,0:T(8,128)(2,1)}), bf16[4,16,2048]{2,1,0:T(8,128)(2,1)S(1)}, u32[]{:S(2)}, u32[]{:S(2)}) %all-to-all-start.2) | async-done | bytes 262176 | tf_op jit(solution)/shard_map/all_to_all | solution.py:28
  94.5 4.5 %convolution_convert_fusion.2 = bf16[16,1536]{1,0:T(8,128)(2,1)S(1)} fusion(bf16[2048,1536]{0,1:T(8,128)(2,1)} %bitcast.173, bf16[16,2048]{1,0:T(8,128)(2,1)S(1)} %reduce_sum.173, f32[2048]{0:T(1024)S(1)} %bitcast.205, f32[16]{0:T(128)S(1)} %add_rsqrt_fusion.7), kind=kOutput, calls=%fused_computation.7 | convolution fusion | flops 100818944 | bytes 6414400 | tf_op jit(solution)/shard_map/dot_general | solution.py:172
  100.8 1.0 broadcast_in_dim.146
  101.9 5.4 %all-to-all-start.4 = ((bf16[32,4,4,4,128]{4,2,3,1,0:T(4,128)(2,1)}), bf16[32,4,4,4,128]{4,2,3,1,0:T(4,128)(2,1)}, u32[]{:S(2)}, u32[]{:S(2)}) async-start(bf16[32,4,4,4,128]{4,2,3,1,0:T(4,128)(2,1)} %broadcast_in_dim.146), calls=%async_computation.4 | async-start | bytes 1048576 | tf_op jit(solution)/shard_map/all_to_all | solution.py:28
  107.3 1.2 gather_fusion.2
  108.6 2.4 gather_fusion
  111.1 1.3 broadcast_select_fusion
  112.4 9.9 %all-to-all-done.4 = bf16[32,4,4,4,128]{4,2,3,1,0:T(4,128)(2,1)} async-done(((bf16[32,4,4,4,128]{4,2,3,1,0:T(4,128)(2,1)}), bf16[32,4,4,4,128]{4,2,3,1,0:T(4,128)(2,1)}, u32[]{:S(2)}, u32[]{:S(2)}) %all-to-all-start.4) | async-done | bytes 524320 | tf_op jit(solution)/shard_map/all_to_all | solution.py:28
  122.3 4.2 %all-to-all-start.3 = ((f32[128,4,4,128]{3,2,1,0:T(4,128)}), f32[128,4,4,128]{3,2,1,0:T(4,128)S(1)}, u32[]{:S(2)}, u32[]{:S(2)}) async-start(f32[128,4,4,128]{3,2,1,0:T(4,128)} %broadcast_select_fusion), calls=%async_computation.3 | async-start | bytes 2097152 | tf_op jit(solution)/shard_map/all_to_all | solution.py:138
  126.5 11.2 %copy.364 = bf16[1,128,16,2,512]{1,4,3,2,0:T(8,128)(2,1)} copy(bf16[1,128,16,2,512]{4,3,2,1,0:T(2,128)(2,1)} %param.19) | data formatting | bytes 8388608 | tf_op args[4]
  137.7 7.9 %copy.365 = bf16[128,16,2,4,128]{4,1,3,0,2:T(8,128)(2,1)} copy(bf16[128,16,2,4,128]{0,4,3,2,1:T(8,128)(2,1)} %bitcast.176) | data formatting | bytes 8388608 | tf_op jit(solution)/shard_map/reshape;squeeze | solution.py:142
  145.6 5.3 %gather_fusion.1 = bf16[128,2,4,16,128]{4,3,2,1,0:T(8,128)(2,1)} fusion(bf16[2,128,4,16,128]{4,3,2,1,0:T(8,128)(2,1)} %bitcast.175, s32[1024]{0:T(1024)S(1)} %pad_clamp_fusion), kind=kCustom, calls=%fused_computation.1 | custom fusion | bytes 8389120 | tf_op jit(solution)/shard_map/jit(_take)/gather | solution.py:144
  151.2 2.6 fusion
  153.9 3.7 %select_reduce_fusion.1 = (f32[128,4,4]{1,2,0:T(4,128)S(1)}, f32[128,4,4,16]{3,1,2,0:T(4,128)}) fusion(pred[128,4,16]{2,1,0:T(4,128)(4,1)S(1)} %broadcast_compare_fusion, f32[4]{0:T(128)S(1)} %bitcast.225, bf16[128,4,4,128]{3,1,2,0:T(4,128)(2,1)} %bitcast.21, bf16[2,128,4,16,128]{4,3,2,1,0:T(8,128)(2,1)S(1)} %fusion), kind=kOutput, calls=%fused_computation.58 | convolution fusion | flops 8484864 | bytes 2826752 | tf_op jit(solution)/shard_map/rthd,rhwd->rthw/dot_general | solution.py:194
  158.3 3.1 fusion.35
  161.4 1.7 copy.369
  163.0 2.7 fusion.9
  165.8 1.2 copy.368
  167.1 1.4 pad_maximum_fusion
  168.5 1.3 copy.372
  169.8 1.0 copy-done.4
  170.8 9.6 %all-to-all-start.5 = ((f32[32,4,17,128]{3,1,2,0:T(4,128)}), f32[32,4,17,128]{3,1,2,0:T(4,128)S(1)}, u32[]{:S(2)}, u32[]{:S(2)}) async-start(f32[32,4,17,128]{3,1,2,0:T(4,128)} %copy.372), calls=%async_computation.5 | async-start | bytes 2228224 | tf_op jit(solution)/shard_map/all_to_all | solution.py:226
  181.2 2.4 copy.449
  183.6 2.6 reshape.276.state_ref
  187.5 1.4 copy.358
  188.9 1.4 copy.357
  190.3 6.4 %shard_map.158 = (f32[4,128,512]{2,1,0:T(8,128)}, f32[4,4,512]{2,1,0:T(4,128)}) custom-call(f32[64]{0:T(128)} %reshape_reshape.6.beta_ref, f32[4,128,512]{2,1,0:T(8,128)} %reshape.276.state_ref, f32[4,4,128,4]{3,2,1,0:T(8,128)} %bitcast.182, f32[4,4,128,4]{3,2,1,0:T(8,128)} %bitcast.180, f32[4,4,512]{2,1,0:T(4,128)} %get-tuple-element.33.value_ref), custom_call_target="tpu_custom_call" | custom-call | flops 8388608 | bytes 2097152 | tf_op jit(solution)/shard_map/pallas_call | solution.py:71
  199.4 1.4 fusion.81
  200.8 4.4 %all-to-all-done.5 = f32[32,4,17,128]{3,1,2,0:T(4,128)S(1)} async-done(((f32[32,4,17,128]{3,1,2,0:T(4,128)}), f32[32,4,17,128]{3,1,2,0:T(4,128)S(1)}, u32[]{:S(2)}, u32[]{:S(2)}) %all-to-all-start.5) | async-done | bytes 1114144 | tf_op jit(solution)/shard_map/all_to_all | solution.py:226
  207.0 1.0 copy.378
  209.5 1.1 fusion.25
  211.0 1.5 collective-permute-start
  212.4 3.5 %collective-permute-done = f32[16,2048]{1,0:T(8,128)S(1)} collective-permute-done((f32[16,2048]{1,0:T(8,128)S(1)}, f32[16,2048]{1,0:T(8,128)S(1)}, u32[]{:S(2)}, u32[]{:S(2)}) %collective-permute-start) | collective-permute-done | bytes 131104 | tf_op jit(solution)/shard_map/ppermute | solution.py:36
  215.9 1.6 collective-permute-start.1
  217.6 5.0 %collective-permute-done.1 = f32[16,2048]{1,0:T(8,128)S(1)} collective-permute-done((f32[16,2048]{1,0:T(8,128)S(1)}, f32[16,2048]{1,0:T(8,128)S(1)}, u32[]{:S(2)}, u32[]{:S(2)}) %collective-permute-start.1) | collective-permute-done | bytes 131104 | tf_op jit(solution)/shard_map/ppermute | solution.py:36
  222.5 1.3 collective-permute-start.2
  224.9 4.5 %convolution_convert_fusion.1 = bf16[16,1536]{1,0:T(8,128)(2,1)S(1)} fusion(bf16[2048,1536]{0,1:T(8,128)(2,1)} %bitcast.174, bf16[16,2048]{1,0:T(8,128)(2,1)S(1)} %collective-permute-done.2, f32[16]{0:T(128)S(1)} %add_rsqrt_fusion.6, f32[2048]{0:T(1024)S(1)} %bitcast.207), kind=kOutput, calls=%fused_computation.6 | convolution fusion | flops 100818944 | bytes 6414400 | tf_op jit(solution)/shard_map/dot_general | solution.py:172
  230.9 24.3 %all_to_all.50 = bf16[32,4,4,4,128]{4,2,3,1,0:T(4,128)(2,1)S(1)} all-to-all(bf16[32,4,4,4,128]{4,2,3,1,0:T(4,128)(2,1)S(1)} %broadcast_in_dim.150), channel_id=1, replica_groups=mesh['section'=2,'req'=32,'head'=4] {'req'}, dimensions={0} | all-to-all | bytes 1048576 | tf_op jit(solution)/shard_map/all_to_all | solution.py:28
  255.2 3.1 select_reduce_fusion
  258.3 1.8 fusion.10
  260.2 1.4 fusion.37
  261.8 1.5 copy.393
  263.6 1.3 copy.397
  264.9 4.7 %all-to-all-start.7 = ((f32[32,4,17,128]{3,1,2,0:T(4,128)}), f32[32,4,17,128]{3,1,2,0:T(4,128)S(1)}, u32[]{:S(2)}, u32[]{:S(2)}) async-start(f32[32,4,17,128]{3,1,2,0:T(4,128)} %copy.397), calls=%async_computation.7 | async-start | bytes 2228224 | tf_op jit(solution)/shard_map/all_to_all | solution.py:226
  270.8 1.4 copy.386
  272.2 1.3 copy.385
  273.6 6.4 %shard_map.159 = (f32[4,128,512]{2,1,0:T(8,128)}, f32[4,4,512]{2,1,0:T(4,128)}) custom-call(f32[64]{0:T(128)} %reshape_reshape.7.beta_ref, f32[4,128,512]{2,1,0:T(8,128)} %reshape.276.state_ref, f32[4,4,128,4]{3,2,1,0:T(8,128)} %bitcast.181, f32[4,4,128,4]{3,2,1,0:T(8,128)} %bitcast.179, f32[4,4,512]{2,1,0:T(4,128)} %get-tuple-element.30.value_ref), custom_call_target="tpu_custom_call" | custom-call | flops 8388608 | bytes 2097152 | tf_op jit(solution)/shard_map/pallas_call | solution.py:71
  283.2 15.1 %all-to-all-done.7 = f32[32,4,17,128]{3,1,2,0:T(4,128)S(1)} async-done(((f32[32,4,17,128]{3,1,2,0:T(4,128)}), f32[32,4,17,128]{3,1,2,0:T(4,128)S(1)}, u32[]{:S(2)}, u32[]{:S(2)}) %all-to-all-start.7) | async-done | bytes 1114144 | tf_op jit(solution)/shard_map/all_to_all | solution.py:226
  302.6 1.1 fusion.26
  304.1 1.1 collective-permute-start.3
  305.2 4.7 %collective-permute-done.3 = f32[16,2048]{1,0:T(8,128)S(1)} collective-permute-done((f32[16,2048]{1,0:T(8,128)S(1)}, f32[16,2048]{1,0:T(8,128)S(1)}, u32[]{:S(2)}, u32[]{:S(2)}) %collective-permute-start.3) | collective-permute-done | bytes 131104 | tf_op jit(solution)/shard_map/ppermute | solution.py:36
  309.9 2.1 collective-permute-start.4
  312.0 1.5 broadcast_select_fusion.1
  313.5 1.3 select_n.91
  314.8 1.8 collective-permute-done.4
  (209 shorter events, 26.0 us)
Async XLA Ops:
  0.6 209.9 %copy-start = (bf16[1,512,2048]{2,1,0:T(8,128)(2,1)S(1)}, bf16[1,512,2048]{2,1,0:T(8,128)(2,1)}, u32[]{:S(2)}) copy-start(bf16[1,512,2048]{2,1,0:T(8,128)(2,1)} %param.24) | copy-start | bytes 6291460
  2.1 21.5 %all-to-all-start = ((s32[32,4,4]{2,1,0:T(4,128)}), s32[32,4,4]{2,1,0:T(4,128)S(1)}, u32[]{:S(2)}, u32[]{:S(2)}) async-start(s32[32,4,4]{2,1,0:T(4,128)} %broadcast_in_dim.135), calls=%async_computation | async-start | bytes 131072 | tf_op jit(solution)/shard_map/all_to_all | solution.py:28
  27.0 4.9 %copy-start.23 = (bf16[1,4,3,3,512]{4,1,3,2,0:T(4,128)(2,1)S(1)}, bf16[1,4,3,3,512]{4,1,3,2,0:T(4,128)(2,1)}, u32[]{:S(2)}) copy-start(bf16[1,4,3,3,512]{4,1,3,2,0:T(4,128)(2,1)} %param.21) | copy-start | bytes 110596
  27.0 54.6 %all-to-all-start.1 = ((bf16[32,16,2048]{2,1,0:T(8,128)(2,1)}), bf16[32,16,2048]{2,1,0:T(8,128)(2,1)}, u32[]{:S(2)}, u32[]{:S(2)}) async-start(bf16[32,16,2048]{2,1,0:T(8,128)(2,1)} %bitcast.177), calls=%async_computation.1 | async-start | bytes 4194304 | tf_op jit(solution)/shard_map/all_to_all | solution.py:131
  32.0 67.1 %copy-start.8 = (bf16[1,4,3,3,512]{4,2,1,3,0:T(4,128)(2,1)}, bf16[1,4,3,3,512]{4,2,1,3,0:T(4,128)(2,1)S(1)}, u32[]{:S(2)}) copy-start(bf16[1,4,3,3,512]{4,2,1,3,0:T(4,128)(2,1)S(1)} %copy.450) | copy-start | bytes 110596
  32.0 8.9 %copy-start.32 = (f32[1,4,3,512]{3,1,2,0:T(4,128)S(1)}, f32[1,4,3,512]{3,1,2,0:T(4,128)}, u32[]{:S(2)}) copy-start(f32[1,4,3,512]{3,1,2,0:T(4,128)} %param.26) | copy-start | bytes 73732
  40.9 53.6 %copy-start.24 = (f32[1,2048]{1,0:T(1,128)S(1)}, f32[1,2048]{1,0:T(1,128)}, u32[]{:S(2)}) copy-start(f32[1,2048]{1,0:T(1,128)} %param.27) | copy-start | bytes 24580
  84.3 10.0 %all-to-all-start.2 = ((bf16[4,16,2048]{2,1,0:T(8,128)(2,1)}), bf16[4,16,2048]{2,1,0:T(8,128)(2,1)S(1)}, u32[]{:S(2)}, u32[]{:S(2)}) async-start(bf16[4,16,2048]{2,1,0:T(8,128)(2,1)} %broadcast_in_dim.136), calls=%async_computation.2 | async-start | bytes 524288 | tf_op jit(solution)/shard_map/all_to_all | solution.py:28
  89.1 10.1 %copy-start.15 = (f32[3,512]{1,0:T(4,128)}, f32[3,512]{1,0:T(4,128)S(1)}, u32[]{:S(2)}) copy-start(f32[3,512]{1,0:T(4,128)S(1)} %get-tuple-element.48) | copy-start | bytes 18436
  89.1 10.1 %copy-start.17 = (f32[3,512]{1,0:T(4,128)}, f32[3,512]{1,0:T(4,128)S(1)}, u32[]{:S(2)}) copy-start(f32[3,512]{1,0:T(4,128)S(1)} %get-tuple-element.49) | copy-start | bytes 18436
  94.5 4.5 %copy-start.37 = (f32[16]{0:T(128)}, f32[16]{0:T(128)S(1)}, u32[]{:S(2)}) copy-start(f32[16]{0:T(128)S(1)} %add_rsqrt_fusion.7) | copy-start | bytes 196
  99.0 8.2 %copy-start.41 = (s32[128]{0:T(128)S(1)}, s32[128]{0:T(128)}, u32[]{:S(2)}) copy-start(s32[128]{0:T(128)} %param.16) | copy-start | bytes 1540
  99.0 8.3 %copy-start.1 = (s32[128]{0:T(128)S(1)}, s32[128]{0:T(128)}, u32[]{:S(2)}) copy-start(s32[128]{0:T(128)} %param.17) | copy-start | bytes 1540
  99.4 9.2 %copy-start.7 = (f32[4,4,3,512]{3,1,0,2:T(4,128)}, f32[4,4,3,512]{3,1,0,2:T(4,128)S(1)}, u32[]{:S(2)}) copy-start(f32[4,4,3,512]{3,1,0,2:T(4,128)S(1)} %divide_multiply_fusion.1) | copy-start | bytes 294916
  100.8 10.1 %copy-start.21 = (bf16[4,4,4,128]{3,2,1,0:T(4,128)(2,1)}, bf16[4,4,4,128]{3,2,1,0:T(4,128)(2,1)S(1)}, u32[]{:S(2)}) copy-start(bf16[4,4,4,128]{3,2,1,0:T(4,128)(2,1)S(1)} %get-tuple-element.28) | copy-start | bytes 49156
  101.9 20.4 %all-to-all-start.4 = ((bf16[32,4,4,4,128]{4,2,3,1,0:T(4,128)(2,1)}), bf16[32,4,4,4,128]{4,2,3,1,0:T(4,128)(2,1)}, u32[]{:S(2)}, u32[]{:S(2)}) async-start(bf16[32,4,4,4,128]{4,2,3,1,0:T(4,128)(2,1)} %broadcast_in_dim.146), calls=%async_computation.4 | async-start | bytes 1048576 | tf_op jit(solution)/shard_map/all_to_all | solution.py:28
  122.3 47.5 %all-to-all-start.3 = ((f32[128,4,4,128]{3,2,1,0:T(4,128)}), f32[128,4,4,128]{3,2,1,0:T(4,128)S(1)}, u32[]{:S(2)}, u32[]{:S(2)}) async-start(f32[128,4,4,128]{3,2,1,0:T(4,128)} %broadcast_select_fusion), calls=%async_computation.3 | async-start | bytes 2097152 | tf_op jit(solution)/shard_map/all_to_all | solution.py:138
  151.2 11.9 %copy-start.5 = (pred[128,4,16]{2,1,0:T(4,128)(4,1)}, pred[128,4,16]{2,1,0:T(4,128)(4,1)S(1)}, u32[]{:S(2)}) copy-start(pred[128,4,16]{2,1,0:T(4,128)(4,1)S(1)} %broadcast_compare_fusion) | copy-start | bytes 24580
  151.2 2.7 copy-start.44
  153.8 3.7 %copy-start.2 = (bf16[2,128,4,16,128]{4,3,2,1,0:T(8,128)(2,1)}, bf16[2,128,4,16,128]{4,3,2,1,0:T(8,128)(2,1)S(1)}, u32[]{:S(2)}) copy-start(bf16[2,128,4,16,128]{4,3,2,1,0:T(8,128)(2,1)S(1)} %fusion) | copy-start | bytes 12582916
  165.7 1.3 copy-start.30
  165.7 1.3 copy-start.31
  168.5 12.0 %copy-start.12 = (bf16[1,4,4,2,512]{4,3,2,1,0:T(2,128)(2,1)S(1)}, bf16[1,4,4,2,512]{4,3,2,1,0:T(2,128)(2,1)}, u32[]{:S(2)}) copy-start(bf16[1,4,4,2,512]{4,3,2,1,0:T(2,128)(2,1)} %param.22) | copy-start | bytes 98308
  169.8 1.0 copy-start.4
  170.8 34.4 %all-to-all-start.5 = ((f32[32,4,17,128]{3,1,2,0:T(4,128)}), f32[32,4,17,128]{3,1,2,0:T(4,128)S(1)}, u32[]{:S(2)}, u32[]{:S(2)}) async-start(f32[32,4,17,128]{3,1,2,0:T(4,128)} %copy.372), calls=%async_computation.5 | async-start | bytes 2228224 | tf_op jit(solution)/shard_map/all_to_all | solution.py:226
  180.5 18.1 %copy-start.35 = (pred[4,8]{1,0:T(4,128)(4,1)}, pred[4,8]{1,0:T(4,128)(4,1)S(1)}, u32[]{:S(2)}) copy-start(pred[4,8]{1,0:T(4,128)(4,1)S(1)} %concatenate.50) | copy-start | bytes 100
  181.2 17.1 %copy-start.33 = (bf16[4,4,512]{2,1,0:T(4,128)(2,1)}, bf16[4,4,512]{2,1,0:T(4,128)(2,1)S(1)}, u32[]{:S(2)}) copy-start(bf16[4,4,512]{2,1,0:T(4,128)(2,1)S(1)} %get-tuple-element.10) | copy-start | bytes 49156
  181.2 5.0 %copy-start.25 = (f32[1,2048]{1,0:T(1,128)S(1)}, f32[1,2048]{1,0:T(1,128)}, u32[]{:S(2)}) copy-start(f32[1,2048]{1,0:T(1,128)} %param.27) | copy-start | bytes 24580
  181.2 5.0 %copy-start.38 = (f32[16]{0:T(128)S(1)}, f32[16]{0:T(128)}, u32[]{:S(2)}) copy-start(f32[16]{0:T(128)} %copy-done.37) | copy-start | bytes 196
  181.2 5.0 %copy-start.42 = (bf16[1,2048,4]{1,2,0:T(4,128)(2,1)S(1)}, bf16[1,2048,4]{1,2,0:T(4,128)(2,1)}, u32[]{:S(2)}) copy-start(bf16[1,2048,4]{1,2,0:T(4,128)(2,1)} %param.25) | copy-start | bytes 49156
  181.2 6.0 %copy-start.14 = (f32[4,4,1,512]{3,1,0,2:T(4,128)S(1)}, f32[4,4,1,512]{3,1,0,2:T(4,128)}, u32[]{:S(2)}) copy-start(f32[4,4,1,512]{3,1,0,2:T(4,128)} %get-tuple-element.35) | copy-start | bytes 98308
  181.2 6.3 %copy-start.13 = (f32[4,4,4,128]{3,2,1,0:T(4,128)S(1)}, f32[4,4,4,128]{3,2,1,0:T(4,128)}, u32[]{:S(2)}) copy-start(f32[4,4,4,128]{3,2,1,0:T(4,128)} %get-tuple-element.29) | copy-start | bytes 98308
  188.9 9.5 %copy-start.22 = (bf16[4,4,4,128]{3,2,1,0:T(4,128)(2,1)S(1)}, bf16[4,4,4,128]{3,2,1,0:T(4,128)(2,1)}, u32[]{:S(2)}) copy-start(bf16[4,4,4,128]{3,2,1,0:T(4,128)(2,1)} %copy-done.21) | copy-start | bytes 49156
  188.9 9.5 %copy-start.45 = (f32[1,4]{1,0:T(1,128)S(1)}, f32[1,4]{1,0:T(1,128)}, u32[]{:S(2)}) copy-start(f32[1,4]{1,0:T(1,128)} %param.29) | copy-start | bytes 52
  198.6 6.6 %copy-start.29 = (f32[4,4,4,8]{3,1,2,0:T(4,128)}, f32[4,4,4,8]{3,1,2,0:T(4,128)S(1)}, u32[]{:S(2)}) copy-start(f32[4,4,4,8]{3,1,2,0:T(4,128)S(1)} %get-tuple-element.43) | copy-start | bytes 6148
  198.6 8.5 %copy-start.19 = (f32[4,4,4]{1,2,0:T(4,128)}, f32[4,4,4]{1,2,0:T(4,128)S(1)}, u32[]{:S(2)}) copy-start(f32[4,4,4]{1,2,0:T(4,128)S(1)} %get-tuple-element.42) | copy-start | bytes 772
  205.5 1.5 copy-start.20
  209.5 15.4 %copy-start.26 = (f32[1,2048]{1,0:T(1,128)S(1)}, f32[1,2048]{1,0:T(1,128)}, u32[]{:S(2)}) copy-start(f32[1,2048]{1,0:T(1,128)} %param.27) | copy-start | bytes 24580
  211.0 5.0 %collective-permute-start = (f32[16,2048]{1,0:T(8,128)S(1)}, f32[16,2048]{1,0:T(8,128)S(1)}, u32[]{:S(2)}, u32[]{:S(2)}) collective-permute-start(f32[16,2048]{1,0:T(8,128)S(1)} %fusion.3), channel_id=1, source_target_pairs={{0,1},{1,0},{2,3},{3,2},{4,5},{5,4},{6,7},{7,6},{8,9},{9,8},{10,11... | collective-permute-start | bytes 393224 | tf_op jit(solution)/shard_map/ppermute | solution.py:36
  215.9 6.6 %collective-permute-start.1 = (f32[16,2048]{1,0:T(8,128)S(1)}, f32[16,2048]{1,0:T(8,128)S(1)}, u32[]{:S(2)}, u32[]{:S(2)}) collective-permute-start(f32[16,2048]{1,0:T(8,128)S(1)} %add.211), channel_id=1, source_target_pairs={{0,2},{1,3},{2,0},{3,1},{4,6},{5,7},{6,4},{7,5},{8,10},{9,11},{10,... | collective-permute-start | bytes 393224 | tf_op jit(solution)/shard_map/ppermute | solution.py:36
  222.5 6.9 %copy-start.10 = (bf16[16,2048]{1,0:T(8,128)(2,1)}, bf16[16,2048]{1,0:T(8,128)(2,1)S(1)}, u32[]{:S(2)}) copy-start(bf16[16,2048]{1,0:T(8,128)(2,1)S(1)} %fusion.53) | copy-start | bytes 196612
  222.5 2.2 collective-permute-start.2
  224.9 4.6 %copy-start.39 = (f32[16]{0:T(128)}, f32[16]{0:T(128)S(1)}, u32[]{:S(2)}) copy-start(f32[16]{0:T(128)S(1)} %add_rsqrt_fusion.6) | copy-start | bytes 196
  224.9 4.7 %copy-start.9 = (bf16[1,4,3,3,512]{4,2,1,3,0:T(4,128)(2,1)S(1)}, bf16[1,4,3,3,512]{4,2,1,3,0:T(4,128)(2,1)}, u32[]{:S(2)}) copy-start(bf16[1,4,3,3,512]{4,2,1,3,0:T(4,128)(2,1)} %copy-done.8) | copy-start | bytes 110596
  224.9 4.7 %copy-start.16 = (f32[3,512]{1,0:T(4,128)S(1)}, f32[3,512]{1,0:T(4,128)}, u32[]{:S(2)}) copy-start(f32[3,512]{1,0:T(4,128)} %copy-done.15) | copy-start | bytes 18436
  224.9 4.7 %copy-start.18 = (f32[3,512]{1,0:T(4,128)S(1)}, f32[3,512]{1,0:T(4,128)}, u32[]{:S(2)}) copy-start(f32[3,512]{1,0:T(4,128)} %copy-done.17) | copy-start | bytes 18436
  229.5 25.7 %copy-start.6 = (pred[128,4,16]{2,1,0:T(4,128)(4,1)S(1)}, pred[128,4,16]{2,1,0:T(4,128)(4,1)}, u32[]{:S(2)}) copy-start(pred[128,4,16]{2,1,0:T(4,128)(4,1)} %copy-done.5) | copy-start | bytes 24580
  229.5 25.7 %copy-start.46 = (f32[1,4]{1,0:T(1,128)S(1)}, f32[1,4]{1,0:T(1,128)}, u32[]{:S(2)}) copy-start(f32[1,4]{1,0:T(1,128)} %param.29) | copy-start | bytes 52
  255.2 3.1 copy-start.3
  263.6 6.0 %copy-start.27 = (f32[1,2048]{1,0:T(1,128)S(1)}, f32[1,2048]{1,0:T(1,128)}, u32[]{:S(2)}) copy-start(f32[1,2048]{1,0:T(1,128)} %param.27) | copy-start | bytes 24580
  263.6 6.0 %copy-start.40 = (f32[16]{0:T(128)S(1)}, f32[16]{0:T(128)}, u32[]{:S(2)}) copy-start(f32[16]{0:T(128)} %copy-done.39) | copy-start | bytes 196
  263.6 6.0 %copy-start.43 = (bf16[1,2048,4]{1,2,0:T(4,128)(2,1)S(1)}, bf16[1,2048,4]{1,2,0:T(4,128)(2,1)}, u32[]{:S(2)}) copy-start(bf16[1,2048,4]{1,2,0:T(4,128)(2,1)} %param.25) | copy-start | bytes 49156
  264.9 33.5 %all-to-all-start.7 = ((f32[32,4,17,128]{3,1,2,0:T(4,128)}), f32[32,4,17,128]{3,1,2,0:T(4,128)S(1)}, u32[]{:S(2)}, u32[]{:S(2)}) async-start(f32[32,4,17,128]{3,1,2,0:T(4,128)} %copy.397), calls=%async_computation.7 | async-start | bytes 2228224 | tf_op jit(solution)/shard_map/all_to_all | solution.py:226
  272.2 9.4 %copy-start.34 = (bf16[4,4,512]{2,1,0:T(4,128)(2,1)S(1)}, bf16[4,4,512]{2,1,0:T(4,128)(2,1)}, u32[]{:S(2)}) copy-start(bf16[4,4,512]{2,1,0:T(4,128)(2,1)} %copy-done.33) | copy-start | bytes 49156
  272.2 9.4 %copy-start.36 = (pred[4,8]{1,0:T(4,128)(4,1)S(1)}, pred[4,8]{1,0:T(4,128)(4,1)}, u32[]{:S(2)}) copy-start(pred[4,8]{1,0:T(4,128)(4,1)} %copy-done.35) | copy-start | bytes 100
  272.2 9.4 %copy-start.47 = (f32[1,4]{1,0:T(1,128)S(1)}, f32[1,4]{1,0:T(1,128)}, u32[]{:S(2)}) copy-start(f32[1,4]{1,0:T(1,128)} %param.29) | copy-start | bytes 52
  281.8 1.4 copy-start.28
  304.1 5.8 %collective-permute-start.3 = (f32[16,2048]{1,0:T(8,128)S(1)}, f32[16,2048]{1,0:T(8,128)S(1)}, u32[]{:S(2)}, u32[]{:S(2)}) collective-permute-start(f32[16,2048]{1,0:T(8,128)S(1)} %fusion.1), channel_id=1, source_target_pairs={{0,1},{1,0},{2,3},{3,2},{4,5},{5,4},{6,7},{7,6},{8,9},{9,8},{10,11... | collective-permute-start | bytes 393224 | tf_op jit(solution)/shard_map/ppermute | solution.py:36
  309.9 6.7 %collective-permute-start.4 = (f32[16,2048]{1,0:T(8,128)S(1)}, f32[16,2048]{1,0:T(8,128)}, u32[]{:S(2)}, u32[]{:S(2)}) collective-permute-start(f32[16,2048]{1,0:T(8,128)S(1)} %add.226), channel_id=1, source_target_pairs={{0,2},{1,3},{2,0},{3,1},{4,6},{5,7},{6,4},{7,5},{8,10},{9,11},{10,... | collective-permute-start | bytes 393224 | tf_op jit(solution)/shard_map/ppermute | solution.py:36
  312.0 4.6 %copy-start.11 = (bf16[16,2048]{1,0:T(8,128)(2,1)S(1)}, bf16[16,2048]{1,0:T(8,128)(2,1)}, u32[]{:S(2)}) copy-start(bf16[16,2048]{1,0:T(8,128)(2,1)} %copy-done.10) | copy-start | bytes 196612

commit v5 on v4

--- a/solution.py
+++ b/solution.py
@@ -30,6 +30,11 @@
 
 def head_sum(value):
     peers = lax.axis_size("head")
+    if peers == 4:
+        first = [(i, i ^ 1) for i in range(peers)]
+        second = [(i, (i + 1) % peers if i % 2 else (i - 1) % peers) for i in range(peers)]
+        value = value + lax.ppermute(value, "head", first)
+        return value + lax.ppermute(value, "head", second)
     step = 1
     while step < peers:
         pairs = [(i, i ^ step) for i in range(peers)]

time: 321 us -> 320 us (level)
  transfers between devices with their start and end apart: 12 -> 12, of which waited for: 11 -> 11; matrix products, arithmetic and copies ran while one was open for 25% -> 26% of each run, Pallas kernels for 4% -> 4%
where the time goes in v5:
time: 320 us; the launch traced here: 315 us
  waiting for transfers between devices  99.2 us (31%)
  local copies, waits for them, and re-layouts  75.2 us (24%)
  starting transfers between devices  51.4 us (16%)
  matrix products  27.5 us (9%)
  blocking collectives  23.9 us (7%)
  other arithmetic  23 us (7%)
  Pallas kernels  12.9 us (4%)
    all_to_all x1, waiting for transfers between devices, shards(): lax.all_to_all(looked_up.reshape(groups, rows, width), 'req', 0, 0, tiled...  40.7 us
    all_to_all x3, waiting for transfers between devices, spread(): return lax.all_to_all(copies, axis, 0, 0, tiled=True)  25 us
    all_to_all x1, blocking collectives, spread(): return lax.all_to_all(copies, axis, 0, 0, tiled=True)  23.9 us
    all_to_all x3, starting transfers between devices, spread(): return lax.all_to_all(copies, axis, 0, 0, tiled=True)  21.7 us
    unnamed x105, local copies, waits for them, and re-layouts  21.7 us
    all_to_all x2, waiting for transfers between devices, layer(): gathered = lax.all_to_all(packed, 'req', 0, 0, tiled=True)  19.5 us
    all_to_all x2, starting transfers between devices, layer(): gathered = lax.all_to_all(packed, 'req', 0, 0, tiled=True)  14.3 us
    pallas_call x2, Pallas kernels, delta_rule(): pl.pallas_call(delta_rule_kernel, out_shape=(jax.ShapeDtypeStruct((slots,...  12.9 us
  transfers between devices with their start and end apart: 12, of which 11 were waited for; matrix products, arithmetic and copies ran while one was open for 26% of the time, Pallas kernels for 4%

profile of v5, /device:TPU:2, one launch (start us, length us, event | category | flops | bytes accessed | tf_op | source)
XLA Modules:
  0.0 314.5 jit_solution(5367259693527491261)
XLA Ops:
  0.6 1.5 broadcast_in_dim.135
  2.1 11.5 %all-to-all-start = ((s32[32,4,4]{2,1,0:T(4,128)}), s32[32,4,4]{2,1,0:T(4,128)S(1)}, u32[]{:S(2)}, u32[]{:S(2)}) async-start(s32[32,4,4]{2,1,0:T(4,128)} %broadcast_in_dim.135), calls=%async_computation | async-start | bytes 131072 | tf_op jit(solution)/shard_map/all_to_all | solution.py:28
  13.6 9.9 %all-to-all-done = s32[32,4,4]{2,1,0:T(4,128)S(1)} async-done(((s32[32,4,4]{2,1,0:T(4,128)}), s32[32,4,4]{2,1,0:T(4,128)S(1)}, u32[]{:S(2)}, u32[]{:S(2)}) %all-to-all-start) | async-done | bytes 2080 | tf_op jit(solution)/shard_map/all_to_all | solution.py:28
  23.7 3.3 %convolution_convert_fusion = bf16[512,2048]{1,0:T(8,128)(2,1)} fusion(bf16[250,2048]{1,0:T(8,128)(2,1)} %param.18, s32[250]{0:T(256)S(1)} %iota_add_fusion, s32[512]{0:T(512)S(1)} %eq.19), kind=kOutput, calls=%fused_computation.5 | convolution fusion | flops 525464576 | bytes 3124200 | tf_op jit(solution)/shard_map/dot_general | solution.py:135
  27.0 4.9 %all-to-all-start.1 = ((bf16[32,16,2048]{2,1,0:T(8,128)(2,1)}), bf16[32,16,2048]{2,1,0:T(8,128)(2,1)}, u32[]{:S(2)}, u32[]{:S(2)}) async-start(bf16[32,16,2048]{2,1,0:T(8,128)(2,1)} %bitcast.177), calls=%async_computation.1 | async-start | bytes 4194304 | tf_op jit(solution)/shard_map/all_to_all | solution.py:136
  32.0 8.9 %copy.355 = bf16[1,2048,3,512]{1,3,2,0:T(8,128)(2,1)} copy(bf16[1,2048,3,512]{3,1,2,0:T(8,128)(2,1)} %param.23) | data formatting | bytes 12582912 | tf_op args[8]
  40.9 40.7 %all-to-all-done.1 = bf16[32,16,2048]{2,1,0:T(8,128)(2,1)} async-done(((bf16[32,16,2048]{2,1,0:T(8,128)(2,1)}), bf16[32,16,2048]{2,1,0:T(8,128)(2,1)}, u32[]{:S(2)}, u32[]{:S(2)}) %all-to-all-start.1) | async-done | bytes 2097184 | tf_op jit(solution)/shard_map/all_to_all | solution.py:136
  81.6 1.9 reduce_sum.172
  84.3 4.8 %all-to-all-start.2 = ((bf16[4,16,2048]{2,1,0:T(8,128)(2,1)}), bf16[4,16,2048]{2,1,0:T(8,128)(2,1)S(1)}, u32[]{:S(2)}, u32[]{:S(2)}) async-start(bf16[4,16,2048]{2,1,0:T(8,128)(2,1)} %broadcast_in_dim.136), calls=%async_computation.2 | async-start | bytes 524288 | tf_op jit(solution)/shard_map/all_to_all | solution.py:28
  89.1 5.2 %all-to-all-done.2 = bf16[4,16,2048]{2,1,0:T(8,128)(2,1)S(1)} async-done(((bf16[4,16,2048]{2,1,0:T(8,128)(2,1)}), bf16[4,16,2048]{2,1,0:T(8,128)(2,1)S(1)}, u32[]{:S(2)}, u32[]{:S(2)}) %all-to-all-start.2) | async-done | bytes 262176 | tf_op jit(solution)/shard_map/all_to_all | solution.py:28
  94.5 4.5 %convolution_convert_fusion.2 = bf16[16,1536]{1,0:T(8,128)(2,1)S(1)} fusion(bf16[2048,1536]{0,1:T(8,128)(2,1)} %bitcast.173, bf16[16,2048]{1,0:T(8,128)(2,1)S(1)} %reduce_sum.173, f32[2048]{0:T(1024)S(1)} %bitcast.205, f32[16]{0:T(128)S(1)} %add_rsqrt_fusion.7), kind=kOutput, calls=%fused_computation.7 | convolution fusion | flops 100818944 | bytes 6414400 | tf_op jit(solution)/shard_map/dot_general | solution.py:177
  100.8 1.0 broadcast_in_dim.146
  101.9 5.4 %all-to-all-start.4 = ((bf16[32,4,4,4,128]{4,2,3,1,0:T(4,128)(2,1)}), bf16[32,4,4,4,128]{4,2,3,1,0:T(4,128)(2,1)}, u32[]{:S(2)}, u32[]{:S(2)}) async-start(bf16[32,4,4,4,128]{4,2,3,1,0:T(4,128)(2,1)} %broadcast_in_dim.146), calls=%async_computation.4 | async-start | bytes 1048576 | tf_op jit(solution)/shard_map/all_to_all | solution.py:28
  107.3 1.2 gather_fusion.2
  108.6 2.4 gather_fusion
  111.1 1.3 broadcast_select_fusion
  112.4 9.9 %all-to-all-done.4 = bf16[32,4,4,4,128]{4,2,3,1,0:T(4,128)(2,1)} async-done(((bf16[32,4,4,4,128]{4,2,3,1,0:T(4,128)(2,1)}), bf16[32,4,4,4,128]{4,2,3,1,0:T(4,128)(2,1)}, u32[]{:S(2)}, u32[]{:S(2)}) %all-to-all-start.4) | async-done | bytes 524320 | tf_op jit(solution)/shard_map/all_to_all | solution.py:28
  122.3 4.2 %all-to-all-start.3 = ((f32[128,4,4,128]{3,2,1,0:T(4,128)}), f32[128,4,4,128]{3,2,1,0:T(4,128)S(1)}, u32[]{:S(2)}, u32[]{:S(2)}) async-start(f32[128,4,4,128]{3,2,1,0:T(4,128)} %broadcast_select_fusion), calls=%async_computation.3 | async-start | bytes 2097152 | tf_op jit(solution)/shard_map/all_to_all | solution.py:143
  126.5 11.2 %copy.364 = bf16[1,128,16,2,512]{1,4,3,2,0:T(8,128)(2,1)} copy(bf16[1,128,16,2,512]{4,3,2,1,0:T(2,128)(2,1)} %param.19) | data formatting | bytes 8388608 | tf_op args[4]
  137.7 7.9 %copy.365 = bf16[128,16,2,4,128]{4,1,3,0,2:T(8,128)(2,1)} copy(bf16[128,16,2,4,128]{0,4,3,2,1:T(8,128)(2,1)} %bitcast.176) | data formatting | bytes 8388608 | tf_op jit(solution)/shard_map/reshape;squeeze | solution.py:147
  145.6 5.3 %gather_fusion.1 = bf16[128,2,4,16,128]{4,3,2,1,0:T(8,128)(2,1)} fusion(bf16[2,128,4,16,128]{4,3,2,1,0:T(8,128)(2,1)} %bitcast.175, s32[1024]{0:T(1024)S(1)} %pad_clamp_fusion), kind=kCustom, calls=%fused_computation.1 | custom fusion | bytes 8389120 | tf_op jit(solution)/shard_map/jit(_take)/gather | solution.py:149
  151.2 2.6 fusion
  153.9 3.7 %select_reduce_fusion.1 = (f32[128,4,4]{1,2,0:T(4,128)S(1)}, f32[128,4,4,16]{3,1,2,0:T(4,128)}) fusion(pred[128,4,16]{2,1,0:T(4,128)(4,1)S(1)} %broadcast_compare_fusion, f32[4]{0:T(128)S(1)} %bitcast.225, bf16[128,4,4,128]{3,1,2,0:T(4,128)(2,1)} %bitcast.21, bf16[2,128,4,16,128]{4,3,2,1,0:T(8,128)(2,1)S(1)} %fusion), kind=kOutput, calls=%fused_computation.58 | convolution fusion | flops 8484864 | bytes 2826752 | tf_op jit(solution)/shard_map/rthd,rhwd->rthw/dot_general | solution.py:199
  158.3 3.1 fusion.35
  161.4 1.7 copy.369
  163.0 2.7 fusion.9
  165.8 1.2 copy.368
  167.1 1.4 pad_maximum_fusion
  168.5 1.3 copy.372
  169.8 1.0 copy-done.4
  170.8 9.6 %all-to-all-start.5 = ((f32[32,4,17,128]{3,1,2,0:T(4,128)}), f32[32,4,17,128]{3,1,2,0:T(4,128)S(1)}, u32[]{:S(2)}, u32[]{:S(2)}) async-start(f32[32,4,17,128]{3,1,2,0:T(4,128)} %copy.372), calls=%async_computation.5 | async-start | bytes 2228224 | tf_op jit(solution)/shard_map/all_to_all | solution.py:231
  181.2 2.4 copy.449
  183.6 2.6 reshape.276.state_ref
  187.5 1.4 copy.358
  188.9 1.4 copy.357
  190.3 6.4 %shard_map.158 = (f32[4,128,512]{2,1,0:T(8,128)}, f32[4,4,512]{2,1,0:T(4,128)}) custom-call(f32[64]{0:T(128)} %reshape_reshape.6.beta_ref, f32[4,128,512]{2,1,0:T(8,128)} %reshape.276.state_ref, f32[4,4,128,4]{3,2,1,0:T(8,128)} %bitcast.182, f32[4,4,128,4]{3,2,1,0:T(8,128)} %bitcast.180, f32[4,4,512]{2,1,0:T(4,128)} %get-tuple-element.33.value_ref), custom_call_target="tpu_custom_call" | custom-call | flops 8388608 | bytes 2097152 | tf_op jit(solution)/shard_map/pallas_call | solution.py:76
  199.4 1.4 fusion.81
  200.8 4.4 %all-to-all-done.5 = f32[32,4,17,128]{3,1,2,0:T(4,128)S(1)} async-done(((f32[32,4,17,128]{3,1,2,0:T(4,128)}), f32[32,4,17,128]{3,1,2,0:T(4,128)S(1)}, u32[]{:S(2)}, u32[]{:S(2)}) %all-to-all-start.5) | async-done | bytes 1114144 | tf_op jit(solution)/shard_map/all_to_all | solution.py:231
  207.0 1.0 copy.378
  209.5 1.1 fusion.25
  211.0 1.5 collective-permute-start
  212.4 3.5 %collective-permute-done = f32[16,2048]{1,0:T(8,128)S(1)} collective-permute-done((f32[16,2048]{1,0:T(8,128)S(1)}, f32[16,2048]{1,0:T(8,128)S(1)}, u32[]{:S(2)}, u32[]{:S(2)}) %collective-permute-start) | collective-permute-done | bytes 131104 | tf_op jit(solution)/shard_map/ppermute | solution.py:36
  216.1 4.9 %collective-permute-done.1 = f32[16,2048]{1,0:T(8,128)S(1)} collective-permute-done((f32[16,2048]{1,0:T(8,128)S(1)}, f32[16,2048]{1,0:T(8,128)S(1)}, u32[]{:S(2)}, u32[]{:S(2)}) %collective-permute-start.1) | collective-permute-done | bytes 131104 | tf_op jit(solution)/shard_map/ppermute | solution.py:37
  221.0 1.3 collective-permute-start.2
  223.4 4.5 %convolution_convert_fusion.1 = bf16[16,1536]{1,0:T(8,128)(2,1)S(1)} fusion(bf16[2048,1536]{0,1:T(8,128)(2,1)} %bitcast.174, bf16[16,2048]{1,0:T(8,128)(2,1)S(1)} %collective-permute-done.2, f32[16]{0:T(128)S(1)} %add_rsqrt_fusion.6, f32[2048]{0:T(1024)S(1)} %bitcast.207), kind=kOutput, calls=%fused_computation.6 | convolution fusion | flops 100818944 | bytes 6414400 | tf_op jit(solution)/shard_map/dot_general | solution.py:177
  229.4 23.9 %all_to_all.50 = bf16[32,4,4,4,128]{4,2,3,1,0:T(4,128)(2,1)S(1)} all-to-all(bf16[32,4,4,4,128]{4,2,3,1,0:T(4,128)(2,1)S(1)} %broadcast_in_dim.150), channel_id=1, replica_groups=mesh['section'=2,'req'=32,'head'=4] {'req'}, dimensions={0} | all-to-all | bytes 1048576 | tf_op jit(solution)/shard_map/all_to_all | solution.py:28
  253.3 3.1 select_reduce_fusion
  256.4 1.8 fusion.10
  258.2 1.4 fusion.37
  259.8 1.5 copy.393
  261.6 1.3 copy.397
  262.9 4.7 %all-to-all-start.7 = ((f32[32,4,17,128]{3,1,2,0:T(4,128)}), f32[32,4,17,128]{3,1,2,0:T(4,128)S(1)}, u32[]{:S(2)}, u32[]{:S(2)}) async-start(f32[32,4,17,128]{3,1,2,0:T(4,128)} %copy.397), calls=%async_computation.7 | async-start | bytes 2228224 | tf_op jit(solution)/shard_map/all_to_all | solution.py:231
  268.9 1.4 copy.386
  270.3 1.3 copy.385
  271.6 6.4 %shard_map.159 = (f32[4,128,512]{2,1,0:T(8,128)}, f32[4,4,512]{2,1,0:T(4,128)}) custom-call(f32[64]{0:T(128)} %reshape_reshape.7.beta_ref, f32[4,128,512]{2,1,0:T(8,128)} %reshape.276.state_ref, f32[4,4,128,4]{3,2,1,0:T(8,128)} %bitcast.181, f32[4,4,128,4]{3,2,1,0:T(8,128)} %bitcast.179, f32[4,4,512]{2,1,0:T(4,128)} %get-tuple-element.30.value_ref), custom_call_target="tpu_custom_call" | custom-call | flops 8388608 | bytes 2097152 | tf_op jit(solution)/shard_map/pallas_call | solution.py:76
  281.3 15.1 %all-to-all-done.7 = f32[32,4,17,128]{3,1,2,0:T(4,128)S(1)} async-done(((f32[32,4,17,128]{3,1,2,0:T(4,128)}), f32[32,4,17,128]{3,1,2,0:T(4,128)S(1)}, u32[]{:S(2)}, u32[]{:S(2)}) %all-to-all-start.7) | async-done | bytes 1114144 | tf_op jit(solution)/shard_map/all_to_all | solution.py:231
  298.3 1.0 copy.403
  300.7 1.1 fusion.26
  302.1 2.7 collective-permute-start.3
  304.8 2.9 collective-permute-done.3
  308.5 1.5 broadcast_select_fusion.1
  310.0 1.3 select_n.91
  311.3 1.7 collective-permute-done.4
  312.9 0.9 fusion.66
  (209 shorter events, 25.0 us)
Async XLA Ops:
  0.6 209.9 %copy-start = (bf16[1,512,2048]{2,1,0:T(8,128)(2,1)S(1)}, bf16[1,512,2048]{2,1,0:T(8,128)(2,1)}, u32[]{:S(2)}) copy-start(bf16[1,512,2048]{2,1,0:T(8,128)(2,1)} %param.24) | copy-start | bytes 6291460
  2.1 21.5 %all-to-all-start = ((s32[32,4,4]{2,1,0:T(4,128)}), s32[32,4,4]{2,1,0:T(4,128)S(1)}, u32[]{:S(2)}, u32[]{:S(2)}) async-start(s32[32,4,4]{2,1,0:T(4,128)} %broadcast_in_dim.135), calls=%async_computation | async-start | bytes 131072 | tf_op jit(solution)/shard_map/all_to_all | solution.py:28
  27.0 4.9 %copy-start.23 = (bf16[1,4,3,3,512]{4,1,3,2,0:T(4,128)(2,1)S(1)}, bf16[1,4,3,3,512]{4,1,3,2,0:T(4,128)(2,1)}, u32[]{:S(2)}) copy-start(bf16[1,4,3,3,512]{4,1,3,2,0:T(4,128)(2,1)} %param.21) | copy-start | bytes 110596
  27.0 54.6 %all-to-all-start.1 = ((bf16[32,16,2048]{2,1,0:T(8,128)(2,1)}), bf16[32,16,2048]{2,1,0:T(8,128)(2,1)}, u32[]{:S(2)}, u32[]{:S(2)}) async-start(bf16[32,16,2048]{2,1,0:T(8,128)(2,1)} %bitcast.177), calls=%async_computation.1 | async-start | bytes 4194304 | tf_op jit(solution)/shard_map/all_to_all | solution.py:136
  32.0 67.1 %copy-start.8 = (bf16[1,4,3,3,512]{4,2,1,3,0:T(4,128)(2,1)}, bf16[1,4,3,3,512]{4,2,1,3,0:T(4,128)(2,1)S(1)}, u32[]{:S(2)}) copy-start(bf16[1,4,3,3,512]{4,2,1,3,0:T(4,128)(2,1)S(1)} %copy.450) | copy-start | bytes 110596
  32.0 8.9 %copy-start.32 = (f32[1,4,3,512]{3,1,2,0:T(4,128)S(1)}, f32[1,4,3,512]{3,1,2,0:T(4,128)}, u32[]{:S(2)}) copy-start(f32[1,4,3,512]{3,1,2,0:T(4,128)} %param.26) | copy-start | bytes 73732
  40.9 53.6 %copy-start.24 = (f32[1,2048]{1,0:T(1,128)S(1)}, f32[1,2048]{1,0:T(1,128)}, u32[]{:S(2)}) copy-start(f32[1,2048]{1,0:T(1,128)} %param.27) | copy-start | bytes 24580
  84.3 10.0 %all-to-all-start.2 = ((bf16[4,16,2048]{2,1,0:T(8,128)(2,1)}), bf16[4,16,2048]{2,1,0:T(8,128)(2,1)S(1)}, u32[]{:S(2)}, u32[]{:S(2)}) async-start(bf16[4,16,2048]{2,1,0:T(8,128)(2,1)} %broadcast_in_dim.136), calls=%async_computation.2 | async-start | bytes 524288 | tf_op jit(solution)/shard_map/all_to_all | solution.py:28
  89.1 10.1 %copy-start.15 = (f32[3,512]{1,0:T(4,128)}, f32[3,512]{1,0:T(4,128)S(1)}, u32[]{:S(2)}) copy-start(f32[3,512]{1,0:T(4,128)S(1)} %get-tuple-element.48) | copy-start | bytes 18436
  89.1 10.1 %copy-start.17 = (f32[3,512]{1,0:T(4,128)}, f32[3,512]{1,0:T(4,128)S(1)}, u32[]{:S(2)}) copy-start(f32[3,512]{1,0:T(4,128)S(1)} %get-tuple-element.49) | copy-start | bytes 18436
  94.5 4.5 %copy-start.37 = (f32[16]{0:T(128)}, f32[16]{0:T(128)S(1)}, u32[]{:S(2)}) copy-start(f32[16]{0:T(128)S(1)} %add_rsqrt_fusion.7) | copy-start | bytes 196
  99.0 8.2 %copy-start.41 = (s32[128]{0:T(128)S(1)}, s32[128]{0:T(128)}, u32[]{:S(2)}) copy-start(s32[128]{0:T(128)} %param.16) | copy-start | bytes 1540
  99.0 8.3 %copy-start.1 = (s32[128]{0:T(128)S(1)}, s32[128]{0:T(128)}, u32[]{:S(2)}) copy-start(s32[128]{0:T(128)} %param.17) | copy-start | bytes 1540
  99.4 9.2 %copy-start.7 = (f32[4,4,3,512]{3,1,0,2:T(4,128)}, f32[4,4,3,512]{3,1,0,2:T(4,128)S(1)}, u32[]{:S(2)}) copy-start(f32[4,4,3,512]{3,1,0,2:T(4,128)S(1)} %divide_multiply_fusion.1) | copy-start | bytes 294916
  100.8 10.1 %copy-start.21 = (bf16[4,4,4,128]{3,2,1,0:T(4,128)(2,1)}, bf16[4,4,4,128]{3,2,1,0:T(4,128)(2,1)S(1)}, u32[]{:S(2)}) copy-start(bf16[4,4,4,128]{3,2,1,0:T(4,128)(2,1)S(1)} %get-tuple-element.28) | copy-start | bytes 49156
  101.9 20.4 %all-to-all-start.4 = ((bf16[32,4,4,4,128]{4,2,3,1,0:T(4,128)(2,1)}), bf16[32,4,4,4,128]{4,2,3,1,0:T(4,128)(2,1)}, u32[]{:S(2)}, u32[]{:S(2)}) async-start(bf16[32,4,4,4,128]{4,2,3,1,0:T(4,128)(2,1)} %broadcast_in_dim.146), calls=%async_computation.4 | async-start | bytes 1048576 | tf_op jit(solution)/shard_map/all_to_all | solution.py:28
  122.3 47.5 %all-to-all-start.3 = ((f32[128,4,4,128]{3,2,1,0:T(4,128)}), f32[128,4,4,128]{3,2,1,0:T(4,128)S(1)}, u32[]{:S(2)}, u32[]{:S(2)}) async-start(f32[128,4,4,128]{3,2,1,0:T(4,128)} %broadcast_select_fusion), calls=%async_computation.3 | async-start | bytes 2097152 | tf_op jit(solution)/shard_map/all_to_all | solution.py:143
  151.2 11.9 %copy-start.5 = (pred[128,4,16]{2,1,0:T(4,128)(4,1)}, pred[128,4,16]{2,1,0:T(4,128)(4,1)S(1)}, u32[]{:S(2)}) copy-start(pred[128,4,16]{2,1,0:T(4,128)(4,1)S(1)} %broadcast_compare_fusion) | copy-start | bytes 24580
  151.2 2.7 copy-start.44
  153.8 3.7 %copy-start.2 = (bf16[2,128,4,16,128]{4,3,2,1,0:T(8,128)(2,1)}, bf16[2,128,4,16,128]{4,3,2,1,0:T(8,128)(2,1)S(1)}, u32[]{:S(2)}) copy-start(bf16[2,128,4,16,128]{4,3,2,1,0:T(8,128)(2,1)S(1)} %fusion) | copy-start | bytes 12582916
  165.7 1.3 copy-start.30
  165.7 1.3 copy-start.31
  168.5 12.0 %copy-start.12 = (bf16[1,4,4,2,512]{4,3,2,1,0:T(2,128)(2,1)S(1)}, bf16[1,4,4,2,512]{4,3,2,1,0:T(2,128)(2,1)}, u32[]{:S(2)}) copy-start(bf16[1,4,4,2,512]{4,3,2,1,0:T(2,128)(2,1)} %param.22) | copy-start | bytes 98308
  169.8 1.0 copy-start.4
  170.8 34.4 %all-to-all-start.5 = ((f32[32,4,17,128]{3,1,2,0:T(4,128)}), f32[32,4,17,128]{3,1,2,0:T(4,128)S(1)}, u32[]{:S(2)}, u32[]{:S(2)}) async-start(f32[32,4,17,128]{3,1,2,0:T(4,128)} %copy.372), calls=%async_computation.5 | async-start | bytes 2228224 | tf_op jit(solution)/shard_map/all_to_all | solution.py:231
  180.5 18.1 %copy-start.35 = (pred[4,8]{1,0:T(4,128)(4,1)}, pred[4,8]{1,0:T(4,128)(4,1)S(1)}, u32[]{:S(2)}) copy-start(pred[4,8]{1,0:T(4,128)(4,1)S(1)} %concatenate.50) | copy-start | bytes 100
  181.2 17.1 %copy-start.33 = (bf16[4,4,512]{2,1,0:T(4,128)(2,1)}, bf16[4,4,512]{2,1,0:T(4,128)(2,1)S(1)}, u32[]{:S(2)}) copy-start(bf16[4,4,512]{2,1,0:T(4,128)(2,1)S(1)} %get-tuple-element.10) | copy-start | bytes 49156
  181.2 5.0 %copy-start.25 = (f32[1,2048]{1,0:T(1,128)S(1)}, f32[1,2048]{1,0:T(1,128)}, u32[]{:S(2)}) copy-start(f32[1,2048]{1,0:T(1,128)} %param.27) | copy-start | bytes 24580
  181.2 5.0 %copy-start.38 = (f32[16]{0:T(128)S(1)}, f32[16]{0:T(128)}, u32[]{:S(2)}) copy-start(f32[16]{0:T(128)} %copy-done.37) | copy-start | bytes 196
  181.2 5.0 %copy-start.42 = (bf16[1,2048,4]{1,2,0:T(4,128)(2,1)S(1)}, bf16[1,2048,4]{1,2,0:T(4,128)(2,1)}, u32[]{:S(2)}) copy-start(bf16[1,2048,4]{1,2,0:T(4,128)(2,1)} %param.25) | copy-start | bytes 49156
  181.2 6.0 %copy-start.14 = (f32[4,4,1,512]{3,1,0,2:T(4,128)S(1)}, f32[4,4,1,512]{3,1,0,2:T(4,128)}, u32[]{:S(2)}) copy-start(f32[4,4,1,512]{3,1,0,2:T(4,128)} %get-tuple-element.35) | copy-start | bytes 98308
  181.2 6.3 %copy-start.13 = (f32[4,4,4,128]{3,2,1,0:T(4,128)S(1)}, f32[4,4,4,128]{3,2,1,0:T(4,128)}, u32[]{:S(2)}) copy-start(f32[4,4,4,128]{3,2,1,0:T(4,128)} %get-tuple-element.29) | copy-start | bytes 98308
  188.9 9.5 %copy-start.22 = (bf16[4,4,4,128]{3,2,1,0:T(4,128)(2,1)S(1)}, bf16[4,4,4,128]{3,2,1,0:T(4,128)(2,1)}, u32[]{:S(2)}) copy-start(bf16[4,4,4,128]{3,2,1,0:T(4,128)(2,1)} %copy-done.21) | copy-start | bytes 49156
  188.9 9.5 %copy-start.45 = (f32[1,4]{1,0:T(1,128)S(1)}, f32[1,4]{1,0:T(1,128)}, u32[]{:S(2)}) copy-start(f32[1,4]{1,0:T(1,128)} %param.29) | copy-start | bytes 52
  198.6 6.6 %copy-start.29 = (f32[4,4,4,8]{3,1,2,0:T(4,128)}, f32[4,4,4,8]{3,1,2,0:T(4,128)S(1)}, u32[]{:S(2)}) copy-start(f32[4,4,4,8]{3,1,2,0:T(4,128)S(1)} %get-tuple-element.43) | copy-start | bytes 6148
  198.6 8.5 %copy-start.19 = (f32[4,4,4]{1,2,0:T(4,128)}, f32[4,4,4]{1,2,0:T(4,128)S(1)}, u32[]{:S(2)}) copy-start(f32[4,4,4]{1,2,0:T(4,128)S(1)} %get-tuple-element.42) | copy-start | bytes 772
  205.5 1.5 copy-start.20
  209.5 13.9 %copy-start.26 = (f32[1,2048]{1,0:T(1,128)S(1)}, f32[1,2048]{1,0:T(1,128)}, u32[]{:S(2)}) copy-start(f32[1,2048]{1,0:T(1,128)} %param.27) | copy-start | bytes 24580
  211.0 5.0 %collective-permute-start = (f32[16,2048]{1,0:T(8,128)S(1)}, f32[16,2048]{1,0:T(8,128)S(1)}, u32[]{:S(2)}, u32[]{:S(2)}) collective-permute-start(f32[16,2048]{1,0:T(8,128)S(1)} %fusion.3), channel_id=1, source_target_pairs={{0,1},{1,0},{2,3},{3,2},{4,5},{5,4},{6,7},{7,6},{8,9},{9,8},{10,11... | collective-permute-start | bytes 393224 | tf_op jit(solution)/shard_map/ppermute | solution.py:36
  215.9 5.1 %collective-permute-start.1 = (f32[16,2048]{1,0:T(8,128)S(1)}, f32[16,2048]{1,0:T(8,128)S(1)}, u32[]{:S(2)}, u32[]{:S(2)}) collective-permute-start(f32[16,2048]{1,0:T(8,128)S(1)} %add.211), channel_id=1, source_target_pairs={{0,3},{1,2},{2,1},{3,0},{4,7},{5,6},{6,5},{7,4},{8,11},{9,10},{10,... | collective-permute-start | bytes 393224 | tf_op jit(solution)/shard_map/ppermute | solution.py:37
  221.0 6.9 %copy-start.10 = (bf16[16,2048]{1,0:T(8,128)(2,1)}, bf16[16,2048]{1,0:T(8,128)(2,1)S(1)}, u32[]{:S(2)}) copy-start(bf16[16,2048]{1,0:T(8,128)(2,1)S(1)} %fusion.53) | copy-start | bytes 196612
  221.0 2.2 collective-permute-start.2
  223.4 4.6 %copy-start.39 = (f32[16]{0:T(128)}, f32[16]{0:T(128)S(1)}, u32[]{:S(2)}) copy-start(f32[16]{0:T(128)S(1)} %add_rsqrt_fusion.6) | copy-start | bytes 196
  223.4 4.7 %copy-start.9 = (bf16[1,4,3,3,512]{4,2,1,3,0:T(4,128)(2,1)S(1)}, bf16[1,4,3,3,512]{4,2,1,3,0:T(4,128)(2,1)}, u32[]{:S(2)}) copy-start(bf16[1,4,3,3,512]{4,2,1,3,0:T(4,128)(2,1)} %copy-done.8) | copy-start | bytes 110596
  223.4 4.7 %copy-start.16 = (f32[3,512]{1,0:T(4,128)S(1)}, f32[3,512]{1,0:T(4,128)}, u32[]{:S(2)}) copy-start(f32[3,512]{1,0:T(4,128)} %copy-done.15) | copy-start | bytes 18436
  223.4 4.7 %copy-start.18 = (f32[3,512]{1,0:T(4,128)S(1)}, f32[3,512]{1,0:T(4,128)}, u32[]{:S(2)}) copy-start(f32[3,512]{1,0:T(4,128)} %copy-done.17) | copy-start | bytes 18436
  228.0 25.3 %copy-start.6 = (pred[128,4,16]{2,1,0:T(4,128)(4,1)S(1)}, pred[128,4,16]{2,1,0:T(4,128)(4,1)}, u32[]{:S(2)}) copy-start(pred[128,4,16]{2,1,0:T(4,128)(4,1)} %copy-done.5) | copy-start | bytes 24580
  228.0 25.3 %copy-start.46 = (f32[1,4]{1,0:T(1,128)S(1)}, f32[1,4]{1,0:T(1,128)}, u32[]{:S(2)}) copy-start(f32[1,4]{1,0:T(1,128)} %param.29) | copy-start | bytes 52
  253.3 3.1 copy-start.3
  261.6 6.0 %copy-start.27 = (f32[1,2048]{1,0:T(1,128)S(1)}, f32[1,2048]{1,0:T(1,128)}, u32[]{:S(2)}) copy-start(f32[1,2048]{1,0:T(1,128)} %param.27) | copy-start | bytes 24580
  261.6 6.0 %copy-start.40 = (f32[16]{0:T(128)S(1)}, f32[16]{0:T(128)}, u32[]{:S(2)}) copy-start(f32[16]{0:T(128)} %copy-done.39) | copy-start | bytes 196
  261.6 6.0 %copy-start.43 = (bf16[1,2048,4]{1,2,0:T(4,128)(2,1)S(1)}, bf16[1,2048,4]{1,2,0:T(4,128)(2,1)}, u32[]{:S(2)}) copy-start(bf16[1,2048,4]{1,2,0:T(4,128)(2,1)} %param.25) | copy-start | bytes 49156
  262.9 33.5 %all-to-all-start.7 = ((f32[32,4,17,128]{3,1,2,0:T(4,128)}), f32[32,4,17,128]{3,1,2,0:T(4,128)S(1)}, u32[]{:S(2)}, u32[]{:S(2)}) async-start(f32[32,4,17,128]{3,1,2,0:T(4,128)} %copy.397), calls=%async_computation.7 | async-start | bytes 2228224 | tf_op jit(solution)/shard_map/all_to_all | solution.py:231
  270.3 9.4 %copy-start.34 = (bf16[4,4,512]{2,1,0:T(4,128)(2,1)S(1)}, bf16[4,4,512]{2,1,0:T(4,128)(2,1)}, u32[]{:S(2)}) copy-start(bf16[4,4,512]{2,1,0:T(4,128)(2,1)} %copy-done.33) | copy-start | bytes 49156
  270.3 9.4 %copy-start.36 = (pred[4,8]{1,0:T(4,128)(4,1)S(1)}, pred[4,8]{1,0:T(4,128)(4,1)}, u32[]{:S(2)}) copy-start(pred[4,8]{1,0:T(4,128)(4,1)} %copy-done.35) | copy-start | bytes 100
  270.3 9.4 %copy-start.47 = (f32[1,4]{1,0:T(1,128)S(1)}, f32[1,4]{1,0:T(1,128)}, u32[]{:S(2)}) copy-start(f32[1,4]{1,0:T(1,128)} %param.29) | copy-start | bytes 52
  279.9 1.4 copy-start.28
  302.1 5.6 %collective-permute-start.3 = (f32[16,2048]{1,0:T(8,128)S(1)}, f32[16,2048]{1,0:T(8,128)S(1)}, u32[]{:S(2)}, u32[]{:S(2)}) collective-permute-start(f32[16,2048]{1,0:T(8,128)S(1)} %fusion.1), channel_id=1, source_target_pairs={{0,1},{1,0},{2,3},{3,2},{4,5},{5,4},{6,7},{7,6},{8,9},{9,8},{10,11... | collective-permute-start | bytes 393224 | tf_op jit(solution)/shard_map/ppermute | solution.py:36
  307.8 5.2 %collective-permute-start.4 = (f32[16,2048]{1,0:T(8,128)S(1)}, f32[16,2048]{1,0:T(8,128)}, u32[]{:S(2)}, u32[]{:S(2)}) collective-permute-start(f32[16,2048]{1,0:T(8,128)S(1)} %add.226), channel_id=1, source_target_pairs={{0,3},{1,2},{2,1},{3,0},{4,7},{5,6},{6,5},{7,4},{8,11},{9,10},{10,... | collective-permute-start | bytes 393224 | tf_op jit(solution)/shard_map/ppermute | solution.py:37
  308.5 4.5 %copy-start.11 = (bf16[16,2048]{1,0:T(8,128)(2,1)S(1)}, bf16[16,2048]{1,0:T(8,128)(2,1)}, u32[]{:S(2)}) copy-start(bf16[16,2048]{1,0:T(8,128)(2,1)} %copy-done.10) | copy-start | bytes 196612
